TPU v7x, 512 devices: a whole 4x8x8 slice. The times are simulated.
512 devices in a mesh: lat: 16 (over z_hi, x, core), lon: 32 (over z_lo, y).
Axes of the slice: x: 4, y: 8, z: 8 (z_hi: 2, z_lo: 4; z = z_hi * 4 + z_lo), core: 2. Of those that a mesh axis runs over, the one named last changes fastest.
Arguments:
- field: bfloat16 [64, 4096, 512], P('lat', 'lon'), may hold values from -6 to 6
- lon_width: int32 [64], P('lat'), may hold values from 1 to 256, as said below
- lon_taps: float32 [64, 9, 513], P('lat'), may hold values from -0.375 to 0.375
- row_scale: float32 [64], P('lat'), may hold values from 0.05 to 0.2
- support: int32 [1536, 3], P('lat'), may hold values from -2 to 8, as said below
- mix_weight: bfloat16 [9, 512, 512], replicated, may hold values from -0.25 to 0.25
Outputs:
- block_out: bfloat16 [64, 4096, 512], P('lat', 'lon')
Inputs may be any that keep to these rules, and one draw needn't show every extreme that they name: `lon_width`: the first row of the slab has a half-width of 256. `support`: the output row lies in the entry's band, the input row within 2 rows of it; every output row has 24 entries, stored in order of output row.
All inputs are finite; a program needn't handle non-finite values.
Results may differ from a plain program's by a relative error of at most 0.0057.
Values may be sent and summed in bfloat16 or wider, within the bound.
No kernel may reach another device: no remote copies, remote signals or barrier semaphores. Data moves between devices by JAX's collectives and lax.ppermute only.
A program may use at most 192 MiB of HBM per device.

v0:
```python
import jax
import jax.numpy as jnp
from jax import lax
from jax.experimental import pallas as pl
from jax.experimental.pallas import tpu as pltpu
from jax.sharding import PartitionSpec as P

SPAN = 2
RIM = 2


def shifted(value, axis, by):
    length = lax.axis_size(axis)
    return lax.ppermute(value, axis, [(i, (i + by) % length) for i in range(length)])


def with_halo(block, sides, width):
    for axis, dim in sides:
        count = lax.axis_size(axis)
        forward = [(i, i + 1) for i in range(count - 1)]
        backward = [(target, source) for source, target in forward]
        low = lax.ppermute(
            lax.slice_in_dim(block, block.shape[dim] - width, None, axis=dim), axis, forward
        )
        high = lax.ppermute(lax.slice_in_dim(block, 0, width, axis=dim), axis, backward)
        block = jnp.concatenate([low, block, high], axis=dim)
    return block


def masked_taps(lon_taps, lon_width):
    length = lon_taps.shape[2]
    middle = (length - 1) // 2
    distance = jnp.abs(jnp.arange(length, dtype=jnp.int32) - middle)
    keep = distance[None, None, :] <= lon_width[:, None, None]
    return jnp.where(keep, lon_taps, 0.0).astype(jnp.bfloat16)


def _toeplitz_kernel(taps_ref, out_ref):
    kinds = taps_ref.shape[1]
    cols = out_ref.shape[2]
    for kind in range(kinds):
        row = taps_ref[0, kind : kind + 1, :]
        wide = jnp.broadcast_to(row, (cols, row.shape[1]))
        out_ref[0, kind] = pltpu.roll(wide, 0, 1, stride=1, stride_axis=0).astype(out_ref.dtype)


def band_matrix(short_taps, cols, window):
    rows, kinds, length = short_taps.shape
    padded = jnp.pad(short_taps.astype(jnp.float32), ((0, 0), (0, 0), (0, window - length)))
    return pl.pallas_call(
        _toeplitz_kernel,
        grid=(rows,),
        in_specs=[pl.BlockSpec((1, kinds, window), lambda i: (i, 0, 0))],
        out_specs=pl.BlockSpec((1, kinds, cols, window), lambda i: (i, 0, 0, 0)),
        out_shape=jax.ShapeDtypeStruct((rows, kinds, cols, window), jnp.bfloat16),
    )(padded)


def longitude_halo(source):
    west = shifted(source, "lon", 1)
    east = shifted(source, "lon", -1)
    far_west = shifted(west, "lon", 1)
    far_east = shifted(east, "lon", -1)
    return far_west, west, east, far_east


def coupling(out_rows, in_rows, basis, valid, output_rows, input_rows, kinds):
    out_match = (out_rows[:, None] == jnp.arange(output_rows, dtype=jnp.int32)[None, :]) & valid[
        :, None
    ]
    in_match = (basis * input_rows + in_rows)[:, None] == jnp.arange(
        kinds * input_rows, dtype=jnp.int32
    )[None, :]
    table = jnp.dot(
        out_match.astype(jnp.float32).T,
        in_match.astype(jnp.float32),
        precision=lax.Precision.HIGHEST,
    )
    return table.reshape(output_rows, kinds, input_rows)


def combine(counts, mixed):
    total = None
    for basis_index in range(mixed.shape[0]):
        for row in range(mixed.shape[1]):
            term = counts[:, basis_index, row][:, None, None] * mixed[basis_index, row][None]
            total = term if total is None else total + term
    return total


def on_device(field, lon_width, lon_taps, row_scale, support, mix_weight):
    rows = field.shape[0]
    cols = field.shape[1]
    kinds = lon_taps.shape[1]
    far_west, west, east, far_east = longitude_halo(field)
    short_taps = masked_taps(lon_taps, lon_width)
    window = cols * (2 * SPAN + 1)
    toeplitz = band_matrix(short_taps, cols, window)
    local = jnp.einsum(
        "ikjp,ipc->ikjc",
        toeplitz[:, :, :, SPAN * cols : (SPAN + 1) * cols],
        field,
        preferred_element_type=jnp.float32,
    )
    halo = jnp.concatenate([far_west, west, east, far_east], axis=1)
    halo_taps = jnp.concatenate(
        [toeplitz[:, :, :, : SPAN * cols], toeplitz[:, :, :, (SPAN + 1) * cols :]], axis=3
    )
    responses = (
        local + jnp.einsum("ikjp,ipc->ikjc", halo_taps, halo, preferred_element_type=jnp.float32)
    ).astype(jnp.bfloat16)
    entries = support.shape[0]
    lists = with_halo(support, (("lat", 0),), entries)
    above = lists[:entries]
    below = lists[2 * entries :]
    out_rows = jnp.concatenate(
        [support[:, 0] + RIM, above[:, 0] - rows + RIM, below[:, 0] + rows + RIM]
    )
    in_rows = jnp.concatenate([support[:, 1], above[:, 1] - rows, below[:, 1] + rows])
    basis = jnp.concatenate([support[:, 2], above[:, 2], below[:, 2]])
    valid = jnp.concatenate(
        [(support[:, 1] >= 0) & (support[:, 1] < rows), above[:, 1] >= rows, below[:, 1] < 0]
    )
    counts = coupling(out_rows, in_rows, basis, valid, rows + 2 * RIM, rows, kinds)
    mixed = jnp.einsum(
        "ikjc,kcd->kijd", responses, mix_weight, preferred_element_type=jnp.float32
    )
    edges = jnp.concatenate([counts[:RIM], counts[rows + RIM :]], axis=0)
    outgoing = combine(edges, mixed)
    incoming = with_halo(outgoing.astype(jnp.bfloat16), (("lat", 0),), RIM).astype(jnp.float32)
    inner = combine(counts[RIM : RIM + rows], mixed)
    inner = inner + jnp.pad(incoming[:RIM], ((0, rows - RIM), (0, 0), (0, 0)))
    inner = inner + jnp.pad(incoming[3 * RIM :], ((rows - RIM, 0), (0, 0), (0, 0)))
    return (inner * row_scale[:, None, None]).astype(jnp.bfloat16)


def solution(mesh):
    in_specs = (
        P("lat", "lon", None),
        P("lat"),
        P("lat", None, None),
        P("lat"),
        P("lat", None),
        P(),
    )
    out_specs = P("lat", "lon", None)
    return jax.shard_map(
        on_device, mesh=mesh, in_specs=in_specs, out_specs=out_specs, check_vma=False
    )
```

profile of v0, /device:TPU:7, one launch (start us, length us, event | category | flops | bytes accessed | tf_op | source)
XLA Modules:
  0.0 117.4 jit_solution(2853828675805712703)
XLA Ops:
  0.0 11.1 %collective-permute-start = (s32[96,3]{0,1:T(4,128)}, s32[96,3]{0,1:T(4,128)S(1)}, u32[]{:S(2)}, u32[]{:S(2)}) collective-permute-start(s32[96,3]{0,1:T(4,128)} %param.10), channel_id=1, source_target_pairs={{0,32},{32,64},{64,96},{96,128},{128,160},{160,192},{192,224},{224... | collective-permute-start | bytes 3464 | tf_op jit(solution)/shard_map/ppermute | solution.py:22
  11.1 1.9 %collective-permute-start.1 = (s32[96,3]{0,1:T(4,128)}, s32[96,3]{0,1:T(4,128)S(1)}, u32[]{:S(2)}, u32[]{:S(2)}) collective-permute-start(s32[96,3]{0,1:T(4,128)} %param.10), channel_id=1, source_target_pairs={{32,0},{64,32},{96,64},{128,96},{160,128},{192,160},{224,192},{256... | collective-permute-start | bytes 3464 | tf_op jit(solution)/shard_map/ppermute | solution.py:25
  13.0 3.2 %collective-permute-start.2 = (bf16[4,128,512]{2,1,0:T(8,128)(2,1)}, bf16[4,128,512]{2,1,0:T(8,128)(2,1)S(1)}, u32[]{:S(2)}, u32[]{:S(2)}) collective-permute-start(bf16[4,128,512]{2,1,0:T(8,128)(2,1)} %param.6), channel_id=1, source_target_pairs={{0,1},{1,2},{2,3},{3,4},{4,5},{5,6},{6,7},{7,8},{8,9},{9,10},{10,1... | collective-permute-start | bytes 1572872 | tf_op jit(solution)/shard_map/ppermute | solution.py:14
  16.3 6.5 %collective-permute-start.4 = (bf16[4,128,512]{2,1,0:T(8,128)(2,1)}, bf16[4,128,512]{2,1,0:T(8,128)(2,1)}, u32[]{:S(2)}, u32[]{:S(2)}) collective-permute-start(bf16[4,128,512]{2,1,0:T(8,128)(2,1)} %param.6), channel_id=1, source_target_pairs={{0,31},{1,0},{2,1},{3,2},{4,3},{5,4},{6,5},{7,6},{8,7},{9,8},{10,9... | collective-permute-start | bytes 1572872 | tf_op jit(solution)/shard_map/ppermute | solution.py:14
  22.8 0.8 add_bitcast_fusion.4
  23.6 0.7 broadcast_compare_fusion
  24.3 0.9 fusion.20
  25.3 0.7 pad_convert_fusion.taps_ref
  25.9 4.7 %shard_map.64 = bf16[4,9,128,640]{3,2,1,0:T(8,128)(2,1)} custom-call(f32[4,9,640]{2,1,0:T(8,128)} %pad_convert_fusion.taps_ref), custom_call_target="tpu_custom_call" | custom-call | tf_op jit(solution)/shard_map/pallas_call | solution.py:50
  30.6 4.3 %fusion.100 = (bf16[4,9,128,256]{3,2,1,0:T(8,128)(2,1)S(1)}, bf16[4,9,128,256]{3,2,1,0:T(8,128)(2,1)}) fusion(bf16[4,9,128,640]{3,2,1,0:T(8,128)(2,1)} %shard_map.64), kind=kLoop, calls=%fused_computation.267 | loop fusion | bytes 9437184 | tf_op jit(solution)/shard_map/slice | solution.py:107
  34.9 0.7 compare_and_fusion
  35.6 0.0 collective-permute-done
  35.6 0.0 collective-permute-done.1
  35.6 0.1 pad_add_fusion
  35.7 0.0 collective-permute-done.2
  35.7 1.9 %collective-permute-start.3 = (bf16[4,128,512]{2,1,0:T(8,128)(2,1)S(1)}, bf16[4,128,512]{2,1,0:T(8,128)(2,1)}, u32[]{:S(2)}, u32[]{:S(2)}) collective-permute-start(bf16[4,128,512]{2,1,0:T(8,128)(2,1)S(1)} %collective-permute-done.2), channel_id=1, source_target_pairs={{0,1},{1,2},{2,3},{3,4},{4,5},{5,6},{6,7},{7,8},{8,9},{9,10},{10,1... | collective-permute-start | bytes 1572872 | tf_op jit(solution)/shard_map/ppermute | solution.py:14
  37.7 0.0 collective-permute-done.4
  37.7 7.3 %collective-permute-start.5 = (bf16[4,128,512]{2,1,0:T(8,128)(2,1)}, bf16[4,128,512]{2,1,0:T(8,128)(2,1)}, u32[]{:S(2)}, u32[]{:S(2)}) collective-permute-start(bf16[4,128,512]{2,1,0:T(8,128)(2,1)} %collective-permute-done.4), channel_id=1, source_target_pairs={{0,31},{1,0},{2,1},{3,2},{4,3},{5,4},{6,5},{7,6},{8,7},{9,8},{10,9... | collective-permute-start | bytes 1572872 | tf_op jit(solution)/shard_map/ppermute | solution.py:14
  44.9 0.1 pad_add_fusion.1
  45.0 0.3 fusion.22
  45.3 0.1 slice.518
  45.4 0.1 copy.51
  45.5 0.1 slice.520
  45.6 0.1 copy.52
  45.7 0.3 fusion.70
  46.0 0.2 fusion.97
  46.2 0.2 fusion.88
  46.4 0.7 fusion.79
  47.1 4.8 %collective-permute-done.3 = bf16[4,128,512]{2,1,0:T(8,128)(2,1)} collective-permute-done((bf16[4,128,512]{2,1,0:T(8,128)(2,1)S(1)}, bf16[4,128,512]{2,1,0:T(8,128)(2,1)}, u32[]{:S(2)}, u32[]{:S(2)}) %collective-permute-start.3) | collective-permute-done | bytes 524320 | tf_op jit(solution)/shard_map/ppermute | solution.py:14
  51.9 2.0 %collective-permute-done.5 = bf16[4,128,512]{2,1,0:T(8,128)(2,1)} collective-permute-done((bf16[4,128,512]{2,1,0:T(8,128)(2,1)}, bf16[4,128,512]{2,1,0:T(8,128)(2,1)}, u32[]{:S(2)}, u32[]{:S(2)}) %collective-permute-start.5) | collective-permute-done | bytes 524320 | tf_op jit(solution)/shard_map/ppermute | solution.py:14
  53.9 8.4 %fusion.2 = f32[4,9,128,512]{3,2,0,1:T(8,128)} fusion(bf16[4,128,512]{2,1,0:T(8,128)(2,1)} %collective-permute-done.5, bf16[4,128,512]{2,1,0:T(8,128)(2,1)} %collective-permute-done.4, bf16[4,128,512]{2,1,0:T(8,128)(2,1)S(1)} %collective-permute-done.2, bf16[4,128,512]{2,1,0:T(8,128)(2,1)} %collective-permute-done.3, ...), kind=kOutput, calls=%fused_computation.4 | convolution fusion | flops 2433744896 | bytes 16252928 | tf_op jit(solution)/shard_map/ikjp,ipc->ikjc/dot_general | solution.py:110
  62.3 0.0 copy-done.43
  62.3 12.8 %fusion = f32[9,4,128,512]{3,2,1,0:T(8,128)} fusion(f32[4,9,128,512]{3,2,0,1:T(8,128)} %fusion.2, bf16[9,512,512]{2,1,0:T(8,128)(2,1)} %param.11, bf16[4,128,512]{2,1,0:T(8,128)(2,1)S(1)} %copy-done.43, bf16[4,9,128,640]{3,2,1,0:T(8,128)(2,1)} %shard_map.64), kind=kOutput, calls=%fused_computation.1 | convolution fusion | flops 3024617472 | bytes 25296896 | tf_op jit(solution)/shard_map/ikjc,kcd->kijd/dot_general | solution.py:125
  75.1 3.2 %slice_bitcast_fusion.35 = (f32[128,512]{1,0:T(8,128)S(1)}, f32[128,512]{1,0:T(8,128)S(1)}, f32[128,512]{1,0:T(8,128)S(1)}, f32[128,512]{1,0:T(8,128)S(1)}, f32[...) fusion(f32[9,4,128,512]{3,2,1,0:T(8,128)} %fusion), kind=kLoop, calls=%fused_computation.59 | loop fusion | bytes 9961472 | tf_op jit(solution)/shard_map/mul | solution.py:86
  78.3 0.0 copy-start
  78.3 0.0 copy-start.2
  78.3 0.0 copy-start.4
  78.4 0.0 copy-start.6
  78.4 0.0 copy-start.8
  78.4 0.0 copy-start.10
  78.4 0.0 copy-start.12
  78.4 0.0 copy-start.14
  78.4 0.0 copy-start.44
  78.4 3.6 %slice_bitcast_fusion.34 = (f32[128,512]{1,0:T(8,128)S(1)}, f32[128,512]{1,0:T(8,128)S(1)}, f32[128,512]{1,0:T(8,128)S(1)}, f32[128,512]{1,0:T(8,128)S(1)}, f32[...) fusion(f32[9,4,128,512]{3,2,1,0:T(8,128)} %fusion), kind=kLoop, calls=%fused_computation.58 | loop fusion | bytes 8912896 | tf_op jit(solution)/shard_map/mul | solution.py:86
  82.1 0.0 copy-start.16
  82.1 0.0 copy-start.18
  82.1 0.0 copy-start.20
  82.1 0.0 copy-start.22
  82.1 0.0 copy-start.24
  82.1 0.0 copy-start.26
  82.2 3.2 %add_convert_fusion.2 = bf16[4,128,512]{2,1,0:T(8,128)(2,1)S(1)} fusion(f32[4]{0:T(128)S(1)} %get-tuple-element.75, f32[4]{0:T(128)S(1)} %get-tuple-element.76, f32[4]{0:T(128)S(1)} %get-tuple-element.74, f32[4]{0:T(128)S(1)} %get-tuple-element.73, f32[4]{0:T(128)S(1)} %get-tuple-element.72, f32[4]{0:T(128)S(1)} %get-tuple-element.71, ...), kind=kLoop, calls=%fused_computation.21 | loop fusion | flops 18874368 | bytes 9962048 | tf_op jit(solution)/shard_map/convert_element_type | solution.py:130
  85.7 0.0 copy-start.45
  85.7 0.0 copy-start.46
  85.7 0.8 fusion.101
  86.5 8.5 %collective-permute-start.6 = (bf16[2,128,512]{2,1,0:T(8,128)(2,1)}, bf16[2,128,512]{2,1,0:T(8,128)(2,1)}, u32[]{:S(2)}, u32[]{:S(2)}) collective-permute-start(bf16[2,128,512]{2,1,0:T(8,128)(2,1)} %get-tuple-element.115), channel_id=1, source_target_pairs={{0,32},{32,64},{64,96},{96,128},{128,160},{160,192},{192,224},{224... | collective-permute-start | bytes 786440 | tf_op jit(solution)/shard_map/ppermute | solution.py:22
  95.0 2.1 %collective-permute-start.7 = (bf16[2,128,512]{2,1,0:T(8,128)(2,1)}, bf16[2,128,512]{2,1,0:T(8,128)(2,1)}, u32[]{:S(2)}, u32[]{:S(2)}) collective-permute-start(bf16[2,128,512]{2,1,0:T(8,128)(2,1)} %get-tuple-element.116), channel_id=1, source_target_pairs={{32,0},{64,32},{96,64},{128,96},{160,128},{192,160},{224,192},{256... | collective-permute-start | bytes 786440 | tf_op jit(solution)/shard_map/ppermute | solution.py:25
  97.2 0.1 slice.441
  97.4 0.3 slice_reduce_fusion.34
  97.7 0.3 slice_reduce_fusion.35
  98.0 0.6 collective-permute-done.6
  98.6 10.4 %collective-permute-done.7 = bf16[2,128,512]{2,1,0:T(8,128)(2,1)} collective-permute-done((bf16[2,128,512]{2,1,0:T(8,128)(2,1)}, bf16[2,128,512]{2,1,0:T(8,128)(2,1)}, u32[]{:S(2)}, u32[]{:S(2)}) %collective-permute-start.7) | collective-permute-done | bytes 262176 | tf_op jit(solution)/shard_map/ppermute | solution.py:25
  109.1 1.0 maximum_convert_fusion.1
  110.1 1.2 %maximum_convert_fusion = f32[8,128,512]{2,1,0:T(8,128)S(1)} fusion(bf16[2,128,512]{2,1,0:T(8,128)(2,1)} %collective-permute-done.7, bf16[4,128,512]{2,1,0:T(8,128)(2,1)S(1)} %add_convert_fusion.2, bf16[2,128,512]{2,1,0:T(8,128)(2,1)} %collective-permute-done.6), kind=kLoop, calls=%fused_computation.20 | loop fusion | flops 1572864 | bytes 3145728 | tf_op jit(solution)/shard_map/convert_element_type | solution.py:130
  111.4 5.9 %fusion.17 = bf16[4,128,512]{2,1,0:T(8,128)(2,1)} fusion(f32[8,128,512]{2,1,0:T(8,128)S(1)} %maximum_convert_fusion, f32[2,128,512]{2,1,0:T(8,128)S(1)} %maximum_convert_fusion.1, f32[4]{0:T(128)S(1)} %copy-done.45, f32[128,512]{1,0:T(8,128)S(1)} %get-tuple-element.78, f32[4]{0:T(128)S(1)} %get-tuple-element.6, f32[128,512]{1,0:T(8,128)S(1)} %get-tuple-element.79, ...), kind=kLoop, calls=%fused_computation.19 | loop fusion | flops 19922944 | bytes 11534932 | tf_op jit(solution)/shard_map/convert_element_type | solution.py:134
  (83 shorter events, 0.2 us)
Async XLA Ops:
  0.0 35.6 %collective-permute-start = (s32[96,3]{0,1:T(4,128)}, s32[96,3]{0,1:T(4,128)S(1)}, u32[]{:S(2)}, u32[]{:S(2)}) collective-permute-start(s32[96,3]{0,1:T(4,128)} %param.10), channel_id=1, source_target_pairs={{0,32},{32,64},{64,96},{96,128},{128,160},{160,192},{192,224},{224... | collective-permute-start | bytes 3464 | tf_op jit(solution)/shard_map/ppermute | solution.py:22
  11.1 24.5 %collective-permute-start.1 = (s32[96,3]{0,1:T(4,128)}, s32[96,3]{0,1:T(4,128)S(1)}, u32[]{:S(2)}, u32[]{:S(2)}) collective-permute-start(s32[96,3]{0,1:T(4,128)} %param.10), channel_id=1, source_target_pairs={{32,0},{64,32},{96,64},{128,96},{160,128},{192,160},{224,192},{256... | collective-permute-start | bytes 3464 | tf_op jit(solution)/shard_map/ppermute | solution.py:25
  13.0 22.7 %collective-permute-start.2 = (bf16[4,128,512]{2,1,0:T(8,128)(2,1)}, bf16[4,128,512]{2,1,0:T(8,128)(2,1)S(1)}, u32[]{:S(2)}, u32[]{:S(2)}) collective-permute-start(bf16[4,128,512]{2,1,0:T(8,128)(2,1)} %param.6), channel_id=1, source_target_pairs={{0,1},{1,2},{2,3},{3,4},{4,5},{5,6},{6,7},{7,8},{8,9},{9,10},{10,1... | collective-permute-start | bytes 1572872 | tf_op jit(solution)/shard_map/ppermute | solution.py:14
  16.3 21.4 %collective-permute-start.4 = (bf16[4,128,512]{2,1,0:T(8,128)(2,1)}, bf16[4,128,512]{2,1,0:T(8,128)(2,1)}, u32[]{:S(2)}, u32[]{:S(2)}) collective-permute-start(bf16[4,128,512]{2,1,0:T(8,128)(2,1)} %param.6), channel_id=1, source_target_pairs={{0,31},{1,0},{2,1},{3,2},{4,3},{5,4},{6,5},{7,6},{8,7},{9,8},{10,9... | collective-permute-start | bytes 1572872 | tf_op jit(solution)/shard_map/ppermute | solution.py:14
  35.7 16.2 %collective-permute-start.3 = (bf16[4,128,512]{2,1,0:T(8,128)(2,1)S(1)}, bf16[4,128,512]{2,1,0:T(8,128)(2,1)}, u32[]{:S(2)}, u32[]{:S(2)}) collective-permute-start(bf16[4,128,512]{2,1,0:T(8,128)(2,1)S(1)} %collective-permute-done.2), channel_id=1, source_target_pairs={{0,1},{1,2},{2,3},{3,4},{4,5},{5,6},{6,7},{7,8},{8,9},{9,10},{10,1... | collective-permute-start | bytes 1572872 | tf_op jit(solution)/shard_map/ppermute | solution.py:14
  37.7 16.2 %collective-permute-start.5 = (bf16[4,128,512]{2,1,0:T(8,128)(2,1)}, bf16[4,128,512]{2,1,0:T(8,128)(2,1)}, u32[]{:S(2)}, u32[]{:S(2)}) collective-permute-start(bf16[4,128,512]{2,1,0:T(8,128)(2,1)} %collective-permute-done.4), channel_id=1, source_target_pairs={{0,31},{1,0},{2,1},{3,2},{4,3},{5,4},{6,5},{7,6},{8,7},{9,8},{10,9... | collective-permute-start | bytes 1572872 | tf_op jit(solution)/shard_map/ppermute | solution.py:14
  53.9 8.4 %copy-start.43 = (bf16[4,128,512]{2,1,0:T(8,128)(2,1)S(1)}, bf16[4,128,512]{2,1,0:T(8,128)(2,1)}, u32[]{:S(2)}) copy-start(bf16[4,128,512]{2,1,0:T(8,128)(2,1)} %param.6) | copy-start | bytes 1572868
  78.3 7.1 %copy-start = (f32[128,512]{1,0:T(8,128)}, f32[128,512]{1,0:T(8,128)S(1)}, u32[]{:S(2)}) copy-start(f32[128,512]{1,0:T(8,128)S(1)} %get-tuple-element.88) | copy-start | bytes 786436
  78.3 7.1 %copy-start.2 = (f32[128,512]{1,0:T(8,128)}, f32[128,512]{1,0:T(8,128)S(1)}, u32[]{:S(2)}) copy-start(f32[128,512]{1,0:T(8,128)S(1)} %get-tuple-element.89) | copy-start | bytes 786436
  78.3 7.1 %copy-start.4 = (f32[128,512]{1,0:T(8,128)}, f32[128,512]{1,0:T(8,128)S(1)}, u32[]{:S(2)}) copy-start(f32[128,512]{1,0:T(8,128)S(1)} %get-tuple-element.90) | copy-start | bytes 786436
  78.4 7.1 %copy-start.6 = (f32[128,512]{1,0:T(8,128)}, f32[128,512]{1,0:T(8,128)S(1)}, u32[]{:S(2)}) copy-start(f32[128,512]{1,0:T(8,128)S(1)} %get-tuple-element.91) | copy-start | bytes 786436
  78.4 7.1 %copy-start.8 = (f32[128,512]{1,0:T(8,128)}, f32[128,512]{1,0:T(8,128)S(1)}, u32[]{:S(2)}) copy-start(f32[128,512]{1,0:T(8,128)S(1)} %get-tuple-element.92) | copy-start | bytes 786436
  78.4 7.1 %copy-start.10 = (f32[128,512]{1,0:T(8,128)}, f32[128,512]{1,0:T(8,128)S(1)}, u32[]{:S(2)}) copy-start(f32[128,512]{1,0:T(8,128)S(1)} %get-tuple-element.93) | copy-start | bytes 786436
  78.4 7.1 %copy-start.12 = (f32[128,512]{1,0:T(8,128)}, f32[128,512]{1,0:T(8,128)S(1)}, u32[]{:S(2)}) copy-start(f32[128,512]{1,0:T(8,128)S(1)} %get-tuple-element.94) | copy-start | bytes 786436
  78.4 7.1 %copy-start.14 = (f32[128,512]{1,0:T(8,128)}, f32[128,512]{1,0:T(8,128)S(1)}, u32[]{:S(2)}) copy-start(f32[128,512]{1,0:T(8,128)S(1)} %get-tuple-element.95) | copy-start | bytes 786436
  78.4 3.8 %copy-start.44 = (f32[4]{0:T(128)S(1)}, f32[4]{0:T(128)}, u32[]{:S(2)}) copy-start(f32[4]{0:T(128)} %get-tuple-element.67) | copy-start | bytes 52
  82.1 3.4 %copy-start.16 = (f32[128,512]{1,0:T(8,128)}, f32[128,512]{1,0:T(8,128)S(1)}, u32[]{:S(2)}) copy-start(f32[128,512]{1,0:T(8,128)S(1)} %get-tuple-element.96) | copy-start | bytes 786436
  82.1 3.4 %copy-start.18 = (f32[128,512]{1,0:T(8,128)}, f32[128,512]{1,0:T(8,128)S(1)}, u32[]{:S(2)}) copy-start(f32[128,512]{1,0:T(8,128)S(1)} %get-tuple-element.97) | copy-start | bytes 786436
  82.1 3.4 %copy-start.20 = (f32[128,512]{1,0:T(8,128)}, f32[128,512]{1,0:T(8,128)S(1)}, u32[]{:S(2)}) copy-start(f32[128,512]{1,0:T(8,128)S(1)} %get-tuple-element.98) | copy-start | bytes 786436
  82.1 3.4 %copy-start.22 = (f32[128,512]{1,0:T(8,128)}, f32[128,512]{1,0:T(8,128)S(1)}, u32[]{:S(2)}) copy-start(f32[128,512]{1,0:T(8,128)S(1)} %get-tuple-element.99) | copy-start | bytes 786436
  82.1 3.4 %copy-start.24 = (f32[128,512]{1,0:T(8,128)}, f32[128,512]{1,0:T(8,128)S(1)}, u32[]{:S(2)}) copy-start(f32[128,512]{1,0:T(8,128)S(1)} %get-tuple-element.100) | copy-start | bytes 786436
  82.1 3.4 %copy-start.26 = (f32[128,512]{1,0:T(8,128)}, f32[128,512]{1,0:T(8,128)S(1)}, u32[]{:S(2)}) copy-start(f32[128,512]{1,0:T(8,128)S(1)} %get-tuple-element.101) | copy-start | bytes 786436
  82.1 3.4 %copy-start.28 = (f32[128,512]{1,0:T(8,128)}, f32[128,512]{1,0:T(8,128)S(1)}, u32[]{:S(2)}) copy-start(f32[128,512]{1,0:T(8,128)S(1)} %get-tuple-element.102) | copy-start | bytes 786436
  82.1 3.4 %copy-start.30 = (f32[128,512]{1,0:T(8,128)}, f32[128,512]{1,0:T(8,128)S(1)}, u32[]{:S(2)}) copy-start(f32[128,512]{1,0:T(8,128)S(1)} %get-tuple-element.103) | copy-start | bytes 786436
  82.1 3.4 %copy-start.32 = (f32[128,512]{1,0:T(8,128)}, f32[128,512]{1,0:T(8,128)S(1)}, u32[]{:S(2)}) copy-start(f32[128,512]{1,0:T(8,128)S(1)} %get-tuple-element.104) | copy-start | bytes 786436
  82.2 3.4 %copy-start.34 = (f32[128,512]{1,0:T(8,128)}, f32[128,512]{1,0:T(8,128)S(1)}, u32[]{:S(2)}) copy-start(f32[128,512]{1,0:T(8,128)S(1)} %get-tuple-element.105) | copy-start | bytes 786436
  82.2 3.4 %copy-start.36 = (f32[128,512]{1,0:T(8,128)}, f32[128,512]{1,0:T(8,128)S(1)}, u32[]{:S(2)}) copy-start(f32[128,512]{1,0:T(8,128)S(1)} %get-tuple-element.106) | copy-start | bytes 786436
  82.2 3.4 %copy-start.37 = (f32[128,512]{1,0:T(8,128)}, f32[128,512]{1,0:T(8,128)S(1)}, u32[]{:S(2)}) copy-start(f32[128,512]{1,0:T(8,128)S(1)} %get-tuple-element.107) | copy-start | bytes 786436
  82.2 3.4 %copy-start.38 = (f32[128,512]{1,0:T(8,128)}, f32[128,512]{1,0:T(8,128)S(1)}, u32[]{:S(2)}) copy-start(f32[128,512]{1,0:T(8,128)S(1)} %get-tuple-element.108) | copy-start | bytes 786436
  82.2 3.4 %copy-start.39 = (f32[128,512]{1,0:T(8,128)}, f32[128,512]{1,0:T(8,128)S(1)}, u32[]{:S(2)}) copy-start(f32[128,512]{1,0:T(8,128)S(1)} %get-tuple-element.109) | copy-start | bytes 786436
  82.2 3.4 %copy-start.40 = (f32[128,512]{1,0:T(8,128)}, f32[128,512]{1,0:T(8,128)S(1)}, u32[]{:S(2)}) copy-start(f32[128,512]{1,0:T(8,128)S(1)} %get-tuple-element.110) | copy-start | bytes 786436
  82.2 3.4 %copy-start.41 = (f32[128,512]{1,0:T(8,128)}, f32[128,512]{1,0:T(8,128)S(1)}, u32[]{:S(2)}) copy-start(f32[128,512]{1,0:T(8,128)S(1)} %get-tuple-element.111) | copy-start | bytes 786436
  82.2 3.4 %copy-start.42 = (f32[128,512]{1,0:T(8,128)}, f32[128,512]{1,0:T(8,128)S(1)}, u32[]{:S(2)}) copy-start(f32[128,512]{1,0:T(8,128)S(1)} %get-tuple-element.112) | copy-start | bytes 786436
  85.7 25.6 %copy-start.45 = (f32[4]{0:T(128)S(1)}, f32[4]{0:T(128)}, u32[]{:S(2)}) copy-start(f32[4]{0:T(128)} %param.9) | copy-start | bytes 52
  85.7 25.6 %copy-start.46 = (pred[4]{0:T(512)(128)(4,1)S(1)}, pred[4]{0:T(512)(128)(4,1)}, u32[]{:S(2)}) copy-start(pred[4]{0:T(512)(128)(4,1)} %constant.24.clone.1) | copy-start | bytes 16
  86.5 12.1 %collective-permute-start.6 = (bf16[2,128,512]{2,1,0:T(8,128)(2,1)}, bf16[2,128,512]{2,1,0:T(8,128)(2,1)}, u32[]{:S(2)}, u32[]{:S(2)}) collective-permute-start(bf16[2,128,512]{2,1,0:T(8,128)(2,1)} %get-tuple-element.115), channel_id=1, source_target_pairs={{0,32},{32,64},{64,96},{96,128},{128,160},{160,192},{192,224},{224... | collective-permute-start | bytes 786440 | tf_op jit(solution)/shard_map/ppermute | solution.py:22
  95.0 14.0 %collective-permute-start.7 = (bf16[2,128,512]{2,1,0:T(8,128)(2,1)}, bf16[2,128,512]{2,1,0:T(8,128)(2,1)}, u32[]{:S(2)}, u32[]{:S(2)}) collective-permute-start(bf16[2,128,512]{2,1,0:T(8,128)(2,1)} %get-tuple-element.116), channel_id=1, source_target_pairs={{32,0},{64,32},{96,64},{128,96},{160,128},{192,160},{224,192},{256... | collective-permute-start | bytes 786440 | tf_op jit(solution)/shard_map/ppermute | solution.py:25
  97.2 14.0 %copy-start.1 = (f32[128,512]{1,0:T(8,128)S(1)}, f32[128,512]{1,0:T(8,128)}, u32[]{:S(2)}) copy-start(f32[128,512]{1,0:T(8,128)} %copy-done) | copy-start | bytes 786436
  97.2 14.0 %copy-start.3 = (f32[128,512]{1,0:T(8,128)S(1)}, f32[128,512]{1,0:T(8,128)}, u32[]{:S(2)}) copy-start(f32[128,512]{1,0:T(8,128)} %copy-done.2) | copy-start | bytes 786436
  97.2 14.0 %copy-start.5 = (f32[128,512]{1,0:T(8,128)S(1)}, f32[128,512]{1,0:T(8,128)}, u32[]{:S(2)}) copy-start(f32[128,512]{1,0:T(8,128)} %copy-done.4) | copy-start | bytes 786436
  97.3 14.0 %copy-start.7 = (f32[128,512]{1,0:T(8,128)S(1)}, f32[128,512]{1,0:T(8,128)}, u32[]{:S(2)}) copy-start(f32[128,512]{1,0:T(8,128)} %copy-done.6) | copy-start | bytes 786436
  97.3 14.0 %copy-start.9 = (f32[128,512]{1,0:T(8,128)S(1)}, f32[128,512]{1,0:T(8,128)}, u32[]{:S(2)}) copy-start(f32[128,512]{1,0:T(8,128)} %copy-done.8) | copy-start | bytes 786436
  97.3 14.0 %copy-start.11 = (f32[128,512]{1,0:T(8,128)S(1)}, f32[128,512]{1,0:T(8,128)}, u32[]{:S(2)}) copy-start(f32[128,512]{1,0:T(8,128)} %copy-done.10) | copy-start | bytes 786436
  97.3 14.0 %copy-start.13 = (f32[128,512]{1,0:T(8,128)S(1)}, f32[128,512]{1,0:T(8,128)}, u32[]{:S(2)}) copy-start(f32[128,512]{1,0:T(8,128)} %copy-done.12) | copy-start | bytes 786436
  97.3 14.0 %copy-start.15 = (f32[128,512]{1,0:T(8,128)S(1)}, f32[128,512]{1,0:T(8,128)}, u32[]{:S(2)}) copy-start(f32[128,512]{1,0:T(8,128)} %copy-done.14) | copy-start | bytes 786436
  97.3 14.0 %copy-start.17 = (f32[128,512]{1,0:T(8,128)S(1)}, f32[128,512]{1,0:T(8,128)}, u32[]{:S(2)}) copy-start(f32[128,512]{1,0:T(8,128)} %copy-done.16) | copy-start | bytes 786436
  97.3 14.0 %copy-start.19 = (f32[128,512]{1,0:T(8,128)S(1)}, f32[128,512]{1,0:T(8,128)}, u32[]{:S(2)}) copy-start(f32[128,512]{1,0:T(8,128)} %copy-done.18) | copy-start | bytes 786436
  97.3 14.0 %copy-start.21 = (f32[128,512]{1,0:T(8,128)S(1)}, f32[128,512]{1,0:T(8,128)}, u32[]{:S(2)}) copy-start(f32[128,512]{1,0:T(8,128)} %copy-done.20) | copy-start | bytes 786436
  97.3 14.0 %copy-start.23 = (f32[128,512]{1,0:T(8,128)S(1)}, f32[128,512]{1,0:T(8,128)}, u32[]{:S(2)}) copy-start(f32[128,512]{1,0:T(8,128)} %copy-done.22) | copy-start | bytes 786436
  97.3 14.0 %copy-start.25 = (f32[128,512]{1,0:T(8,128)S(1)}, f32[128,512]{1,0:T(8,128)}, u32[]{:S(2)}) copy-start(f32[128,512]{1,0:T(8,128)} %copy-done.24) | copy-start | bytes 786436
  97.4 14.0 %copy-start.27 = (f32[128,512]{1,0:T(8,128)S(1)}, f32[128,512]{1,0:T(8,128)}, u32[]{:S(2)}) copy-start(f32[128,512]{1,0:T(8,128)} %copy-done.26) | copy-start | bytes 786436
  97.4 14.0 %copy-start.29 = (f32[128,512]{1,0:T(8,128)S(1)}, f32[128,512]{1,0:T(8,128)}, u32[]{:S(2)}) copy-start(f32[128,512]{1,0:T(8,128)} %copy-done.28) | copy-start | bytes 786436
  97.4 14.0 %copy-start.31 = (f32[128,512]{1,0:T(8,128)S(1)}, f32[128,512]{1,0:T(8,128)}, u32[]{:S(2)}) copy-start(f32[128,512]{1,0:T(8,128)} %copy-done.30) | copy-start | bytes 786436
  97.4 14.0 %copy-start.33 = (f32[128,512]{1,0:T(8,128)S(1)}, f32[128,512]{1,0:T(8,128)}, u32[]{:S(2)}) copy-start(f32[128,512]{1,0:T(8,128)} %copy-done.32) | copy-start | bytes 786436
  97.4 14.0 %copy-start.35 = (f32[128,512]{1,0:T(8,128)S(1)}, f32[128,512]{1,0:T(8,128)}, u32[]{:S(2)}) copy-start(f32[128,512]{1,0:T(8,128)} %copy-done.34) | copy-start | bytes 786436
where the time goes:
time: 118 us; the launch traced here: 117 us
  starting transfers between devices  42.6 us (36%)
  matrix products  21.5 us (18%)
  waiting for transfers between devices  17.8 us (15%)
  other arithmetic  16.7 us (14%)
  local copies, waits for them, and re-layouts  13.2 us (11%)
  Pallas kernels  4.7 us (4%)
    ppermute x2, starting transfers between devices, with_halo(): lax.ppermute(lax.slice_in_dim(block, block.shape[dim] - width, None, axis...  19.6 us
    ppermute x4, starting transfers between devices, shifted(): lax.ppermute(value, axis, [(i, (i + by) % length) for i in range(length)])  18.9 us
    dot_general x1, matrix products, on_device(): jnp.einsum('ikjc,kcd->kijd', responses, mix_weight, preferred_element_typ...  12.8 us
    ppermute x2, waiting for transfers between devices, with_halo(): lax.ppermute(lax.slice_in_dim(block, 0, width, axis=dim), axis, backward)  10.4 us
    dot_general x1, matrix products, on_device(): jnp.einsum('ikjp,ipc->ikjc', halo_taps, halo, preferred_element_type=jnp....  8.4 us
    mul x2, local copies, waits for them, and re-layouts, combine(): counts[:, basis_index, row][:, None, None] * mixed[basis_index, row][None]  6.83 us
    ppermute x4, waiting for transfers between devices, shifted(): lax.ppermute(value, axis, [(i, (i + by) % length) for i in range(length)])  6.77 us
    convert_element_type x1, other arithmetic, on_device(): return (inner * row_scale[:, None, None]).astype(jnp.bfloat16)  5.94 us
  transfers between devices with their start and end apart: 8, of which 4 were waited for; matrix products, arithmetic and copies ran while one was open for 9% of the time, Pallas kernels for 4%

commit v1 on v0

--- a/solution.py
+++ b/solution.py
@@ -35,27 +35,6 @@
     return jnp.where(keep, lon_taps, 0.0).astype(jnp.bfloat16)
 
 
-def _toeplitz_kernel(taps_ref, out_ref):
-    kinds = taps_ref.shape[1]
-    cols = out_ref.shape[2]
-    for kind in range(kinds):
-        row = taps_ref[0, kind : kind + 1, :]
-        wide = jnp.broadcast_to(row, (cols, row.shape[1]))
-        out_ref[0, kind] = pltpu.roll(wide, 0, 1, stride=1, stride_axis=0).astype(out_ref.dtype)
-
-
-def band_matrix(short_taps, cols, window):
-    rows, kinds, length = short_taps.shape
-    padded = jnp.pad(short_taps.astype(jnp.float32), ((0, 0), (0, 0), (0, window - length)))
-    return pl.pallas_call(
-        _toeplitz_kernel,
-        grid=(rows,),
-        in_specs=[pl.BlockSpec((1, kinds, window), lambda i: (i, 0, 0))],
-        out_specs=pl.BlockSpec((1, kinds, cols, window), lambda i: (i, 0, 0, 0)),
-        out_shape=jax.ShapeDtypeStruct((rows, kinds, cols, window), jnp.bfloat16),
-    )(padded)
-
-
 def longitude_halo(source):
     west = shifted(source, "lon", 1)
     east = shifted(source, "lon", -1)
@@ -79,36 +58,83 @@
     return table.reshape(output_rows, kinds, input_rows)
 
 
-def combine(counts, mixed):
-    total = None
-    for basis_index in range(mixed.shape[0]):
-        for row in range(mixed.shape[1]):
-            term = counts[:, basis_index, row][:, None, None] * mixed[basis_index, row][None]
-            total = term if total is None else total + term
-    return total
+def _block_kernel(counts_ref, taps_ref, far_west_ref, west_ref, local_ref, east_ref, far_east_ref,
+                  weight_ref, edge_ref, inner_ref, window_ref, mixed_ref):
+    row = pl.program_id(0)
+    rows = pl.num_programs(0)
+    kinds = taps_ref.shape[1]
+    cols = local_ref.shape[1]
+    parts = (far_west_ref, west_ref, local_ref, east_ref, far_east_ref)
+    for index, part in enumerate(parts):
+        window_ref[index * cols : (index + 1) * cols, :] = part[0]
+    for kind in range(kinds):
+        taps = taps_ref[0, kind : kind + 1, :]
+        wide = jnp.broadcast_to(taps, (cols, taps.shape[1]))
+        band = pltpu.roll(wide, 0, 1, stride=1, stride_axis=0).astype(jnp.bfloat16)
+        response = jnp.dot(band, window_ref[...], preferred_element_type=jnp.float32)
+        mixed_ref[kind, row] = jnp.dot(
+            response.astype(jnp.bfloat16), weight_ref[kind], preferred_element_type=jnp.float32
+        )
+
+    @pl.when(row == rows - 1)
+    def _():
+        input_rows = mixed_ref.shape[1]
+        output_rows = input_rows + 2 * RIM
+        chunk = 16
+
+        def body(step, carry):
+            start = pl.multiple_of(step * chunk, chunk)
+            edge_index = 0
+            for out_row in range(output_rows):
+                total = None
+                for kind in range(kinds):
+                    for in_row in range(max(0, out_row - 2 * RIM), min(input_rows, out_row + 1)):
+                        scale = counts_ref[(out_row * kinds + kind) * input_rows + in_row]
+                        term = scale * mixed_ref[kind, in_row, pl.ds(start, chunk), :]
+                        total = term if total is None else total + term
+                if RIM <= out_row < RIM + input_rows:
+                    inner_ref[out_row - RIM, pl.ds(start, chunk), :] = total
+                else:
+                    edge_ref[edge_index, pl.ds(start, chunk), :] = total.astype(edge_ref.dtype)
+                    edge_index += 1
+            return carry
+
+        lax.fori_loop(0, cols // chunk, body, 0)
+
+
+def block_partials(counts, short_taps, parts, mix_weight):
+    rows, cols, channels = parts[0].shape
+    kinds = short_taps.shape[1]
+    window = cols * len(parts)
+    padded = jnp.pad(
+        short_taps.astype(jnp.float32), ((0, 0), (0, 0), (0, window - short_taps.shape[2]))
+    )
+    part_spec = pl.BlockSpec((1, cols, channels), lambda i: (i, 0, 0))
+    whole = lambda shape: pl.BlockSpec(shape, lambda i: (0,) * len(shape))
+    return pl.pallas_call(
+        _block_kernel,
+        grid=(rows,),
+        in_specs=[pl.BlockSpec(memory_space=pltpu.SMEM), pl.BlockSpec((1, kinds, window), lambda i: (i, 0, 0))]
+        + [part_spec] * len(parts)
+        + [whole(mix_weight.shape)],
+        out_specs=[whole((2 * RIM, cols, channels)), whole((rows, cols, channels))],
+        out_shape=[
+            jax.ShapeDtypeStruct((2 * RIM, cols, channels), jnp.bfloat16),
+            jax.ShapeDtypeStruct((rows, cols, channels), jnp.float32),
+        ],
+        scratch_shapes=[
+            pltpu.VMEM((window, channels), jnp.bfloat16),
+            pltpu.VMEM((kinds, rows, cols, mix_weight.shape[2]), jnp.float32),
+        ],
+        compiler_params=pltpu.CompilerParams(dimension_semantics=("arbitrary",)),
+    )(counts.reshape(-1), padded, *parts, mix_weight)
 
 
 def on_device(field, lon_width, lon_taps, row_scale, support, mix_weight):
     rows = field.shape[0]
-    cols = field.shape[1]
     kinds = lon_taps.shape[1]
     far_west, west, east, far_east = longitude_halo(field)
     short_taps = masked_taps(lon_taps, lon_width)
-    window = cols * (2 * SPAN + 1)
-    toeplitz = band_matrix(short_taps, cols, window)
-    local = jnp.einsum(
-        "ikjp,ipc->ikjc",
-        toeplitz[:, :, :, SPAN * cols : (SPAN + 1) * cols],
-        field,
-        preferred_element_type=jnp.float32,
-    )
-    halo = jnp.concatenate([far_west, west, east, far_east], axis=1)
-    halo_taps = jnp.concatenate(
-        [toeplitz[:, :, :, : SPAN * cols], toeplitz[:, :, :, (SPAN + 1) * cols :]], axis=3
-    )
-    responses = (
-        local + jnp.einsum("ikjp,ipc->ikjc", halo_taps, halo, preferred_element_type=jnp.float32)
-    ).astype(jnp.bfloat16)
     entries = support.shape[0]
     lists = with_halo(support, (("lat", 0),), entries)
     above = lists[:entries]
@@ -122,13 +148,10 @@
         [(support[:, 1] >= 0) & (support[:, 1] < rows), above[:, 1] >= rows, below[:, 1] < 0]
     )
     counts = coupling(out_rows, in_rows, basis, valid, rows + 2 * RIM, rows, kinds)
-    mixed = jnp.einsum(
-        "ikjc,kcd->kijd", responses, mix_weight, preferred_element_type=jnp.float32
+    outgoing, inner = block_partials(
+        counts, short_taps, (far_west, west, field, east, far_east), mix_weight
     )
-    edges = jnp.concatenate([counts[:RIM], counts[rows + RIM :]], axis=0)
-    outgoing = combine(edges, mixed)
-    incoming = with_halo(outgoing.astype(jnp.bfloat16), (("lat", 0),), RIM).astype(jnp.float32)
-    inner = combine(counts[RIM : RIM + rows], mixed)
+    incoming = with_halo(outgoing, (("lat", 0),), RIM).astype(jnp.float32)
     inner = inner + jnp.pad(incoming[:RIM], ((0, rows - RIM), (0, 0), (0, 0)))
     inner = inner + jnp.pad(incoming[3 * RIM :], ((rows - RIM, 0), (0, 0), (0, 0)))
     return (inner * row_scale[:, None, None]).astype(jnp.bfloat16)

time: 118 us -> 93.4 us (0.79)
  matrix products: 21.5 us -> 0.31 us
  Pallas kernels: 4.7 us -> 19.8 us
  other arithmetic: 16.7 us -> 5.36 us
  local copies, waits for them, and re-layouts: 13.2 us -> 2.63 us
  waiting for transfers between devices: 17.8 us -> 22.5 us
  starting transfers between devices: 42.6 us -> 40.9 us
    dot_general x2 -> x0, matrix products: 21.2 us -> none  [the longest x1 12.8 us: on_device(): jnp.einsum('ikjc,kcd->kijd', responses, mix_weight, preferred_element_typ...]
    pallas_call x1, Pallas kernels: 4.7 us -> 19.8 us  [block_partials(): pl.pallas_call(_block_kernel, grid=(rows,), in_specs=[pl.BlockSpec(memory...]
    mul x2 -> x0, local copies, waits for them, and re-layouts: 6.83 us -> none  [combine(): counts[:, basis_index, row][:, None, None] * mixed[basis_index, row][None]]
    slice x10 -> x0, local copies, waits for them, and re-layouts: 5.3 us -> none  [the longest x1 4.25 us: on_device(): toeplitz[:, :, :, :SPAN * cols]]
    convert_element_type x1, other arithmetic: 5.94 us -> 1.18 us  [on_device(): return (inner * row_scale[:, None, None]).astype(jnp.bfloat16)]
    convert_element_type x2 -> x1, other arithmetic: 4.35 us -> 0.16 us  [on_device(): incoming = with_halo(outgoing, (('lat', 0),), RIM).astype(jnp.float32)]
    ppermute x4, waiting for transfers between devices: 6.77 us -> 10.7 us  [shifted(): lax.ppermute(value, axis, [(i, (i + by) % length) for i in range(length)])]
    ppermute x2, starting transfers between devices: 19.6 us -> 17.8 us  [with_halo(): lax.ppermute(lax.slice_in_dim(block, block.shape[dim] - width, None, axis...]
  transfers between devices with their start and end apart: 8 -> 8, of which waited for: 4 -> 5; matrix products, arithmetic and copies ran while one was open for 9% -> 5% of each run, Pallas kernels for 4% -> 0%
where the time goes in v1:
time: 93.4 us; the launch traced here: 91.7 us
  starting transfers between devices  40.9 us (44%)
  waiting for transfers between devices  22.5 us (24%)
  Pallas kernels  19.8 us (21%)
  other arithmetic  5.36 us (6%)
  local copies, waits for them, and re-layouts  2.63 us (3%)
    pallas_call x1, Pallas kernels, block_partials(): pl.pallas_call(_block_kernel, grid=(rows,), in_specs=[pl.BlockSpec(memory...  19.8 us
    ppermute x4, starting transfers between devices, shifted(): lax.ppermute(value, axis, [(i, (i + by) % length) for i in range(length)])  19.2 us
    ppermute x2, starting transfers between devices, with_halo(): lax.ppermute(lax.slice_in_dim(block, block.shape[dim] - width, None, axis...  17.8 us
    ppermute x4, waiting for transfers between devices, shifted(): lax.ppermute(value, axis, [(i, (i + by) % length) for i in range(length)])  10.7 us
    ppermute x2, waiting for transfers between devices, with_halo(): lax.ppermute(lax.slice_in_dim(block, 0, width, axis=dim), axis, backward)  10.6 us
    ppermute x2, starting transfers between devices, with_halo(): lax.ppermute(lax.slice_in_dim(block, 0, width, axis=dim), axis, backward)  3.97 us
  transfers between devices with their start and end apart: 8, of which 5 were waited for; matrix products, arithmetic and copies ran while one was open for 5% of the time, Pallas kernels for 0%

profile of v1, /device:TPU:7, one launch (start us, length us, event | category | flops | bytes accessed | tf_op | source)
XLA Modules:
  0.0 91.7 jit_solution(17835681871192378350)
XLA Ops:
  0.0 11.1 %collective-permute-start = (s32[96,3]{0,1:T(4,128)}, s32[96,3]{0,1:T(4,128)S(1)}, u32[]{:S(2)}, u32[]{:S(2)}) collective-permute-start(s32[96,3]{0,1:T(4,128)} %param.10), channel_id=1, source_target_pairs={{0,32},{32,64},{64,96},{96,128},{128,160},{160,192},{192,224},{224... | collective-permute-start | bytes 3464 | tf_op jit(solution)/shard_map/ppermute | solution.py:22
  11.1 1.9 %collective-permute-start.1 = (s32[96,3]{0,1:T(4,128)}, s32[96,3]{0,1:T(4,128)S(1)}, u32[]{:S(2)}, u32[]{:S(2)}) collective-permute-start(s32[96,3]{0,1:T(4,128)} %param.10), channel_id=1, source_target_pairs={{32,0},{64,32},{96,64},{128,96},{160,128},{192,160},{224,192},{256... | collective-permute-start | bytes 3464 | tf_op jit(solution)/shard_map/ppermute | solution.py:25
  13.0 3.2 %collective-permute-start.2 = (bf16[4,128,512]{2,1,0:T(8,128)(2,1)}, bf16[4,128,512]{2,1,0:T(8,128)(2,1)S(1)}, u32[]{:S(2)}, u32[]{:S(2)}) collective-permute-start(bf16[4,128,512]{2,1,0:T(8,128)(2,1)} %local_ref.1), channel_id=1, source_target_pairs={{0,1},{1,2},{2,3},{3,4},{4,5},{5,6},{6,7},{7,8},{8,9},{9,10},{10,1... | collective-permute-start | bytes 1572872 | tf_op jit(solution)/shard_map/ppermute | solution.py:14
  16.3 6.5 %collective-permute-start.4 = (bf16[4,128,512]{2,1,0:T(8,128)(2,1)}, bf16[4,128,512]{2,1,0:T(8,128)(2,1)S(1)}, u32[]{:S(2)}, u32[]{:S(2)}) collective-permute-start(bf16[4,128,512]{2,1,0:T(8,128)(2,1)} %local_ref.1), channel_id=1, source_target_pairs={{0,31},{1,0},{2,1},{3,2},{4,3},{5,4},{6,5},{7,6},{8,7},{9,8},{10,9... | collective-permute-start | bytes 1572872 | tf_op jit(solution)/shard_map/ppermute | solution.py:14
  22.8 0.7 compare_and_fusion
  23.5 0.8 add_bitcast_fusion.4
  24.3 0.7 broadcast_compare_fusion
  25.0 0.9 fusion.4
  25.9 0.7 pad_convert_fusion.taps_ref
  26.6 0.0 collective-permute-done
  26.6 0.0 collective-permute-done.1
  26.6 0.1 pad_add_fusion.1
  26.7 2.6 %collective-permute-done.2.west_ref = bf16[4,128,512]{2,1,0:T(8,128)(2,1)S(1)} collective-permute-done((bf16[4,128,512]{2,1,0:T(8,128)(2,1)}, bf16[4,128,512]{2,1,0:T(8,128)(2,1)S(1)}, u32[]{:S(2)}, u32[]{:S(2)}) %collective-permute-start.2) | collective-permute-done | bytes 524320 | tf_op jit(solution)/shard_map/ppermute | solution.py:14
  29.3 0.0 copy-start.2
  29.3 1.9 %collective-permute-start.3 = (bf16[4,128,512]{2,1,0:T(8,128)(2,1)S(1)}, bf16[4,128,512]{2,1,0:T(8,128)(2,1)S(1)}, u32[]{:S(2)}, u32[]{:S(2)}) collective-permute-start(bf16[4,128,512]{2,1,0:T(8,128)(2,1)S(1)} %collective-permute-done.2.west_ref), channel_id=1, source_target_pairs={{0,1},{1,2},{2,3},{3,4},{4,5},{5,6},{6,7},{7,8},{8,9},{9,10},{10,1... | collective-permute-start | bytes 1572872 | tf_op jit(solution)/shard_map/ppermute | solution.py:14
  31.3 0.0 collective-permute-done.4.east_ref
  31.3 0.0 copy-start.3
  31.3 7.5 %collective-permute-start.5 = (bf16[4,128,512]{2,1,0:T(8,128)(2,1)S(1)}, bf16[4,128,512]{2,1,0:T(8,128)(2,1)S(1)}, u32[]{:S(2)}, u32[]{:S(2)}) collective-permute-start(bf16[4,128,512]{2,1,0:T(8,128)(2,1)S(1)} %collective-permute-done.4.east_ref), channel_id=1, source_target_pairs={{0,31},{1,0},{2,1},{3,2},{4,3},{5,4},{6,5},{7,6},{8,7},{9,8},{10,9... | collective-permute-start | bytes 1572872 | tf_op jit(solution)/shard_map/ppermute | solution.py:14
  38.8 0.1 pad_add_fusion
  38.9 0.3 fusion.6
  39.2 0.7 reshape_reshape.3.counts_ref
  39.9 6.0 %collective-permute-done.3.far_west_ref = bf16[4,128,512]{2,1,0:T(8,128)(2,1)S(1)} collective-permute-done((bf16[4,128,512]{2,1,0:T(8,128)(2,1)S(1)}, bf16[4,128,512]{2,1,0:T(8,128)(2,1)S(1)}, u32[]{:S(2)}, u32[]{:S(2)}) %collective-permute-start.3) | collective-permute-done | bytes 524320 | tf_op jit(solution)/shard_map/ppermute | solution.py:14
  45.9 0.0 copy-start.4
  45.9 2.0 %collective-permute-done.5.far_east_ref = bf16[4,128,512]{2,1,0:T(8,128)(2,1)S(1)} collective-permute-done((bf16[4,128,512]{2,1,0:T(8,128)(2,1)S(1)}, bf16[4,128,512]{2,1,0:T(8,128)(2,1)S(1)}, u32[]{:S(2)}, u32[]{:S(2)}) %collective-permute-start.5) | collective-permute-done | bytes 524320 | tf_op jit(solution)/shard_map/ppermute | solution.py:14
  48.0 0.0 copy-done.2
  48.0 0.0 copy-done.3
  48.0 0.0 copy-done.4
  48.0 0.0 copy-start.5
  48.0 0.8 copy-done.5
  48.8 19.8 %shard_map.64 = (bf16[4,128,512]{2,1,0:T(8,128)(2,1)}, f32[4,128,512]{2,1,0:T(8,128)}) custom-call(f32[288]{0:T(512)} %reshape_reshape.3.counts_ref, f32[4,9,640]{2,1,0:T(8,128)} %pad_convert_fusion.taps_ref, bf16[4,128,512]{2,1,0:T(8,128)(2,1)} %copy-done.4, bf16[4,128,512]{2,1,0:T(8,128)(2,1)} %copy-done.2, bf16[4,128,512]{2,1,0:T(8,128)(2,1)} %local_ref.1, ...), custom_call_target="tpu_custom_call" | custom-call | tf_op jit(solution)/shard_map/pallas_call | solution.py:114
  68.6 0.0 copy-start
  68.6 1.1 %fusion.12 = (bf16[2,128,512]{2,1,0:T(8,128)(2,1)S(1)}, bf16[2,128,512]{2,1,0:T(8,128)(2,1)S(1)}) fusion(bf16[4,128,512]{2,1,0:T(8,128)(2,1)} %get-tuple-element.8), kind=kLoop, calls=%fused_computation.35 | loop fusion | bytes 1048576 | tf_op jit(solution)/shard_map/slice | solution.py:23
  69.8 6.7 %collective-permute-start.6 = (bf16[2,128,512]{2,1,0:T(8,128)(2,1)S(1)}, bf16[2,128,512]{2,1,0:T(8,128)(2,1)S(1)}, u32[]{:S(2)}, u32[]{:S(2)}) collective-permute-start(bf16[2,128,512]{2,1,0:T(8,128)(2,1)S(1)} %get-tuple-element.9), channel_id=1, source_target_pairs={{0,32},{32,64},{64,96},{96,128},{128,160},{160,192},{192,224},{224... | collective-permute-start | bytes 786440 | tf_op jit(solution)/shard_map/ppermute | solution.py:22
  76.4 0.0 copy-start.1
  76.4 0.0 copy-start.6
  76.4 0.0 copy-start.7
  76.5 2.1 %collective-permute-start.7 = (bf16[2,128,512]{2,1,0:T(8,128)(2,1)S(1)}, bf16[2,128,512]{2,1,0:T(8,128)(2,1)S(1)}, u32[]{:S(2)}, u32[]{:S(2)}) collective-permute-start(bf16[2,128,512]{2,1,0:T(8,128)(2,1)S(1)} %get-tuple-element.10), channel_id=1, source_target_pairs={{32,0},{64,32},{96,64},{128,96},{160,128},{192,160},{224,192},{256... | collective-permute-start | bytes 786440 | tf_op jit(solution)/shard_map/ppermute | solution.py:25
  78.5 1.2 %collective-permute-done.6 = bf16[2,128,512]{2,1,0:T(8,128)(2,1)S(1)} collective-permute-done((bf16[2,128,512]{2,1,0:T(8,128)(2,1)S(1)}, bf16[2,128,512]{2,1,0:T(8,128)(2,1)S(1)}, u32[]{:S(2)}, u32[]{:S(2)}) %collective-permute-start.6) | collective-permute-done | bytes 262176 | tf_op jit(solution)/shard_map/ppermute | solution.py:22
  79.7 10.6 %collective-permute-done.7 = bf16[2,128,512]{2,1,0:T(8,128)(2,1)S(1)} collective-permute-done((bf16[2,128,512]{2,1,0:T(8,128)(2,1)S(1)}, bf16[2,128,512]{2,1,0:T(8,128)(2,1)S(1)}, u32[]{:S(2)}, u32[]{:S(2)}) %collective-permute-start.7) | collective-permute-done | bytes 262176 | tf_op jit(solution)/shard_map/ppermute | solution.py:25
  90.3 0.0 copy-done
  90.3 0.2 maximum_convert_fusion
  90.5 0.0 copy-done.1
  90.5 0.0 copy-done.6
  90.5 0.0 copy-done.7
  90.5 1.2 %fusion.3 = bf16[4,128,512]{2,1,0:T(8,128)(2,1)} fusion(f32[4,128,512]{2,1,0:T(8,128)S(1)} %copy-done.1, f32[8,128,512]{2,1,0:T(8,128)S(1)} %maximum_convert_fusion, f32[2,128,512]{2,1,0:T(8,128)S(1)} %maximum_convert_fusion.1, f32[4]{0:T(128)S(1)} %copy-done.6, pred[4]{0:T(512)(128)(4,1)S(1)} %copy-done.7), kind=kLoop, calls=%fused_computation.4 | loop fusion | flops 1310720 | bytes 3145748 | tf_op jit(solution)/shard_map/convert_element_type | solution.py:157
  (6 shorter events, 0.1 us)
Async XLA Ops:
  0.0 26.6 %collective-permute-start = (s32[96,3]{0,1:T(4,128)}, s32[96,3]{0,1:T(4,128)S(1)}, u32[]{:S(2)}, u32[]{:S(2)}) collective-permute-start(s32[96,3]{0,1:T(4,128)} %param.10), channel_id=1, source_target_pairs={{0,32},{32,64},{64,96},{96,128},{128,160},{160,192},{192,224},{224... | collective-permute-start | bytes 3464 | tf_op jit(solution)/shard_map/ppermute | solution.py:22
  11.1 15.5 %collective-permute-start.1 = (s32[96,3]{0,1:T(4,128)}, s32[96,3]{0,1:T(4,128)S(1)}, u32[]{:S(2)}, u32[]{:S(2)}) collective-permute-start(s32[96,3]{0,1:T(4,128)} %param.10), channel_id=1, source_target_pairs={{32,0},{64,32},{96,64},{128,96},{160,128},{192,160},{224,192},{256... | collective-permute-start | bytes 3464 | tf_op jit(solution)/shard_map/ppermute | solution.py:25
  13.0 16.3 %collective-permute-start.2 = (bf16[4,128,512]{2,1,0:T(8,128)(2,1)}, bf16[4,128,512]{2,1,0:T(8,128)(2,1)S(1)}, u32[]{:S(2)}, u32[]{:S(2)}) collective-permute-start(bf16[4,128,512]{2,1,0:T(8,128)(2,1)} %local_ref.1), channel_id=1, source_target_pairs={{0,1},{1,2},{2,3},{3,4},{4,5},{5,6},{6,7},{7,8},{8,9},{9,10},{10,1... | collective-permute-start | bytes 1572872 | tf_op jit(solution)/shard_map/ppermute | solution.py:14
  16.3 15.0 %collective-permute-start.4 = (bf16[4,128,512]{2,1,0:T(8,128)(2,1)}, bf16[4,128,512]{2,1,0:T(8,128)(2,1)S(1)}, u32[]{:S(2)}, u32[]{:S(2)}) collective-permute-start(bf16[4,128,512]{2,1,0:T(8,128)(2,1)} %local_ref.1), channel_id=1, source_target_pairs={{0,31},{1,0},{2,1},{3,2},{4,3},{5,4},{6,5},{7,6},{8,7},{9,8},{10,9... | collective-permute-start | bytes 1572872 | tf_op jit(solution)/shard_map/ppermute | solution.py:14
  29.3 18.6 %copy-start.2 = (bf16[4,128,512]{2,1,0:T(8,128)(2,1)}, bf16[4,128,512]{2,1,0:T(8,128)(2,1)S(1)}, u32[]{:S(2)}) copy-start(bf16[4,128,512]{2,1,0:T(8,128)(2,1)S(1)} %collective-permute-done.2.west_ref) | copy-start | bytes 1572868
  29.3 16.6 %collective-permute-start.3 = (bf16[4,128,512]{2,1,0:T(8,128)(2,1)S(1)}, bf16[4,128,512]{2,1,0:T(8,128)(2,1)S(1)}, u32[]{:S(2)}, u32[]{:S(2)}) collective-permute-start(bf16[4,128,512]{2,1,0:T(8,128)(2,1)S(1)} %collective-permute-done.2.west_ref), channel_id=1, source_target_pairs={{0,1},{1,2},{2,3},{3,4},{4,5},{5,6},{6,7},{7,8},{8,9},{9,10},{10,1... | collective-permute-start | bytes 1572872 | tf_op jit(solution)/shard_map/ppermute | solution.py:14
  31.3 16.7 %copy-start.3 = (bf16[4,128,512]{2,1,0:T(8,128)(2,1)}, bf16[4,128,512]{2,1,0:T(8,128)(2,1)S(1)}, u32[]{:S(2)}) copy-start(bf16[4,128,512]{2,1,0:T(8,128)(2,1)S(1)} %collective-permute-done.4.east_ref) | copy-start | bytes 1572868
  31.3 16.7 %collective-permute-start.5 = (bf16[4,128,512]{2,1,0:T(8,128)(2,1)S(1)}, bf16[4,128,512]{2,1,0:T(8,128)(2,1)S(1)}, u32[]{:S(2)}, u32[]{:S(2)}) collective-permute-start(bf16[4,128,512]{2,1,0:T(8,128)(2,1)S(1)} %collective-permute-done.4.east_ref), channel_id=1, source_target_pairs={{0,31},{1,0},{2,1},{3,2},{4,3},{5,4},{6,5},{7,6},{8,7},{9,8},{10,9... | collective-permute-start | bytes 1572872 | tf_op jit(solution)/shard_map/ppermute | solution.py:14
  45.9 2.0 %copy-start.4 = (bf16[4,128,512]{2,1,0:T(8,128)(2,1)}, bf16[4,128,512]{2,1,0:T(8,128)(2,1)S(1)}, u32[]{:S(2)}) copy-start(bf16[4,128,512]{2,1,0:T(8,128)(2,1)S(1)} %collective-permute-done.3.far_west_ref) | copy-start | bytes 1572868
  48.0 0.8 copy-start.5
  68.6 21.7 %copy-start = (bf16[4,128,512]{2,1,0:T(8,128)(2,1)S(1)}, bf16[4,128,512]{2,1,0:T(8,128)(2,1)}, u32[]{:S(2)}) copy-start(bf16[4,128,512]{2,1,0:T(8,128)(2,1)} %get-tuple-element.8) | copy-start | bytes 1572868
  69.8 10.0 %collective-permute-start.6 = (bf16[2,128,512]{2,1,0:T(8,128)(2,1)S(1)}, bf16[2,128,512]{2,1,0:T(8,128)(2,1)S(1)}, u32[]{:S(2)}, u32[]{:S(2)}) collective-permute-start(bf16[2,128,512]{2,1,0:T(8,128)(2,1)S(1)} %get-tuple-element.9), channel_id=1, source_target_pairs={{0,32},{32,64},{64,96},{96,128},{128,160},{160,192},{192,224},{224... | collective-permute-start | bytes 786440 | tf_op jit(solution)/shard_map/ppermute | solution.py:22
  76.4 14.1 %copy-start.1 = (f32[4,128,512]{2,1,0:T(8,128)S(1)}, f32[4,128,512]{2,1,0:T(8,128)}, u32[]{:S(2)}) copy-start(f32[4,128,512]{2,1,0:T(8,128)} %get-tuple-element.7) | copy-start | bytes 3145732
  76.4 14.1 %copy-start.6 = (f32[4]{0:T(128)S(1)}, f32[4]{0:T(128)}, u32[]{:S(2)}) copy-start(f32[4]{0:T(128)} %param.9) | copy-start | bytes 52
  76.4 14.1 %copy-start.7 = (pred[4]{0:T(512)(128)(4,1)S(1)}, pred[4]{0:T(512)(128)(4,1)}, u32[]{:S(2)}) copy-start(pred[4]{0:T(512)(128)(4,1)} %constant.24.clone.1) | copy-start | bytes 16
  76.5 13.8 %collective-permute-start.7 = (bf16[2,128,512]{2,1,0:T(8,128)(2,1)S(1)}, bf16[2,128,512]{2,1,0:T(8,128)(2,1)S(1)}, u32[]{:S(2)}, u32[]{:S(2)}) collective-permute-start(bf16[2,128,512]{2,1,0:T(8,128)(2,1)S(1)} %get-tuple-element.10), channel_id=1, source_target_pairs={{32,0},{64,32},{96,64},{128,96},{160,128},{192,160},{224,192},{256... | collective-permute-start | bytes 786440 | tf_op jit(solution)/shard_map/ppermute | solution.py:25

commit v2 on v1

--- a/solution.py
+++ b/solution.py
@@ -58,76 +58,95 @@
     return table.reshape(output_rows, kinds, input_rows)
 
 
-def _block_kernel(counts_ref, taps_ref, far_west_ref, west_ref, local_ref, east_ref, far_east_ref,
-                  weight_ref, edge_ref, inner_ref, window_ref, mixed_ref):
-    row = pl.program_id(0)
-    rows = pl.num_programs(0)
+def _toeplitz_kernel(taps_ref, out_ref):
     kinds = taps_ref.shape[1]
-    cols = local_ref.shape[1]
+    cols = out_ref.shape[2]
+    for kind in range(kinds):
+        row = taps_ref[0, kind : kind + 1, :]
+        wide = jnp.broadcast_to(row, (cols, row.shape[1]))
+        out_ref[0, kind] = pltpu.roll(wide, 0, 1, stride=1, stride_axis=0).astype(out_ref.dtype)
+
+
+def band_matrix(short_taps, cols, window):
+    rows, kinds, length = short_taps.shape
+    padded = jnp.pad(short_taps.astype(jnp.float32), ((0, 0), (0, 0), (0, window - length)))
+    return pl.pallas_call(
+        _toeplitz_kernel,
+        grid=(rows,),
+        in_specs=[pl.BlockSpec((1, kinds, window), lambda i: (i, 0, 0))],
+        out_specs=pl.BlockSpec((1, kinds, cols, window), lambda i: (i, 0, 0, 0)),
+        out_shape=jax.ShapeDtypeStruct((rows, kinds, cols, window), jnp.bfloat16),
+    )(padded)
+
+
+def _block_kernel(counts_ref, band_ref, far_west_ref, west_ref, local_ref, east_ref, far_east_ref,
+                  weight_ref, edge_ref, inner_ref, window_ref, response_ref, mixed_ref, total_ref):
+    kind = pl.program_id(0)
+    kinds = pl.num_programs(0)
+    input_rows, cols, _ = local_ref.shape
+    output_rows = input_rows + 2 * RIM
     parts = (far_west_ref, west_ref, local_ref, east_ref, far_east_ref)
-    for index, part in enumerate(parts):
-        window_ref[index * cols : (index + 1) * cols, :] = part[0]
-    for kind in range(kinds):
-        taps = taps_ref[0, kind : kind + 1, :]
-        wide = jnp.broadcast_to(taps, (cols, taps.shape[1]))
-        band = pltpu.roll(wide, 0, 1, stride=1, stride_axis=0).astype(jnp.bfloat16)
-        response = jnp.dot(band, window_ref[...], preferred_element_type=jnp.float32)
-        mixed_ref[kind, row] = jnp.dot(
-            response.astype(jnp.bfloat16), weight_ref[kind], preferred_element_type=jnp.float32
-        )
 
-    @pl.when(row == rows - 1)
+    @pl.when(kind == 0)
     def _():
-        input_rows = mixed_ref.shape[1]
-        output_rows = input_rows + 2 * RIM
-        chunk = 16
+        for index, part in enumerate(parts):
+            window_ref[:, index * cols : (index + 1) * cols, :] = part[...]
+        total_ref[...] = jnp.zeros_like(total_ref)
 
-        def body(step, carry):
-            start = pl.multiple_of(step * chunk, chunk)
-            edge_index = 0
-            for out_row in range(output_rows):
-                total = None
-                for kind in range(kinds):
-                    for in_row in range(max(0, out_row - 2 * RIM), min(input_rows, out_row + 1)):
-                        scale = counts_ref[(out_row * kinds + kind) * input_rows + in_row]
-                        term = scale * mixed_ref[kind, in_row, pl.ds(start, chunk), :]
-                        total = term if total is None else total + term
-                if RIM <= out_row < RIM + input_rows:
-                    inner_ref[out_row - RIM, pl.ds(start, chunk), :] = total
-                else:
-                    edge_ref[edge_index, pl.ds(start, chunk), :] = total.astype(edge_ref.dtype)
-                    edge_index += 1
-            return carry
+    for in_row in range(input_rows):
+        response = jnp.dot(band_ref[in_row, 0], window_ref[in_row], preferred_element_type=jnp.float32)
+        response_ref[in_row * cols : (in_row + 1) * cols, :] = response.astype(jnp.bfloat16)
+    mixed_ref[...] = jnp.dot(response_ref[...], weight_ref[0], preferred_element_type=jnp.float32)
+    chunk = 16
 
-        lax.fori_loop(0, cols // chunk, body, 0)
+    def body(step, carry):
+        start = pl.multiple_of(step * chunk, chunk)
+        pieces = [mixed_ref[pl.ds(in_row * cols + start, chunk), :] for in_row in range(input_rows)]
+        for out_row in range(output_rows):
+            total = total_ref[out_row, pl.ds(start, chunk), :]
+            for in_row in range(max(0, out_row - 2 * RIM), min(input_rows, out_row + 1)):
+                scale = counts_ref[(out_row * kinds + kind) * input_rows + in_row]
+                total = total + scale * pieces[in_row]
+            total_ref[out_row, pl.ds(start, chunk), :] = total
+        return carry
+
+    lax.fori_loop(0, cols // chunk, body, 0)
+
+    @pl.when(kind == kinds - 1)
+    def _():
+        inner_ref[...] = total_ref[RIM : RIM + input_rows]
+        edge_ref[:RIM] = total_ref[:RIM].astype(edge_ref.dtype)
+        edge_ref[RIM:] = total_ref[RIM + input_rows :].astype(edge_ref.dtype)
 
 
 def block_partials(counts, short_taps, parts, mix_weight):
     rows, cols, channels = parts[0].shape
     kinds = short_taps.shape[1]
     window = cols * len(parts)
-    padded = jnp.pad(
-        short_taps.astype(jnp.float32), ((0, 0), (0, 0), (0, window - short_taps.shape[2]))
-    )
-    part_spec = pl.BlockSpec((1, cols, channels), lambda i: (i, 0, 0))
-    whole = lambda shape: pl.BlockSpec(shape, lambda i: (0,) * len(shape))
+    band = band_matrix(short_taps, cols, window)
+    whole = lambda shape: pl.BlockSpec(shape, lambda k: (0,) * len(shape))
     return pl.pallas_call(
         _block_kernel,
-        grid=(rows,),
-        in_specs=[pl.BlockSpec(memory_space=pltpu.SMEM), pl.BlockSpec((1, kinds, window), lambda i: (i, 0, 0))]
-        + [part_spec] * len(parts)
-        + [whole(mix_weight.shape)],
+        grid=(kinds,),
+        in_specs=[
+            pl.BlockSpec(memory_space=pltpu.SMEM),
+            pl.BlockSpec((rows, 1, cols, window), lambda k: (0, k, 0, 0)),
+        ]
+        + [whole(parts[0].shape)] * len(parts)
+        + [pl.BlockSpec((1,) + mix_weight.shape[1:], lambda k: (k, 0, 0))],
         out_specs=[whole((2 * RIM, cols, channels)), whole((rows, cols, channels))],
         out_shape=[
             jax.ShapeDtypeStruct((2 * RIM, cols, channels), jnp.bfloat16),
             jax.ShapeDtypeStruct((rows, cols, channels), jnp.float32),
         ],
         scratch_shapes=[
-            pltpu.VMEM((window, channels), jnp.bfloat16),
-            pltpu.VMEM((kinds, rows, cols, mix_weight.shape[2]), jnp.float32),
+            pltpu.VMEM((rows, window, channels), jnp.bfloat16),
+            pltpu.VMEM((rows * cols, channels), jnp.bfloat16),
+            pltpu.VMEM((rows * cols, mix_weight.shape[2]), jnp.float32),
+            pltpu.VMEM((rows + 2 * RIM, cols, mix_weight.shape[2]), jnp.float32),
         ],
         compiler_params=pltpu.CompilerParams(dimension_semantics=("arbitrary",)),
-    )(counts.reshape(-1), padded, *parts, mix_weight)
+    )(counts.reshape(-1), band, *parts, mix_weight)
 
 
 def on_device(field, lon_width, lon_taps, row_scale, support, mix_weight):

time: 93.4 us -> 91.3 us (0.978); the launches traced: 91.7 us -> 90.7 us
  waiting for transfers between devices: 22.5 us -> 19.3 us
  starting transfers between devices: 40.9 us -> 42.5 us
    ppermute x4, waiting for transfers between devices: 10.7 us -> 7.56 us  [shifted(): lax.ppermute(value, axis, [(i, (i + by) % length) for i in range(length)])]
    ppermute x2, starting transfers between devices: 17.8 us -> 19.6 us  [with_halo(): lax.ppermute(lax.slice_in_dim(block, block.shape[dim] - width, None, axis...]
    pallas_call x1 -> x2, Pallas kernels: 19.8 us -> 20.2 us  [the longest x1 15.5 us: block_partials(): pl.pallas_call(_block_kernel, grid=(kinds,), in_specs=[pl.BlockSpec(memor...]
  transfers between devices with their start and end apart: 8 -> 8, of which waited for: 5 -> 4; matrix products, arithmetic and copies ran while one was open for 5% -> 5% of each run, Pallas kernels for 0% -> 5%
where the time goes in v2:
time: 91.3 us; the launch traced here: 90.7 us
  starting transfers between devices  42.5 us (47%)
  Pallas kernels  20.2 us (22%)
  waiting for transfers between devices  19.3 us (21%)
  other arithmetic  5.37 us (6%)
  local copies, waits for them, and re-layouts  2.69 us (3%)
    ppermute x2, starting transfers between devices, with_halo(): lax.ppermute(lax.slice_in_dim(block, block.shape[dim] - width, None, axis...  19.6 us
    ppermute x4, starting transfers between devices, shifted(): lax.ppermute(value, axis, [(i, (i + by) % length) for i in range(length)])  18.9 us
    pallas_call x1, Pallas kernels, block_partials(): pl.pallas_call(_block_kernel, grid=(kinds,), in_specs=[pl.BlockSpec(memor...  15.5 us
    ppermute x2, waiting for transfers between devices, with_halo(): lax.ppermute(lax.slice_in_dim(block, 0, width, axis=dim), axis, backward)  10.6 us
    ppermute x4, waiting for transfers between devices, shifted(): lax.ppermute(value, axis, [(i, (i + by) % length) for i in range(length)])  7.56 us
    pallas_call x1, Pallas kernels, band_matrix(): pl.pallas_call(_toeplitz_kernel, grid=(rows,), in_specs=[pl.BlockSpec((1,...  4.75 us
    ppermute x2, starting transfers between devices, with_halo(): lax.ppermute(lax.slice_in_dim(block, 0, width, axis=dim), axis, backward)  3.97 us
  transfers between devices with their start and end apart: 8, of which 4 were waited for; matrix products, arithmetic and copies ran while one was open for 5% of the time, Pallas kernels for 5%

profile of v2, /device:TPU:7, one launch (start us, length us, event | category | flops | bytes accessed | tf_op | source)
XLA Modules:
  0.0 90.7 jit_solution(10430068746036106823)
XLA Ops:
  0.0 11.1 %collective-permute-start = (s32[96,3]{0,1:T(4,128)}, s32[96,3]{0,1:T(4,128)S(1)}, u32[]{:S(2)}, u32[]{:S(2)}) collective-permute-start(s32[96,3]{0,1:T(4,128)} %param.10), channel_id=1, source_target_pairs={{0,32},{32,64},{64,96},{96,128},{128,160},{160,192},{192,224},{224... | collective-permute-start | bytes 3464 | tf_op jit(solution)/shard_map/ppermute | solution.py:22
  11.1 1.9 %collective-permute-start.1 = (s32[96,3]{0,1:T(4,128)}, s32[96,3]{0,1:T(4,128)S(1)}, u32[]{:S(2)}, u32[]{:S(2)}) collective-permute-start(s32[96,3]{0,1:T(4,128)} %param.10), channel_id=1, source_target_pairs={{32,0},{64,32},{96,64},{128,96},{160,128},{192,160},{224,192},{256... | collective-permute-start | bytes 3464 | tf_op jit(solution)/shard_map/ppermute | solution.py:25
  13.0 3.2 %collective-permute-start.2 = (bf16[4,128,512]{2,1,0:T(8,128)(2,1)}, bf16[4,128,512]{2,1,0:T(8,128)(2,1)S(1)}, u32[]{:S(2)}, u32[]{:S(2)}) collective-permute-start(bf16[4,128,512]{2,1,0:T(8,128)(2,1)} %local_ref.1), channel_id=1, source_target_pairs={{0,1},{1,2},{2,3},{3,4},{4,5},{5,6},{6,7},{7,8},{8,9},{9,10},{10,1... | collective-permute-start | bytes 1572872 | tf_op jit(solution)/shard_map/ppermute | solution.py:14
  16.3 6.5 %collective-permute-start.4 = (bf16[4,128,512]{2,1,0:T(8,128)(2,1)}, bf16[4,128,512]{2,1,0:T(8,128)(2,1)S(1)}, u32[]{:S(2)}, u32[]{:S(2)}) collective-permute-start(bf16[4,128,512]{2,1,0:T(8,128)(2,1)} %local_ref.1), channel_id=1, source_target_pairs={{0,31},{1,0},{2,1},{3,2},{4,3},{5,4},{6,5},{7,6},{8,7},{9,8},{10,9... | collective-permute-start | bytes 1572872 | tf_op jit(solution)/shard_map/ppermute | solution.py:14
  22.8 0.7 compare_and_fusion
  23.5 0.8 add_bitcast_fusion.4
  24.3 0.7 broadcast_compare_fusion
  25.0 0.9 %fusion.4 = bf16[4,9,513]{2,1,0:T(8,128)(2,1)S(1)} fusion(f32[4,9,513]{2,0,1:T(4,128)} %param.8, pred[4,513]{1,0:T(4,128)(4,1)S(1)} %broadcast_compare_fusion), kind=kLoop, calls=%fused_computation.8 | loop fusion | flops 18468 | bytes 112860 | tf_op jit(solution)/shard_map/convert_element_type | solution.py:35
  25.9 0.7 pad_convert_fusion.taps_ref
  26.6 4.8 %shard_map.64.band_ref = bf16[4,9,128,640]{3,2,1,0:T(8,128)(2,1)} custom-call(f32[4,9,640]{2,1,0:T(8,128)} %pad_convert_fusion.taps_ref), custom_call_target="tpu_custom_call" | custom-call | tf_op jit(solution)/shard_map/pallas_call | solution.py:73
  31.4 0.0 collective-permute-done
  31.4 0.0 collective-permute-done.1
  31.4 0.1 pad_add_fusion.1
  31.5 0.0 collective-permute-done.2.west_ref
  31.5 0.0 copy-start.2
  31.5 1.9 %collective-permute-start.3 = (bf16[4,128,512]{2,1,0:T(8,128)(2,1)S(1)}, bf16[4,128,512]{2,1,0:T(8,128)(2,1)S(1)}, u32[]{:S(2)}, u32[]{:S(2)}) collective-permute-start(bf16[4,128,512]{2,1,0:T(8,128)(2,1)S(1)} %collective-permute-done.2.west_ref), channel_id=1, source_target_pairs={{0,1},{1,2},{2,3},{3,4},{4,5},{5,6},{6,7},{7,8},{8,9},{9,10},{10,1... | collective-permute-start | bytes 1572872 | tf_op jit(solution)/shard_map/ppermute | solution.py:14
  33.4 0.0 collective-permute-done.4.east_ref
  33.5 0.0 copy-start.3
  33.5 7.3 %collective-permute-start.5 = (bf16[4,128,512]{2,1,0:T(8,128)(2,1)S(1)}, bf16[4,128,512]{2,1,0:T(8,128)(2,1)S(1)}, u32[]{:S(2)}, u32[]{:S(2)}) collective-permute-start(bf16[4,128,512]{2,1,0:T(8,128)(2,1)S(1)} %collective-permute-done.4.east_ref), channel_id=1, source_target_pairs={{0,31},{1,0},{2,1},{3,2},{4,3},{5,4},{6,5},{7,6},{8,7},{9,8},{10,9... | collective-permute-start | bytes 1572872 | tf_op jit(solution)/shard_map/ppermute | solution.py:14
  40.8 0.1 pad_add_fusion
  40.8 0.3 fusion.6
  41.1 0.7 reshape_reshape.3.counts_ref
  41.8 5.8 %collective-permute-done.3.far_west_ref = bf16[4,128,512]{2,1,0:T(8,128)(2,1)S(1)} collective-permute-done((bf16[4,128,512]{2,1,0:T(8,128)(2,1)S(1)}, bf16[4,128,512]{2,1,0:T(8,128)(2,1)S(1)}, u32[]{:S(2)}, u32[]{:S(2)}) %collective-permute-start.3) | collective-permute-done | bytes 524320 | tf_op jit(solution)/shard_map/ppermute | solution.py:14
  47.6 0.0 copy-start.4
  47.6 1.8 %collective-permute-done.5.far_east_ref = bf16[4,128,512]{2,1,0:T(8,128)(2,1)S(1)} collective-permute-done((bf16[4,128,512]{2,1,0:T(8,128)(2,1)S(1)}, bf16[4,128,512]{2,1,0:T(8,128)(2,1)S(1)}, u32[]{:S(2)}, u32[]{:S(2)}) %collective-permute-start.5) | collective-permute-done | bytes 524320 | tf_op jit(solution)/shard_map/ppermute | solution.py:14
  49.4 0.0 copy-done.2
  49.4 0.0 copy-done.3
  49.4 0.0 copy-done.4
  49.4 0.0 copy-start.5
  49.4 0.9 copy-done.5
  50.2 15.5 %shard_map.65 = (bf16[4,128,512]{2,1,0:T(8,128)(2,1)}, f32[4,128,512]{2,1,0:T(8,128)}) custom-call(f32[288]{0:T(512)} %reshape_reshape.3.counts_ref, bf16[4,9,128,640]{3,2,1,0:T(8,128)(2,1)} %shard_map.64.band_ref, bf16[4,128,512]{2,1,0:T(8,128)(2,1)} %copy-done.4, bf16[4,128,512]{2,1,0:T(8,128)(2,1)} %copy-done.2, bf16[4,128,512]{2,1,0:T(8,128)(2,1)} %local_ref.1, ...), custom_call_target="tpu_custom_call" | custom-call | tf_op jit(solution)/shard_map/pallas_call | solution.py:128
  65.7 0.0 copy-start
  65.7 1.1 %fusion.12 = (bf16[2,128,512]{2,1,0:T(8,128)(2,1)S(1)}, bf16[2,128,512]{2,1,0:T(8,128)(2,1)S(1)}) fusion(bf16[4,128,512]{2,1,0:T(8,128)(2,1)} %get-tuple-element.8), kind=kLoop, calls=%fused_computation.35 | loop fusion | bytes 1048576 | tf_op jit(solution)/shard_map/slice | solution.py:23
  66.8 8.5 %collective-permute-start.6 = (bf16[2,128,512]{2,1,0:T(8,128)(2,1)S(1)}, bf16[2,128,512]{2,1,0:T(8,128)(2,1)S(1)}, u32[]{:S(2)}, u32[]{:S(2)}) collective-permute-start(bf16[2,128,512]{2,1,0:T(8,128)(2,1)S(1)} %get-tuple-element.9), channel_id=1, source_target_pairs={{0,32},{32,64},{64,96},{96,128},{128,160},{160,192},{192,224},{224... | collective-permute-start | bytes 786440 | tf_op jit(solution)/shard_map/ppermute | solution.py:22
  75.4 0.0 copy-start.1
  75.4 0.0 copy-start.6
  75.4 0.0 copy-start.7
  75.4 2.1 %collective-permute-start.7 = (bf16[2,128,512]{2,1,0:T(8,128)(2,1)S(1)}, bf16[2,128,512]{2,1,0:T(8,128)(2,1)S(1)}, u32[]{:S(2)}, u32[]{:S(2)}) collective-permute-start(bf16[2,128,512]{2,1,0:T(8,128)(2,1)S(1)} %get-tuple-element.10), channel_id=1, source_target_pairs={{32,0},{64,32},{96,64},{128,96},{160,128},{192,160},{224,192},{256... | collective-permute-start | bytes 786440 | tf_op jit(solution)/shard_map/ppermute | solution.py:25
  77.5 1.2 %collective-permute-done.6 = bf16[2,128,512]{2,1,0:T(8,128)(2,1)S(1)} collective-permute-done((bf16[2,128,512]{2,1,0:T(8,128)(2,1)S(1)}, bf16[2,128,512]{2,1,0:T(8,128)(2,1)S(1)}, u32[]{:S(2)}, u32[]{:S(2)}) %collective-permute-start.6) | collective-permute-done | bytes 262176 | tf_op jit(solution)/shard_map/ppermute | solution.py:22
  78.7 10.6 %collective-permute-done.7 = bf16[2,128,512]{2,1,0:T(8,128)(2,1)S(1)} collective-permute-done((bf16[2,128,512]{2,1,0:T(8,128)(2,1)S(1)}, bf16[2,128,512]{2,1,0:T(8,128)(2,1)S(1)}, u32[]{:S(2)}, u32[]{:S(2)}) %collective-permute-start.7) | collective-permute-done | bytes 262176 | tf_op jit(solution)/shard_map/ppermute | solution.py:25
  89.3 0.0 copy-done
  89.3 0.2 maximum_convert_fusion
  89.5 0.0 copy-done.1
  89.5 0.0 copy-done.6
  89.5 0.0 copy-done.7
  89.5 1.2 %fusion.3 = bf16[4,128,512]{2,1,0:T(8,128)(2,1)} fusion(f32[4,128,512]{2,1,0:T(8,128)S(1)} %copy-done.1, f32[8,128,512]{2,1,0:T(8,128)S(1)} %maximum_convert_fusion, f32[2,128,512]{2,1,0:T(8,128)S(1)} %maximum_convert_fusion.1, f32[4]{0:T(128)S(1)} %copy-done.6, pred[4]{0:T(512)(128)(4,1)S(1)} %copy-done.7), kind=kLoop, calls=%fused_computation.4 | loop fusion | flops 1310720 | bytes 3145748 | tf_op jit(solution)/shard_map/convert_element_type | solution.py:176
  (6 shorter events, 0.1 us)
Async XLA Ops:
  0.0 31.4 %collective-permute-start = (s32[96,3]{0,1:T(4,128)}, s32[96,3]{0,1:T(4,128)S(1)}, u32[]{:S(2)}, u32[]{:S(2)}) collective-permute-start(s32[96,3]{0,1:T(4,128)} %param.10), channel_id=1, source_target_pairs={{0,32},{32,64},{64,96},{96,128},{128,160},{160,192},{192,224},{224... | collective-permute-start | bytes 3464 | tf_op jit(solution)/shard_map/ppermute | solution.py:22
  11.1 20.3 %collective-permute-start.1 = (s32[96,3]{0,1:T(4,128)}, s32[96,3]{0,1:T(4,128)S(1)}, u32[]{:S(2)}, u32[]{:S(2)}) collective-permute-start(s32[96,3]{0,1:T(4,128)} %param.10), channel_id=1, source_target_pairs={{32,0},{64,32},{96,64},{128,96},{160,128},{192,160},{224,192},{256... | collective-permute-start | bytes 3464 | tf_op jit(solution)/shard_map/ppermute | solution.py:25
  13.0 18.5 %collective-permute-start.2 = (bf16[4,128,512]{2,1,0:T(8,128)(2,1)}, bf16[4,128,512]{2,1,0:T(8,128)(2,1)S(1)}, u32[]{:S(2)}, u32[]{:S(2)}) collective-permute-start(bf16[4,128,512]{2,1,0:T(8,128)(2,1)} %local_ref.1), channel_id=1, source_target_pairs={{0,1},{1,2},{2,3},{3,4},{4,5},{5,6},{6,7},{7,8},{8,9},{9,10},{10,1... | collective-permute-start | bytes 1572872 | tf_op jit(solution)/shard_map/ppermute | solution.py:14
  16.3 17.2 %collective-permute-start.4 = (bf16[4,128,512]{2,1,0:T(8,128)(2,1)}, bf16[4,128,512]{2,1,0:T(8,128)(2,1)S(1)}, u32[]{:S(2)}, u32[]{:S(2)}) collective-permute-start(bf16[4,128,512]{2,1,0:T(8,128)(2,1)} %local_ref.1), channel_id=1, source_target_pairs={{0,31},{1,0},{2,1},{3,2},{4,3},{5,4},{6,5},{7,6},{8,7},{9,8},{10,9... | collective-permute-start | bytes 1572872 | tf_op jit(solution)/shard_map/ppermute | solution.py:14
  31.5 17.9 %copy-start.2 = (bf16[4,128,512]{2,1,0:T(8,128)(2,1)}, bf16[4,128,512]{2,1,0:T(8,128)(2,1)S(1)}, u32[]{:S(2)}) copy-start(bf16[4,128,512]{2,1,0:T(8,128)(2,1)S(1)} %collective-permute-done.2.west_ref) | copy-start | bytes 1572868
  31.5 16.1 %collective-permute-start.3 = (bf16[4,128,512]{2,1,0:T(8,128)(2,1)S(1)}, bf16[4,128,512]{2,1,0:T(8,128)(2,1)S(1)}, u32[]{:S(2)}, u32[]{:S(2)}) collective-permute-start(bf16[4,128,512]{2,1,0:T(8,128)(2,1)S(1)} %collective-permute-done.2.west_ref), channel_id=1, source_target_pairs={{0,1},{1,2},{2,3},{3,4},{4,5},{5,6},{6,7},{7,8},{8,9},{9,10},{10,1... | collective-permute-start | bytes 1572872 | tf_op jit(solution)/shard_map/ppermute | solution.py:14
  33.5 15.9 %copy-start.3 = (bf16[4,128,512]{2,1,0:T(8,128)(2,1)}, bf16[4,128,512]{2,1,0:T(8,128)(2,1)S(1)}, u32[]{:S(2)}) copy-start(bf16[4,128,512]{2,1,0:T(8,128)(2,1)S(1)} %collective-permute-done.4.east_ref) | copy-start | bytes 1572868
  33.5 15.9 %collective-permute-start.5 = (bf16[4,128,512]{2,1,0:T(8,128)(2,1)S(1)}, bf16[4,128,512]{2,1,0:T(8,128)(2,1)S(1)}, u32[]{:S(2)}, u32[]{:S(2)}) collective-permute-start(bf16[4,128,512]{2,1,0:T(8,128)(2,1)S(1)} %collective-permute-done.4.east_ref), channel_id=1, source_target_pairs={{0,31},{1,0},{2,1},{3,2},{4,3},{5,4},{6,5},{7,6},{8,7},{9,8},{10,9... | collective-permute-start | bytes 1572872 | tf_op jit(solution)/shard_map/ppermute | solution.py:14
  47.6 1.8 %copy-start.4 = (bf16[4,128,512]{2,1,0:T(8,128)(2,1)}, bf16[4,128,512]{2,1,0:T(8,128)(2,1)S(1)}, u32[]{:S(2)}) copy-start(bf16[4,128,512]{2,1,0:T(8,128)(2,1)S(1)} %collective-permute-done.3.far_west_ref) | copy-start | bytes 1572868
  49.4 0.9 copy-start.5
  65.7 23.6 %copy-start = (bf16[4,128,512]{2,1,0:T(8,128)(2,1)S(1)}, bf16[4,128,512]{2,1,0:T(8,128)(2,1)}, u32[]{:S(2)}) copy-start(bf16[4,128,512]{2,1,0:T(8,128)(2,1)} %get-tuple-element.8) | copy-start | bytes 1572868
  66.8 11.8 %collective-permute-start.6 = (bf16[2,128,512]{2,1,0:T(8,128)(2,1)S(1)}, bf16[2,128,512]{2,1,0:T(8,128)(2,1)S(1)}, u32[]{:S(2)}, u32[]{:S(2)}) collective-permute-start(bf16[2,128,512]{2,1,0:T(8,128)(2,1)S(1)} %get-tuple-element.9), channel_id=1, source_target_pairs={{0,32},{32,64},{64,96},{96,128},{128,160},{160,192},{192,224},{224... | collective-permute-start | bytes 786440 | tf_op jit(solution)/shard_map/ppermute | solution.py:22
  75.4 14.1 %copy-start.1 = (f32[4,128,512]{2,1,0:T(8,128)S(1)}, f32[4,128,512]{2,1,0:T(8,128)}, u32[]{:S(2)}) copy-start(f32[4,128,512]{2,1,0:T(8,128)} %get-tuple-element.7) | copy-start | bytes 3145732
  75.4 14.1 %copy-start.6 = (f32[4]{0:T(128)S(1)}, f32[4]{0:T(128)}, u32[]{:S(2)}) copy-start(f32[4]{0:T(128)} %param.9) | copy-start | bytes 52
  75.4 14.1 %copy-start.7 = (pred[4]{0:T(512)(128)(4,1)S(1)}, pred[4]{0:T(512)(128)(4,1)}, u32[]{:S(2)}) copy-start(pred[4]{0:T(512)(128)(4,1)} %constant.24.clone.1) | copy-start | bytes 16
  75.4 13.8 %collective-permute-start.7 = (bf16[2,128,512]{2,1,0:T(8,128)(2,1)S(1)}, bf16[2,128,512]{2,1,0:T(8,128)(2,1)S(1)}, u32[]{:S(2)}, u32[]{:S(2)}) collective-permute-start(bf16[2,128,512]{2,1,0:T(8,128)(2,1)S(1)} %get-tuple-element.10), channel_id=1, source_target_pairs={{32,0},{64,32},{96,64},{128,96},{160,128},{192,160},{224,192},{256... | collective-permute-start | bytes 786440 | tf_op jit(solution)/shard_map/ppermute | solution.py:25

commit v3 on v2

--- a/solution.py
+++ b/solution.py
@@ -1,3 +1,5 @@
+import functools
+
 import jax
 import jax.numpy as jnp
 from jax import lax
@@ -79,12 +81,12 @@
     )(padded)
 
 
-def _block_kernel(counts_ref, band_ref, far_west_ref, west_ref, local_ref, east_ref, far_east_ref,
-                  weight_ref, edge_ref, inner_ref, window_ref, response_ref, mixed_ref, total_ref):
+def _block_kernel(first, counts_ref, band_ref, far_west_ref, west_ref, local_ref, east_ref,
+                  far_east_ref, weight_ref, total_ref, window_ref, response_ref, mixed_ref):
     kind = pl.program_id(0)
     kinds = pl.num_programs(0)
-    input_rows, cols, _ = local_ref.shape
-    output_rows = input_rows + 2 * RIM
+    group, cols, _ = local_ref.shape
+    reach = group + 2 * RIM
     parts = (far_west_ref, west_ref, local_ref, east_ref, far_east_ref)
 
     @pl.when(kind == 0)
@@ -93,67 +95,67 @@
             window_ref[:, index * cols : (index + 1) * cols, :] = part[...]
         total_ref[...] = jnp.zeros_like(total_ref)
 
-    for in_row in range(input_rows):
+    for in_row in range(group):
         response = jnp.dot(band_ref[in_row, 0], window_ref[in_row], preferred_element_type=jnp.float32)
         response_ref[in_row * cols : (in_row + 1) * cols, :] = response.astype(jnp.bfloat16)
     mixed_ref[...] = jnp.dot(response_ref[...], weight_ref[0], preferred_element_type=jnp.float32)
     chunk = 16
+    rows = first[1]
 
     def body(step, carry):
         start = pl.multiple_of(step * chunk, chunk)
-        pieces = [mixed_ref[pl.ds(in_row * cols + start, chunk), :] for in_row in range(input_rows)]
-        for out_row in range(output_rows):
+        pieces = [mixed_ref[pl.ds(in_row * cols + start, chunk), :] for in_row in range(group)]
+        for out_row in range(reach):
             total = total_ref[out_row, pl.ds(start, chunk), :]
-            for in_row in range(max(0, out_row - 2 * RIM), min(input_rows, out_row + 1)):
-                scale = counts_ref[(out_row * kinds + kind) * input_rows + in_row]
-                total = total + scale * pieces[in_row]
+            for in_row in range(max(0, out_row - 2 * RIM), min(group, out_row + 1)):
+                where = ((first[0] + out_row) * kinds + kind) * rows + first[0] + in_row
+                total = total + counts_ref[where] * pieces[in_row]
             total_ref[out_row, pl.ds(start, chunk), :] = total
         return carry
 
     lax.fori_loop(0, cols // chunk, body, 0)
 
-    @pl.when(kind == kinds - 1)
-    def _():
-        inner_ref[...] = total_ref[RIM : RIM + input_rows]
-        edge_ref[:RIM] = total_ref[:RIM].astype(edge_ref.dtype)
-        edge_ref[RIM:] = total_ref[RIM + input_rows :].astype(edge_ref.dtype)
-
-
-def block_partials(counts, short_taps, parts, mix_weight):
-    rows, cols, channels = parts[0].shape
-    kinds = short_taps.shape[1]
-    window = cols * len(parts)
-    band = band_matrix(short_taps, cols, window)
-    whole = lambda shape: pl.BlockSpec(shape, lambda k: (0,) * len(shape))
+
+def block_partials(counts, band, parts, mix_weight, first, group):
+    rows, cols, channels = parts[2].shape
+    kinds = band.shape[1]
+    window = band.shape[3]
+    index = first // group
+
+    def rows_of(part):
+        if part.shape[0] == group:
+            return pl.BlockSpec((group, cols, channels), lambda k: (0, 0, 0))
+        return pl.BlockSpec((group, cols, channels), lambda k: (index, 0, 0))
+
+    kernel = functools.partial(_block_kernel, (first, rows))
     return pl.pallas_call(
-        _block_kernel,
+        kernel,
         grid=(kinds,),
         in_specs=[
             pl.BlockSpec(memory_space=pltpu.SMEM),
-            pl.BlockSpec((rows, 1, cols, window), lambda k: (0, k, 0, 0)),
+            pl.BlockSpec((group, 1, cols, window), lambda k: (index, k, 0, 0)),
         ]
-        + [whole(parts[0].shape)] * len(parts)
+        + [rows_of(part) for part in parts]
         + [pl.BlockSpec((1,) + mix_weight.shape[1:], lambda k: (k, 0, 0))],
-        out_specs=[whole((2 * RIM, cols, channels)), whole((rows, cols, channels))],
-        out_shape=[
-            jax.ShapeDtypeStruct((2 * RIM, cols, channels), jnp.bfloat16),
-            jax.ShapeDtypeStruct((rows, cols, channels), jnp.float32),
-        ],
+        out_specs=pl.BlockSpec((group + 2 * RIM, cols, channels), lambda k: (0, 0, 0)),
+        out_shape=jax.ShapeDtypeStruct((group + 2 * RIM, cols, channels), jnp.float32),
         scratch_shapes=[
-            pltpu.VMEM((rows, window, channels), jnp.bfloat16),
-            pltpu.VMEM((rows * cols, channels), jnp.bfloat16),
-            pltpu.VMEM((rows * cols, mix_weight.shape[2]), jnp.float32),
-            pltpu.VMEM((rows + 2 * RIM, cols, mix_weight.shape[2]), jnp.float32),
+            pltpu.VMEM((group, window, channels), jnp.bfloat16),
+            pltpu.VMEM((group * cols, channels), jnp.bfloat16),
+            pltpu.VMEM((group * cols, mix_weight.shape[2]), jnp.float32),
         ],
         compiler_params=pltpu.CompilerParams(dimension_semantics=("arbitrary",)),
     )(counts.reshape(-1), band, *parts, mix_weight)
 
 
 def on_device(field, lon_width, lon_taps, row_scale, support, mix_weight):
-    rows = field.shape[0]
+    rows, cols, _ = field.shape
     kinds = lon_taps.shape[1]
-    far_west, west, east, far_east = longitude_halo(field)
+    group = rows // 2
+    west = shifted(field, "lon", 1)
+    east = shifted(field, "lon", -1)
     short_taps = masked_taps(lon_taps, lon_width)
+    band = band_matrix(short_taps, cols, cols * (2 * SPAN + 1))
     entries = support.shape[0]
     lists = with_halo(support, (("lat", 0),), entries)
     above = lists[:entries]
@@ -167,12 +169,28 @@
         [(support[:, 1] >= 0) & (support[:, 1] < rows), above[:, 1] >= rows, below[:, 1] < 0]
     )
     counts = coupling(out_rows, in_rows, basis, valid, rows + 2 * RIM, rows, kinds)
-    outgoing, inner = block_partials(
-        counts, short_taps, (far_west, west, field, east, far_east), mix_weight
-    )
-    incoming = with_halo(outgoing, (("lat", 0),), RIM).astype(jnp.float32)
-    inner = inner + jnp.pad(incoming[:RIM], ((0, rows - RIM), (0, 0), (0, 0)))
-    inner = inner + jnp.pad(incoming[3 * RIM :], ((rows - RIM, 0), (0, 0), (0, 0)))
+    count = lax.axis_size("lat")
+    forward = [(i, i + 1) for i in range(count - 1)]
+    backward = [(target, source) for source, target in forward]
+    far_west = shifted(west[:group], "lon", 1)
+    far_east = shifted(east[:group], "lon", -1)
+    far_west, far_east, next_west, next_east = lax.optimization_barrier(
+        (far_west, far_east, west[group:], east[group:])
+    )
+    later_west = shifted(next_west, "lon", 1)
+    later_east = shifted(next_east, "lon", -1)
+    parts = (far_west, west, field, east, far_east)
+    upper = block_partials(counts, band, parts, mix_weight, 0, group)
+    from_below = lax.ppermute(upper[:RIM].astype(jnp.bfloat16), "lat", backward)
+    from_below, later_west, later_east = lax.optimization_barrier(
+        (from_below, later_west, later_east)
+    )
+    parts = (later_west, west, field, east, later_east)
+    lower = block_partials(counts, band, parts, mix_weight, group, group)
+    from_above = lax.ppermute(lower[group + RIM :].astype(jnp.bfloat16), "lat", forward)
+    inner = upper[RIM:] + lower[: group + RIM]
+    inner = inner + jnp.pad(from_above.astype(jnp.float32), ((0, rows - RIM), (0, 0), (0, 0)))
+    inner = inner + jnp.pad(from_below.astype(jnp.float32), ((rows - RIM, 0), (0, 0), (0, 0)))
     return (inner * row_scale[:, None, None]).astype(jnp.bfloat16)
 
 

time: 91.3 us -> 110 us (1.20)
  Pallas kernels: 20.2 us -> 28.3 us
  waiting for transfers between devices: 19.3 us -> 25.6 us
  starting transfers between devices: 42.5 us -> 45.1 us
    ppermute x0 -> x2, waiting for transfers between devices: none -> 17.6 us  [the longest x1 14.3 us: on_device(): from_below = lax.ppermute(upper[:RIM].astype(jnp.bfloat16), 'lat', backward)]
    ppermute x2 -> x1, waiting for transfers between devices: 10.6 us -> 0.01 us  [with_halo(): lax.ppermute(lax.slice_in_dim(block, 0, width, axis=dim), axis, backward)]
    ppermute x4 -> x6, starting transfers between devices: 18.9 us -> 28.1 us  [shifted(): lax.ppermute(value, axis, [(i, (i + by) % length) for i in range(length)])]
    ppermute x2 -> x1, starting transfers between devices: 19.6 us -> 11.1 us  [with_halo(): lax.ppermute(lax.slice_in_dim(block, block.shape[dim] - width, None, axis...]
    pallas_call x1 -> x2, Pallas kernels: 15.5 us -> 23.6 us  [block_partials(): pl.pallas_call(kernel, grid=(kinds,), in_specs=[pl.BlockSpec(memory_space...]
    ppermute x0 -> x2, starting transfers between devices: none -> 3.97 us  [the longest x1 2.05 us: on_device(): from_below = lax.ppermute(upper[:RIM].astype(jnp.bfloat16), 'lat', backward)]
    ppermute x2 -> x1, starting transfers between devices: 3.97 us -> 1.92 us  [with_halo(): lax.ppermute(lax.slice_in_dim(block, 0, width, axis=dim), axis, backward)]
    ppermute x2 -> x1, waiting for transfers between devices: 1.2 us -> 0.01 us  [with_halo(): lax.ppermute(lax.slice_in_dim(block, block.shape[dim] - width, None, axis...]
  transfers between devices with their start and end apart: 8 -> 10, of which waited for: 4 -> 4; matrix products, arithmetic and copies ran while one was open for 5% -> 6% of each run, Pallas kernels for 5% -> 15%
where the time goes in v3:
time: 110 us; the launch traced here: 109 us
  starting transfers between devices  45.1 us (41%)
  Pallas kernels  28.3 us (26%)
  waiting for transfers between devices  25.6 us (23%)
  other arithmetic  6.37 us (6%)
  local copies, waits for them, and re-layouts  2.94 us (3%)
    ppermute x6, starting transfers between devices, shifted(): lax.ppermute(value, axis, [(i, (i + by) % length) for i in range(length)])  28.1 us
    pallas_call x2, Pallas kernels, block_partials(): pl.pallas_call(kernel, grid=(kinds,), in_specs=[pl.BlockSpec(memory_space...  23.6 us
    ppermute x1, waiting for transfers between devices, on_device(): from_below = lax.ppermute(upper[:RIM].astype(jnp.bfloat16), 'lat', backward)  14.3 us
    ppermute x1, starting transfers between devices, with_halo(): lax.ppermute(lax.slice_in_dim(block, block.shape[dim] - width, None, axis...  11.1 us
    ppermute x6, waiting for transfers between devices, shifted(): lax.ppermute(value, axis, [(i, (i + by) % length) for i in range(length)])  8.03 us
    pallas_call x1, Pallas kernels, band_matrix(): pl.pallas_call(_toeplitz_kernel, grid=(rows,), in_specs=[pl.BlockSpec((1,...  4.75 us
    ppermute x1, waiting for transfers between devices, on_device(): lax.ppermute(lower[group + RIM:].astype(jnp.bfloat16), 'lat', forward)  3.29 us
    convert_element_type x1, other arithmetic, on_device(): return (inner * row_scale[:, None, None]).astype(jnp.bfloat16)  2.37 us
  transfers between devices with their start and end apart: 10, of which 4 were waited for; matrix products, arithmetic and copies ran while one was open for 6% of the time, Pallas kernels for 15%

profile of v3, /device:TPU:7, one launch (start us, length us, event | category | flops | bytes accessed | tf_op | source)
XLA Modules:
  0.0 108.9 jit_solution(15598306325594772109)
XLA Ops:
  0.0 11.1 %collective-permute-start = (s32[96,3]{0,1:T(4,128)}, s32[96,3]{0,1:T(4,128)S(1)}, u32[]{:S(2)}, u32[]{:S(2)}) collective-permute-start(s32[96,3]{0,1:T(4,128)} %param.10), channel_id=1, source_target_pairs={{0,32},{32,64},{64,96},{96,128},{128,160},{160,192},{192,224},{224... | collective-permute-start | bytes 3464 | tf_op jit(solution)/shard_map/ppermute | solution.py:24
  11.1 1.9 %collective-permute-start.1 = (s32[96,3]{0,1:T(4,128)}, s32[96,3]{0,1:T(4,128)S(1)}, u32[]{:S(2)}, u32[]{:S(2)}) collective-permute-start(s32[96,3]{0,1:T(4,128)} %param.10), channel_id=1, source_target_pairs={{32,0},{64,32},{96,64},{128,96},{160,128},{192,160},{224,192},{256... | collective-permute-start | bytes 3464 | tf_op jit(solution)/shard_map/ppermute | solution.py:27
  13.0 7.8 %collective-permute-start.4 = (bf16[4,128,512]{2,1,0:T(8,128)(2,1)}, bf16[4,128,512]{2,1,0:T(8,128)(2,1)S(1)}, u32[]{:S(2)}, u32[]{:S(2)}) collective-permute-start(bf16[4,128,512]{2,1,0:T(8,128)(2,1)} %local_ref.3), channel_id=1, source_target_pairs={{0,31},{1,0},{2,1},{3,2},{4,3},{5,4},{6,5},{7,6},{8,7},{9,8},{10,9... | collective-permute-start | bytes 1572872 | tf_op jit(solution)/shard_map/ppermute | solution.py:16
  20.9 1.9 %collective-permute-start.2 = (bf16[4,128,512]{2,1,0:T(8,128)(2,1)}, bf16[4,128,512]{2,1,0:T(8,128)(2,1)S(1)}, u32[]{:S(2)}, u32[]{:S(2)}) collective-permute-start(bf16[4,128,512]{2,1,0:T(8,128)(2,1)} %local_ref.3), channel_id=1, source_target_pairs={{0,1},{1,2},{2,3},{3,4},{4,5},{5,6},{6,7},{7,8},{8,9},{9,10},{10,1... | collective-permute-start | bytes 1572872 | tf_op jit(solution)/shard_map/ppermute | solution.py:16
  22.8 0.7 compare_and_fusion
  23.5 0.8 add_bitcast_fusion.4
  24.3 0.7 broadcast_compare_fusion
  25.0 0.9 fusion.4
  25.9 0.7 pad_convert_fusion.taps_ref
  26.6 4.8 %shard_map.64.band_ref = bf16[4,9,128,640]{3,2,1,0:T(8,128)(2,1)} custom-call(f32[4,9,640]{2,1,0:T(8,128)} %pad_convert_fusion.taps_ref), custom_call_target="tpu_custom_call" | custom-call | tf_op jit(solution)/shard_map/pallas_call | solution.py:75
  31.4 0.0 collective-permute-done
  31.4 0.0 collective-permute-done.1
  31.4 0.1 pad_add_fusion
  31.5 0.0 collective-permute-done.4.east_ref
  31.5 0.0 copy-start.1
  31.6 7.3 %collective-permute-start.5 = (bf16[2,128,512]{2,1,0:T(8,128)(2,1)S(1)}, bf16[2,128,512]{2,1,0:T(8,128)(2,1)S(1)}, u32[]{:S(2)}, u32[]{:S(2)}) collective-permute-start(bf16[2,128,512]{2,1,0:T(8,128)(2,1)S(1)} %get-tuple-element.20), channel_id=1, source_target_pairs={{0,31},{1,0},{2,1},{3,2},{4,3},{5,4},{6,5},{7,6},{8,7},{9,8},{10,9... | collective-permute-start | bytes 786440 | tf_op jit(solution)/shard_map/ppermute | solution.py:16
  38.9 0.0 collective-permute-done.2.west_ref
  38.9 0.0 copy-start.2
  38.9 1.9 %collective-permute-start.3 = (bf16[2,128,512]{2,1,0:T(8,128)(2,1)S(1)}, bf16[2,128,512]{2,1,0:T(8,128)(2,1)S(1)}, u32[]{:S(2)}, u32[]{:S(2)}) collective-permute-start(bf16[2,128,512]{2,1,0:T(8,128)(2,1)S(1)} %get-tuple-element.22), channel_id=1, source_target_pairs={{0,1},{1,2},{2,3},{3,4},{4,5},{5,6},{6,7},{7,8},{8,9},{9,10},{10,1... | collective-permute-start | bytes 786440 | tf_op jit(solution)/shard_map/ppermute | solution.py:16
  40.8 0.1 pad_add_fusion.1
  40.9 0.3 fusion.6
  41.2 0.7 reshape_reshape.4.counts_ref
  41.9 0.2 collective-permute-done.5.far_east_ref
  42.1 0.0 copy-start.3
  42.2 7.8 %collective-permute-done.3.far_west_ref = bf16[2,128,512]{2,1,0:T(8,128)(2,1)S(1)} collective-permute-done((bf16[2,128,512]{2,1,0:T(8,128)(2,1)S(1)}, bf16[2,128,512]{2,1,0:T(8,128)(2,1)S(1)}, u32[]{:S(2)}, u32[]{:S(2)}) %collective-permute-start.3) | collective-permute-done | bytes 262176 | tf_op jit(solution)/shard_map/ppermute | solution.py:16
  50.0 0.0 copy-start.4
  50.0 1.9 %collective-permute-start.7 = (bf16[2,128,512]{2,1,0:T(8,128)(2,1)S(1)}, bf16[2,128,512]{2,1,0:T(8,128)(2,1)S(1)}, u32[]{:S(2)}, u32[]{:S(2)}) collective-permute-start(bf16[2,128,512]{2,1,0:T(8,128)(2,1)S(1)} %get-tuple-element.14), channel_id=1, source_target_pairs={{0,1},{1,2},{2,3},{3,4},{4,5},{5,6},{6,7},{7,8},{8,9},{9,10},{10,1... | collective-permute-start | bytes 786440 | tf_op jit(solution)/shard_map/ppermute | solution.py:16
  51.9 7.3 %collective-permute-start.8 = (bf16[2,128,512]{2,1,0:T(8,128)(2,1)S(1)}, bf16[2,128,512]{2,1,0:T(8,128)(2,1)}, u32[]{:S(2)}, u32[]{:S(2)}) collective-permute-start(bf16[2,128,512]{2,1,0:T(8,128)(2,1)S(1)} %get-tuple-element.15), channel_id=1, source_target_pairs={{0,31},{1,0},{2,1},{3,2},{4,3},{5,4},{6,5},{7,6},{8,7},{9,8},{10,9... | collective-permute-start | bytes 786440 | tf_op jit(solution)/shard_map/ppermute | solution.py:16
  59.2 0.0 copy-done.1
  59.2 0.0 copy-done.2
  59.2 0.0 copy-done.3
  59.2 0.0 copy-done.4
  59.2 11.7 %shard_map.65 = f32[6,128,512]{2,1,0:T(8,128)} custom-call(f32[288]{0:T(512)} %reshape_reshape.4.counts_ref, bf16[4,9,128,640]{3,2,1,0:T(8,128)(2,1)} %shard_map.64.band_ref, bf16[2,128,512]{2,1,0:T(8,128)(2,1)} %copy-done.4, bf16[4,128,512]{2,1,0:T(8,128)(2,1)} %copy-done.2, bf16[4,128,512]{2,1,0:T(8,128)(2,1)} %local_ref.3, ...), custom_call_target="tpu_custom_call" | custom-call | tf_op jit(solution)/shard_map/pallas_call | solution.py:131
  70.9 1.1 slice.108
  72.0 0.0 copy-start
  72.0 0.0 copy-start.6
  72.0 2.1 %collective-permute-start.6 = (bf16[2,128,512]{2,1,0:T(8,128)(2,1)S(1)}, bf16[2,128,512]{2,1,0:T(8,128)(2,1)S(1)}, u32[]{:S(2)}, u32[]{:S(2)}) collective-permute-start(bf16[2,128,512]{2,1,0:T(8,128)(2,1)S(1)} %slice.108), channel_id=1, source_target_pairs={{32,0},{64,32},{96,64},{128,96},{160,128},{192,160},{224,192},{256... | collective-permute-start | bytes 786440 | tf_op jit(solution)/shard_map/ppermute | solution.py:184
  74.1 0.0 collective-permute-done.7.far_west_ref
  74.1 0.0 copy-start.5
  74.1 0.0 collective-permute-done.8.far_east_ref
  74.1 14.3 %collective-permute-done.6 = bf16[2,128,512]{2,1,0:T(8,128)(2,1)S(1)} collective-permute-done((bf16[2,128,512]{2,1,0:T(8,128)(2,1)S(1)}, bf16[2,128,512]{2,1,0:T(8,128)(2,1)S(1)}, u32[]{:S(2)}, u32[]{:S(2)}) %collective-permute-start.6) | collective-permute-done | bytes 262176 | tf_op jit(solution)/shard_map/ppermute | solution.py:184
  88.4 0.0 copy-done.5
  88.4 11.8 %shard_map.66 = f32[6,128,512]{2,1,0:T(8,128)} custom-call(f32[288]{0:T(512)} %reshape_reshape.4.counts_ref, bf16[4,9,128,640]{3,2,1,0:T(8,128)(2,1)} %shard_map.64.band_ref, bf16[2,128,512]{2,1,0:T(8,128)(2,1)} %copy-done.5, bf16[4,128,512]{2,1,0:T(8,128)(2,1)} %copy-done.2, bf16[4,128,512]{2,1,0:T(8,128)(2,1)} %local_ref.3, ...), custom_call_target="tpu_custom_call" | custom-call | tf_op jit(solution)/shard_map/pallas_call | solution.py:131
  100.3 1.1 slice.107
  101.3 1.9 %collective-permute-start.9 = (bf16[2,128,512]{2,1,0:T(8,128)(2,1)S(1)}, bf16[2,128,512]{2,1,0:T(8,128)(2,1)S(1)}, u32[]{:S(2)}, u32[]{:S(2)}) collective-permute-start(bf16[2,128,512]{2,1,0:T(8,128)(2,1)S(1)} %slice.107), channel_id=1, source_target_pairs={{0,32},{32,64},{64,96},{96,128},{128,160},{160,192},{192,224},{224... | collective-permute-start | bytes 786440 | tf_op jit(solution)/shard_map/ppermute | solution.py:190
  103.3 3.3 %collective-permute-done.9 = bf16[2,128,512]{2,1,0:T(8,128)(2,1)S(1)} collective-permute-done((bf16[2,128,512]{2,1,0:T(8,128)(2,1)S(1)}, bf16[2,128,512]{2,1,0:T(8,128)(2,1)S(1)}, u32[]{:S(2)}, u32[]{:S(2)}) %collective-permute-start.9) | collective-permute-done | bytes 262176 | tf_op jit(solution)/shard_map/ppermute | solution.py:190
  106.6 0.0 copy-done
  106.6 0.0 copy-done.6
  106.6 2.4 %fusion.3 = bf16[4,128,512]{2,1,0:T(8,128)(2,1)} fusion(f32[6,128,512]{2,1,0:T(8,128)} %shard_map.66, f32[6,128,512]{2,1,0:T(8,128)S(1)} %copy-done, f32[4]{0:T(128)S(1)} %copy-done.6, bf16[2,128,512]{2,1,0:T(8,128)(2,1)S(1)} %collective-permute-done.6, bf16[2,128,512]{2,1,0:T(8,128)(2,1)S(1)} %collective-permute-done.9), kind=kLoop, calls=%fused_computation.4 | loop fusion | flops 1835008 | bytes 3145744 | tf_op jit(solution)/shard_map/convert_element_type | solution.py:194
  (7 shorter events, 0.1 us)
Async XLA Ops:
  0.0 31.4 %collective-permute-start = (s32[96,3]{0,1:T(4,128)}, s32[96,3]{0,1:T(4,128)S(1)}, u32[]{:S(2)}, u32[]{:S(2)}) collective-permute-start(s32[96,3]{0,1:T(4,128)} %param.10), channel_id=1, source_target_pairs={{0,32},{32,64},{64,96},{96,128},{128,160},{160,192},{192,224},{224... | collective-permute-start | bytes 3464 | tf_op jit(solution)/shard_map/ppermute | solution.py:24
  11.1 20.3 %collective-permute-start.1 = (s32[96,3]{0,1:T(4,128)}, s32[96,3]{0,1:T(4,128)S(1)}, u32[]{:S(2)}, u32[]{:S(2)}) collective-permute-start(s32[96,3]{0,1:T(4,128)} %param.10), channel_id=1, source_target_pairs={{32,0},{64,32},{96,64},{128,96},{160,128},{192,160},{224,192},{256... | collective-permute-start | bytes 3464 | tf_op jit(solution)/shard_map/ppermute | solution.py:27
  13.0 18.5 %collective-permute-start.4 = (bf16[4,128,512]{2,1,0:T(8,128)(2,1)}, bf16[4,128,512]{2,1,0:T(8,128)(2,1)S(1)}, u32[]{:S(2)}, u32[]{:S(2)}) collective-permute-start(bf16[4,128,512]{2,1,0:T(8,128)(2,1)} %local_ref.3), channel_id=1, source_target_pairs={{0,31},{1,0},{2,1},{3,2},{4,3},{5,4},{6,5},{7,6},{8,7},{9,8},{10,9... | collective-permute-start | bytes 1572872 | tf_op jit(solution)/shard_map/ppermute | solution.py:16
  20.9 18.0 %collective-permute-start.2 = (bf16[4,128,512]{2,1,0:T(8,128)(2,1)}, bf16[4,128,512]{2,1,0:T(8,128)(2,1)S(1)}, u32[]{:S(2)}, u32[]{:S(2)}) collective-permute-start(bf16[4,128,512]{2,1,0:T(8,128)(2,1)} %local_ref.3), channel_id=1, source_target_pairs={{0,1},{1,2},{2,3},{3,4},{4,5},{5,6},{6,7},{7,8},{8,9},{9,10},{10,1... | collective-permute-start | bytes 1572872 | tf_op jit(solution)/shard_map/ppermute | solution.py:16
  31.5 27.6 %copy-start.1 = (bf16[4,128,512]{2,1,0:T(8,128)(2,1)}, bf16[4,128,512]{2,1,0:T(8,128)(2,1)S(1)}, u32[]{:S(2)}) copy-start(bf16[4,128,512]{2,1,0:T(8,128)(2,1)S(1)} %collective-permute-done.4.east_ref) | copy-start | bytes 1572868
  31.6 10.6 %collective-permute-start.5 = (bf16[2,128,512]{2,1,0:T(8,128)(2,1)S(1)}, bf16[2,128,512]{2,1,0:T(8,128)(2,1)S(1)}, u32[]{:S(2)}, u32[]{:S(2)}) collective-permute-start(bf16[2,128,512]{2,1,0:T(8,128)(2,1)S(1)} %get-tuple-element.20), channel_id=1, source_target_pairs={{0,31},{1,0},{2,1},{3,2},{4,3},{5,4},{6,5},{7,6},{8,7},{9,8},{10,9... | collective-permute-start | bytes 786440 | tf_op jit(solution)/shard_map/ppermute | solution.py:16
  38.9 20.3 %copy-start.2 = (bf16[4,128,512]{2,1,0:T(8,128)(2,1)}, bf16[4,128,512]{2,1,0:T(8,128)(2,1)S(1)}, u32[]{:S(2)}) copy-start(bf16[4,128,512]{2,1,0:T(8,128)(2,1)S(1)} %collective-permute-done.2.west_ref) | copy-start | bytes 1572868
  38.9 11.0 %collective-permute-start.3 = (bf16[2,128,512]{2,1,0:T(8,128)(2,1)S(1)}, bf16[2,128,512]{2,1,0:T(8,128)(2,1)S(1)}, u32[]{:S(2)}, u32[]{:S(2)}) collective-permute-start(bf16[2,128,512]{2,1,0:T(8,128)(2,1)S(1)} %get-tuple-element.22), channel_id=1, source_target_pairs={{0,1},{1,2},{2,3},{3,4},{4,5},{5,6},{6,7},{7,8},{8,9},{9,10},{10,1... | collective-permute-start | bytes 786440 | tf_op jit(solution)/shard_map/ppermute | solution.py:16
  42.1 17.0 %copy-start.3 = (bf16[2,128,512]{2,1,0:T(8,128)(2,1)}, bf16[2,128,512]{2,1,0:T(8,128)(2,1)S(1)}, u32[]{:S(2)}) copy-start(bf16[2,128,512]{2,1,0:T(8,128)(2,1)S(1)} %collective-permute-done.5.far_east_ref) | copy-start | bytes 786436
  50.0 9.2 %copy-start.4 = (bf16[2,128,512]{2,1,0:T(8,128)(2,1)}, bf16[2,128,512]{2,1,0:T(8,128)(2,1)S(1)}, u32[]{:S(2)}) copy-start(bf16[2,128,512]{2,1,0:T(8,128)(2,1)S(1)} %collective-permute-done.3.far_west_ref) | copy-start | bytes 786436
  50.0 24.1 %collective-permute-start.7 = (bf16[2,128,512]{2,1,0:T(8,128)(2,1)S(1)}, bf16[2,128,512]{2,1,0:T(8,128)(2,1)S(1)}, u32[]{:S(2)}, u32[]{:S(2)}) collective-permute-start(bf16[2,128,512]{2,1,0:T(8,128)(2,1)S(1)} %get-tuple-element.14), channel_id=1, source_target_pairs={{0,1},{1,2},{2,3},{3,4},{4,5},{5,6},{6,7},{7,8},{8,9},{9,10},{10,1... | collective-permute-start | bytes 786440 | tf_op jit(solution)/shard_map/ppermute | solution.py:16
  51.9 22.2 %collective-permute-start.8 = (bf16[2,128,512]{2,1,0:T(8,128)(2,1)S(1)}, bf16[2,128,512]{2,1,0:T(8,128)(2,1)}, u32[]{:S(2)}, u32[]{:S(2)}) collective-permute-start(bf16[2,128,512]{2,1,0:T(8,128)(2,1)S(1)} %get-tuple-element.15), channel_id=1, source_target_pairs={{0,31},{1,0},{2,1},{3,2},{4,3},{5,4},{6,5},{7,6},{8,7},{9,8},{10,9... | collective-permute-start | bytes 786440 | tf_op jit(solution)/shard_map/ppermute | solution.py:16
  72.0 34.5 %copy-start = (f32[6,128,512]{2,1,0:T(8,128)S(1)}, f32[6,128,512]{2,1,0:T(8,128)}, u32[]{:S(2)}) copy-start(f32[6,128,512]{2,1,0:T(8,128)} %shard_map.65) | copy-start | bytes 4718596
  72.0 34.5 %copy-start.6 = (f32[4]{0:T(128)S(1)}, f32[4]{0:T(128)}, u32[]{:S(2)}) copy-start(f32[4]{0:T(128)} %param.9) | copy-start | bytes 52
  72.0 16.4 %collective-permute-start.6 = (bf16[2,128,512]{2,1,0:T(8,128)(2,1)S(1)}, bf16[2,128,512]{2,1,0:T(8,128)(2,1)S(1)}, u32[]{:S(2)}, u32[]{:S(2)}) collective-permute-start(bf16[2,128,512]{2,1,0:T(8,128)(2,1)S(1)} %slice.108), channel_id=1, source_target_pairs={{32,0},{64,32},{96,64},{128,96},{160,128},{192,160},{224,192},{256... | collective-permute-start | bytes 786440 | tf_op jit(solution)/shard_map/ppermute | solution.py:184
  74.1 14.3 %copy-start.5 = (bf16[2,128,512]{2,1,0:T(8,128)(2,1)}, bf16[2,128,512]{2,1,0:T(8,128)(2,1)S(1)}, u32[]{:S(2)}) copy-start(bf16[2,128,512]{2,1,0:T(8,128)(2,1)S(1)} %collective-permute-done.7.far_west_ref) | copy-start | bytes 786436
  101.3 5.2 %collective-permute-start.9 = (bf16[2,128,512]{2,1,0:T(8,128)(2,1)S(1)}, bf16[2,128,512]{2,1,0:T(8,128)(2,1)S(1)}, u32[]{:S(2)}, u32[]{:S(2)}) collective-permute-start(bf16[2,128,512]{2,1,0:T(8,128)(2,1)S(1)} %slice.107), channel_id=1, source_target_pairs={{0,32},{32,64},{64,96},{96,128},{128,160},{160,192},{192,224},{224... | collective-permute-start | bytes 786440 | tf_op jit(solution)/shard_map/ppermute | solution.py:190

commit v4 on v2

--- a/solution.py
+++ b/solution.py
@@ -35,12 +35,23 @@
     return jnp.where(keep, lon_taps, 0.0).astype(jnp.bfloat16)
 
 
+def crossed(value, by):
+    bands = lax.axis_size("lat")
+    length = lax.axis_size("lon")
+    pairs = []
+    for band in range(bands):
+        step = by if band % 2 == 0 else -by
+        for cell in range(length):
+            pairs.append((band * length + cell, band * length + (cell + step) % length))
+    return lax.ppermute(value, ("lat", "lon"), pairs)
+
+
 def longitude_halo(source):
-    west = shifted(source, "lon", 1)
-    east = shifted(source, "lon", -1)
-    far_west = shifted(west, "lon", 1)
-    far_east = shifted(east, "lon", -1)
-    return far_west, west, east, far_east
+    near_one = crossed(source, 1)
+    near_two = crossed(source, -1)
+    far_one = crossed(near_one, 1)
+    far_two = crossed(near_two, -1)
+    return far_one, near_one, near_two, far_two
 
 
 def coupling(out_rows, in_rows, basis, valid, output_rows, input_rows, kinds):
@@ -79,7 +90,7 @@
     )(padded)
 
 
-def _block_kernel(counts_ref, band_ref, far_west_ref, west_ref, local_ref, east_ref, far_east_ref,
+def _block_kernel(parity_ref, counts_ref, band_ref, far_west_ref, west_ref, local_ref, east_ref, far_east_ref,
                   weight_ref, edge_ref, inner_ref, window_ref, response_ref, mixed_ref, total_ref):
     kind = pl.program_id(0)
     kinds = pl.num_programs(0)
@@ -87,10 +98,18 @@
     output_rows = input_rows + 2 * RIM
     parts = (far_west_ref, west_ref, local_ref, east_ref, far_east_ref)
 
-    @pl.when(kind == 0)
+    @pl.when((kind == 0) & (parity_ref[0] == 0))
     def _():
         for index, part in enumerate(parts):
             window_ref[:, index * cols : (index + 1) * cols, :] = part[...]
+
+    @pl.when((kind == 0) & (parity_ref[0] != 0))
+    def _():
+        for index, part in enumerate(parts[::-1]):
+            window_ref[:, index * cols : (index + 1) * cols, :] = part[...]
+
+    @pl.when(kind == 0)
+    def _():
         total_ref[...] = jnp.zeros_like(total_ref)
 
     for in_row in range(input_rows):
@@ -119,7 +138,7 @@
         edge_ref[RIM:] = total_ref[RIM + input_rows :].astype(edge_ref.dtype)
 
 
-def block_partials(counts, short_taps, parts, mix_weight):
+def block_partials(parity, counts, short_taps, parts, mix_weight):
     rows, cols, channels = parts[0].shape
     kinds = short_taps.shape[1]
     window = cols * len(parts)
@@ -129,6 +148,7 @@
         _block_kernel,
         grid=(kinds,),
         in_specs=[
+            pl.BlockSpec(memory_space=pltpu.SMEM),
             pl.BlockSpec(memory_space=pltpu.SMEM),
             pl.BlockSpec((rows, 1, cols, window), lambda k: (0, k, 0, 0)),
         ]
@@ -146,7 +166,7 @@
             pltpu.VMEM((rows + 2 * RIM, cols, mix_weight.shape[2]), jnp.float32),
         ],
         compiler_params=pltpu.CompilerParams(dimension_semantics=("arbitrary",)),
-    )(counts.reshape(-1), band, *parts, mix_weight)
+    )(parity, counts.reshape(-1), band, *parts, mix_weight)
 
 
 def on_device(field, lon_width, lon_taps, row_scale, support, mix_weight):
@@ -167,8 +187,9 @@
         [(support[:, 1] >= 0) & (support[:, 1] < rows), above[:, 1] >= rows, below[:, 1] < 0]
     )
     counts = coupling(out_rows, in_rows, basis, valid, rows + 2 * RIM, rows, kinds)
+    parity = (lax.axis_index("lat") % 2).astype(jnp.int32).reshape(1)
     outgoing, inner = block_partials(
-        counts, short_taps, (far_west, west, field, east, far_east), mix_weight
+        parity, counts, short_taps, (far_west, west, field, east, far_east), mix_weight
     )
     incoming = with_halo(outgoing, (("lat", 0),), RIM).astype(jnp.float32)
     inner = inner + jnp.pad(incoming[:RIM], ((0, rows - RIM), (0, 0), (0, 0)))

time: 91.3 us -> 96.9 us (1.061)
  waiting for transfers between devices: 19.3 us -> 22.6 us
  starting transfers between devices: 42.5 us -> 44.8 us
    ppermute x4, waiting for transfers between devices: 7.56 us -> 10.8 us  [crossed(): return lax.ppermute(value, ('lat', 'lon'), pairs)]
    ppermute x2, starting transfers between devices: 19.6 us -> 21.8 us  [with_halo(): lax.ppermute(lax.slice_in_dim(block, block.shape[dim] - width, None, axis...]
where the time goes in v4:
time: 96.9 us; the launch traced here: 96.3 us
  starting transfers between devices  44.8 us (46%)
  waiting for transfers between devices  22.6 us (23%)
  Pallas kernels  20.4 us (21%)
  other arithmetic  5.37 us (6%)
  local copies, waits for them, and re-layouts  2.68 us (3%)
    ppermute x2, starting transfers between devices, with_halo(): lax.ppermute(lax.slice_in_dim(block, block.shape[dim] - width, None, axis...  21.8 us
    ppermute x4, starting transfers between devices, crossed(): return lax.ppermute(value, ('lat', 'lon'), pairs)  19 us
    pallas_call x1, Pallas kernels, block_partials(): pl.pallas_call(_block_kernel, grid=(kinds,), in_specs=[pl.BlockSpec(memor...  15.6 us
    ppermute x4, waiting for transfers between devices, crossed(): return lax.ppermute(value, ('lat', 'lon'), pairs)  10.8 us
    ppermute x2, waiting for transfers between devices, with_halo(): lax.ppermute(lax.slice_in_dim(block, 0, width, axis=dim), axis, backward)  10.6 us
    pallas_call x1, Pallas kernels, band_matrix(): pl.pallas_call(_toeplitz_kernel, grid=(rows,), in_specs=[pl.BlockSpec((1,...  4.75 us
    ppermute x2, starting transfers between devices, with_halo(): lax.ppermute(lax.slice_in_dim(block, 0, width, axis=dim), axis, backward)  3.97 us
  transfers between devices with their start and end apart: 8, of which 4 were waited for; matrix products, arithmetic and copies ran while one was open for 5% of the time, Pallas kernels for 5%

profile of v4, /device:TPU:7, one launch (start us, length us, event | category | flops | bytes accessed | tf_op | source)
XLA Modules:
  0.0 96.3 jit_solution(7250081932835413800)
XLA Ops:
  0.0 11.1 %collective-permute-start = (s32[96,3]{0,1:T(4,128)}, s32[96,3]{0,1:T(4,128)S(1)}, u32[]{:S(2)}, u32[]{:S(2)}) collective-permute-start(s32[96,3]{0,1:T(4,128)} %param.10), channel_id=1, source_target_pairs={{0,32},{32,64},{64,96},{96,128},{128,160},{160,192},{192,224},{224... | collective-permute-start | bytes 3464 | tf_op jit(solution)/shard_map/ppermute | solution.py:22
  11.1 1.9 %collective-permute-start.1 = (s32[96,3]{0,1:T(4,128)}, s32[96,3]{0,1:T(4,128)S(1)}, u32[]{:S(2)}, u32[]{:S(2)}) collective-permute-start(s32[96,3]{0,1:T(4,128)} %param.10), channel_id=1, source_target_pairs={{32,0},{64,32},{96,64},{128,96},{160,128},{192,160},{224,192},{256... | collective-permute-start | bytes 3464 | tf_op jit(solution)/shard_map/ppermute | solution.py:25
  13.0 7.8 %collective-permute-start.2 = (bf16[4,128,512]{2,1,0:T(8,128)(2,1)}, bf16[4,128,512]{2,1,0:T(8,128)(2,1)S(1)}, u32[]{:S(2)}, u32[]{:S(2)}) collective-permute-start(bf16[4,128,512]{2,1,0:T(8,128)(2,1)} %local_ref.1), channel_id=1, source_target_pairs={{0,1},{1,2},{2,3},{3,4},{4,5},{5,6},{6,7},{7,8},{8,9},{9,10},{10,1... | collective-permute-start | bytes 1572872 | tf_op jit(solution)/shard_map/ppermute | solution.py:46
  20.9 1.9 %collective-permute-start.4 = (bf16[4,128,512]{2,1,0:T(8,128)(2,1)}, bf16[4,128,512]{2,1,0:T(8,128)(2,1)S(1)}, u32[]{:S(2)}, u32[]{:S(2)}) collective-permute-start(bf16[4,128,512]{2,1,0:T(8,128)(2,1)} %local_ref.1), channel_id=1, source_target_pairs={{0,31},{1,0},{2,1},{3,2},{4,3},{5,4},{6,5},{7,6},{8,7},{9,8},{10,9... | collective-permute-start | bytes 1572872 | tf_op jit(solution)/shard_map/ppermute | solution.py:46
  22.8 0.7 compare_and_fusion
  23.5 0.8 add_bitcast_fusion.4
  24.3 0.7 broadcast_compare_fusion
  25.0 0.9 fusion.4
  25.9 0.7 pad_convert_fusion.taps_ref
  26.6 4.8 %shard_map.64.band_ref = bf16[4,9,128,640]{3,2,1,0:T(8,128)(2,1)} custom-call(f32[4,9,640]{2,1,0:T(8,128)} %pad_convert_fusion.taps_ref), custom_call_target="tpu_custom_call" | custom-call | tf_op jit(solution)/shard_map/pallas_call | solution.py:84
  31.4 0.0 collective-permute-done
  31.4 0.0 collective-permute-done.1
  31.4 0.1 pad_add_fusion.1
  31.5 0.0 collective-permute-done.2.west_ref
  31.5 0.0 copy-start.2
  31.5 7.3 %collective-permute-start.3 = (bf16[4,128,512]{2,1,0:T(8,128)(2,1)S(1)}, bf16[4,128,512]{2,1,0:T(8,128)(2,1)S(1)}, u32[]{:S(2)}, u32[]{:S(2)}) collective-permute-start(bf16[4,128,512]{2,1,0:T(8,128)(2,1)S(1)} %collective-permute-done.2.west_ref), channel_id=1, source_target_pairs={{0,1},{1,2},{2,3},{3,4},{4,5},{5,6},{6,7},{7,8},{8,9},{9,10},{10,1... | collective-permute-start | bytes 1572872 | tf_op jit(solution)/shard_map/ppermute | solution.py:46
  38.8 0.0 collective-permute-done.4.east_ref
  38.8 0.0 copy-start.3
  38.8 1.9 %collective-permute-start.5 = (bf16[4,128,512]{2,1,0:T(8,128)(2,1)S(1)}, bf16[4,128,512]{2,1,0:T(8,128)(2,1)S(1)}, u32[]{:S(2)}, u32[]{:S(2)}) collective-permute-start(bf16[4,128,512]{2,1,0:T(8,128)(2,1)S(1)} %collective-permute-done.4.east_ref), channel_id=1, source_target_pairs={{0,31},{1,0},{2,1},{3,2},{4,3},{5,4},{6,5},{7,6},{8,7},{9,8},{10,9... | collective-permute-start | bytes 1572872 | tf_op jit(solution)/shard_map/ppermute | solution.py:46
  40.8 0.1 pad_add_fusion
  40.9 0.3 fusion.6
  41.2 0.7 reshape_reshape.3.counts_ref
  41.9 8.1 %collective-permute-done.3.far_west_ref = bf16[4,128,512]{2,1,0:T(8,128)(2,1)S(1)} collective-permute-done((bf16[4,128,512]{2,1,0:T(8,128)(2,1)S(1)}, bf16[4,128,512]{2,1,0:T(8,128)(2,1)S(1)}, u32[]{:S(2)}, u32[]{:S(2)}) %collective-permute-start.3) | collective-permute-done | bytes 524320 | tf_op jit(solution)/shard_map/ppermute | solution.py:46
  49.9 0.0 copy-start.4
  49.9 2.8 %collective-permute-done.5.far_east_ref = bf16[4,128,512]{2,1,0:T(8,128)(2,1)S(1)} collective-permute-done((bf16[4,128,512]{2,1,0:T(8,128)(2,1)S(1)}, bf16[4,128,512]{2,1,0:T(8,128)(2,1)S(1)}, u32[]{:S(2)}, u32[]{:S(2)}) %collective-permute-start.5) | collective-permute-done | bytes 524320 | tf_op jit(solution)/shard_map/ppermute | solution.py:46
  52.7 0.0 copy-start.5
  52.7 0.0 copy-done.2
  52.7 0.0 copy-done.3
  52.7 0.0 copy-done.4
  52.7 0.8 copy-done.5
  53.5 15.6 %shard_map.65 = (bf16[4,128,512]{2,1,0:T(8,128)(2,1)}, f32[4,128,512]{2,1,0:T(8,128)}) custom-call(s32[1]{0:T(128)} %bitcast.parity_ref, f32[288]{0:T(512)} %reshape_reshape.3.counts_ref, bf16[4,9,128,640]{3,2,1,0:T(8,128)(2,1)} %shard_map.64.band_ref, bf16[4,128,512]{2,1,0:T(8,128)(2,1)} %copy-done.4, bf16[4,128,512]{2,1,0:T(8,128)(2,1)} %copy-done.2, ...), custom_call_target="tpu_custom_call" | custom-call | tf_op jit(solution)/shard_map/pallas_call | solution.py:147
  69.1 0.0 copy-start
  69.1 1.1 %fusion.12 = (bf16[2,128,512]{2,1,0:T(8,128)(2,1)S(1)}, bf16[2,128,512]{2,1,0:T(8,128)(2,1)S(1)}) fusion(bf16[4,128,512]{2,1,0:T(8,128)(2,1)} %get-tuple-element.8), kind=kLoop, calls=%fused_computation.35 | loop fusion | bytes 1048576 | tf_op jit(solution)/shard_map/slice | solution.py:23
  70.3 10.7 %collective-permute-start.6 = (bf16[2,128,512]{2,1,0:T(8,128)(2,1)S(1)}, bf16[2,128,512]{2,1,0:T(8,128)(2,1)S(1)}, u32[]{:S(2)}, u32[]{:S(2)}) collective-permute-start(bf16[2,128,512]{2,1,0:T(8,128)(2,1)S(1)} %get-tuple-element.9), channel_id=1, source_target_pairs={{0,32},{32,64},{64,96},{96,128},{128,160},{160,192},{192,224},{224... | collective-permute-start | bytes 786440 | tf_op jit(solution)/shard_map/ppermute | solution.py:22
  81.0 0.0 copy-start.1
  81.0 0.0 copy-start.6
  81.0 0.0 copy-start.7
  81.0 2.1 %collective-permute-start.7 = (bf16[2,128,512]{2,1,0:T(8,128)(2,1)S(1)}, bf16[2,128,512]{2,1,0:T(8,128)(2,1)S(1)}, u32[]{:S(2)}, u32[]{:S(2)}) collective-permute-start(bf16[2,128,512]{2,1,0:T(8,128)(2,1)S(1)} %get-tuple-element.10), channel_id=1, source_target_pairs={{32,0},{64,32},{96,64},{128,96},{160,128},{192,160},{224,192},{256... | collective-permute-start | bytes 786440 | tf_op jit(solution)/shard_map/ppermute | solution.py:25
  83.1 1.2 %collective-permute-done.6 = bf16[2,128,512]{2,1,0:T(8,128)(2,1)S(1)} collective-permute-done((bf16[2,128,512]{2,1,0:T(8,128)(2,1)S(1)}, bf16[2,128,512]{2,1,0:T(8,128)(2,1)S(1)}, u32[]{:S(2)}, u32[]{:S(2)}) %collective-permute-start.6) | collective-permute-done | bytes 262176 | tf_op jit(solution)/shard_map/ppermute | solution.py:22
  84.3 10.6 %collective-permute-done.7 = bf16[2,128,512]{2,1,0:T(8,128)(2,1)S(1)} collective-permute-done((bf16[2,128,512]{2,1,0:T(8,128)(2,1)S(1)}, bf16[2,128,512]{2,1,0:T(8,128)(2,1)S(1)}, u32[]{:S(2)}, u32[]{:S(2)}) %collective-permute-start.7) | collective-permute-done | bytes 262176 | tf_op jit(solution)/shard_map/ppermute | solution.py:25
  94.9 0.0 copy-done
  94.9 0.2 maximum_convert_fusion
  95.1 0.0 copy-done.1
  95.1 0.0 copy-done.6
  95.1 0.0 copy-done.7
  95.1 1.2 %fusion.3 = bf16[4,128,512]{2,1,0:T(8,128)(2,1)} fusion(f32[4,128,512]{2,1,0:T(8,128)S(1)} %copy-done.1, f32[8,128,512]{2,1,0:T(8,128)S(1)} %maximum_convert_fusion, f32[2,128,512]{2,1,0:T(8,128)S(1)} %maximum_convert_fusion.1, f32[4]{0:T(128)S(1)} %copy-done.6, pred[4]{0:T(512)(128)(4,1)S(1)} %copy-done.7), kind=kLoop, calls=%fused_computation.4 | loop fusion | flops 1310720 | bytes 3145748 | tf_op jit(solution)/shard_map/convert_element_type | solution.py:197
  (6 shorter events, 0.1 us)
Async XLA Ops:
  0.0 31.4 %collective-permute-start = (s32[96,3]{0,1:T(4,128)}, s32[96,3]{0,1:T(4,128)S(1)}, u32[]{:S(2)}, u32[]{:S(2)}) collective-permute-start(s32[96,3]{0,1:T(4,128)} %param.10), channel_id=1, source_target_pairs={{0,32},{32,64},{64,96},{96,128},{128,160},{160,192},{192,224},{224... | collective-permute-start | bytes 3464 | tf_op jit(solution)/shard_map/ppermute | solution.py:22
  11.1 20.3 %collective-permute-start.1 = (s32[96,3]{0,1:T(4,128)}, s32[96,3]{0,1:T(4,128)S(1)}, u32[]{:S(2)}, u32[]{:S(2)}) collective-permute-start(s32[96,3]{0,1:T(4,128)} %param.10), channel_id=1, source_target_pairs={{32,0},{64,32},{96,64},{128,96},{160,128},{192,160},{224,192},{256... | collective-permute-start | bytes 3464 | tf_op jit(solution)/shard_map/ppermute | solution.py:25
  13.0 18.5 %collective-permute-start.2 = (bf16[4,128,512]{2,1,0:T(8,128)(2,1)}, bf16[4,128,512]{2,1,0:T(8,128)(2,1)S(1)}, u32[]{:S(2)}, u32[]{:S(2)}) collective-permute-start(bf16[4,128,512]{2,1,0:T(8,128)(2,1)} %local_ref.1), channel_id=1, source_target_pairs={{0,1},{1,2},{2,3},{3,4},{4,5},{5,6},{6,7},{7,8},{8,9},{9,10},{10,1... | collective-permute-start | bytes 1572872 | tf_op jit(solution)/shard_map/ppermute | solution.py:46
  20.9 17.9 %collective-permute-start.4 = (bf16[4,128,512]{2,1,0:T(8,128)(2,1)}, bf16[4,128,512]{2,1,0:T(8,128)(2,1)S(1)}, u32[]{:S(2)}, u32[]{:S(2)}) collective-permute-start(bf16[4,128,512]{2,1,0:T(8,128)(2,1)} %local_ref.1), channel_id=1, source_target_pairs={{0,31},{1,0},{2,1},{3,2},{4,3},{5,4},{6,5},{7,6},{8,7},{9,8},{10,9... | collective-permute-start | bytes 1572872 | tf_op jit(solution)/shard_map/ppermute | solution.py:46
  31.5 21.2 %copy-start.2 = (bf16[4,128,512]{2,1,0:T(8,128)(2,1)}, bf16[4,128,512]{2,1,0:T(8,128)(2,1)S(1)}, u32[]{:S(2)}) copy-start(bf16[4,128,512]{2,1,0:T(8,128)(2,1)S(1)} %collective-permute-done.2.west_ref) | copy-start | bytes 1572868
  31.5 18.4 %collective-permute-start.3 = (bf16[4,128,512]{2,1,0:T(8,128)(2,1)S(1)}, bf16[4,128,512]{2,1,0:T(8,128)(2,1)S(1)}, u32[]{:S(2)}, u32[]{:S(2)}) collective-permute-start(bf16[4,128,512]{2,1,0:T(8,128)(2,1)S(1)} %collective-permute-done.2.west_ref), channel_id=1, source_target_pairs={{0,1},{1,2},{2,3},{3,4},{4,5},{5,6},{6,7},{7,8},{8,9},{9,10},{10,1... | collective-permute-start | bytes 1572872 | tf_op jit(solution)/shard_map/ppermute | solution.py:46
  38.8 13.8 %copy-start.3 = (bf16[4,128,512]{2,1,0:T(8,128)(2,1)}, bf16[4,128,512]{2,1,0:T(8,128)(2,1)S(1)}, u32[]{:S(2)}) copy-start(bf16[4,128,512]{2,1,0:T(8,128)(2,1)S(1)} %collective-permute-done.4.east_ref) | copy-start | bytes 1572868
  38.8 13.8 %collective-permute-start.5 = (bf16[4,128,512]{2,1,0:T(8,128)(2,1)S(1)}, bf16[4,128,512]{2,1,0:T(8,128)(2,1)S(1)}, u32[]{:S(2)}, u32[]{:S(2)}) collective-permute-start(bf16[4,128,512]{2,1,0:T(8,128)(2,1)S(1)} %collective-permute-done.4.east_ref), channel_id=1, source_target_pairs={{0,31},{1,0},{2,1},{3,2},{4,3},{5,4},{6,5},{7,6},{8,7},{9,8},{10,9... | collective-permute-start | bytes 1572872 | tf_op jit(solution)/shard_map/ppermute | solution.py:46
  49.9 2.8 %copy-start.4 = (bf16[4,128,512]{2,1,0:T(8,128)(2,1)}, bf16[4,128,512]{2,1,0:T(8,128)(2,1)S(1)}, u32[]{:S(2)}) copy-start(bf16[4,128,512]{2,1,0:T(8,128)(2,1)S(1)} %collective-permute-done.3.far_west_ref) | copy-start | bytes 1572868
  52.7 0.9 copy-start.5
  69.1 25.8 %copy-start = (bf16[4,128,512]{2,1,0:T(8,128)(2,1)S(1)}, bf16[4,128,512]{2,1,0:T(8,128)(2,1)}, u32[]{:S(2)}) copy-start(bf16[4,128,512]{2,1,0:T(8,128)(2,1)} %get-tuple-element.8) | copy-start | bytes 1572868
  70.3 14.0 %collective-permute-start.6 = (bf16[2,128,512]{2,1,0:T(8,128)(2,1)S(1)}, bf16[2,128,512]{2,1,0:T(8,128)(2,1)S(1)}, u32[]{:S(2)}, u32[]{:S(2)}) collective-permute-start(bf16[2,128,512]{2,1,0:T(8,128)(2,1)S(1)} %get-tuple-element.9), channel_id=1, source_target_pairs={{0,32},{32,64},{64,96},{96,128},{128,160},{160,192},{192,224},{224... | collective-permute-start | bytes 786440 | tf_op jit(solution)/shard_map/ppermute | solution.py:22
  81.0 14.1 %copy-start.1 = (f32[4,128,512]{2,1,0:T(8,128)S(1)}, f32[4,128,512]{2,1,0:T(8,128)}, u32[]{:S(2)}) copy-start(f32[4,128,512]{2,1,0:T(8,128)} %get-tuple-element.7) | copy-start | bytes 3145732
  81.0 14.1 %copy-start.6 = (f32[4]{0:T(128)S(1)}, f32[4]{0:T(128)}, u32[]{:S(2)}) copy-start(f32[4]{0:T(128)} %param.9) | copy-start | bytes 52
  81.0 14.1 %copy-start.7 = (pred[4]{0:T(512)(128)(4,1)S(1)}, pred[4]{0:T(512)(128)(4,1)}, u32[]{:S(2)}) copy-start(pred[4]{0:T(512)(128)(4,1)} %constant.41.clone.1) | copy-start | bytes 16
  81.0 13.8 %collective-permute-start.7 = (bf16[2,128,512]{2,1,0:T(8,128)(2,1)S(1)}, bf16[2,128,512]{2,1,0:T(8,128)(2,1)S(1)}, u32[]{:S(2)}, u32[]{:S(2)}) collective-permute-start(bf16[2,128,512]{2,1,0:T(8,128)(2,1)S(1)} %get-tuple-element.10), channel_id=1, source_target_pairs={{32,0},{64,32},{96,64},{128,96},{160,128},{192,160},{224,192},{256... | collective-permute-start | bytes 786440 | tf_op jit(solution)/shard_map/ppermute | solution.py:25

commit v5 on v2

--- a/solution.py
+++ b/solution.py
@@ -35,12 +35,13 @@
     return jnp.where(keep, lon_taps, 0.0).astype(jnp.bfloat16)
 
 
-def longitude_halo(source):
+def longitude_halo(source, support):
     west = shifted(source, "lon", 1)
     east = shifted(source, "lon", -1)
+    west, east, support = lax.optimization_barrier((west, east, support))
     far_west = shifted(west, "lon", 1)
     far_east = shifted(east, "lon", -1)
-    return far_west, west, east, far_east
+    return far_west, west, east, far_east, support
 
 
 def coupling(out_rows, in_rows, basis, valid, output_rows, input_rows, kinds):
@@ -152,7 +153,7 @@
 def on_device(field, lon_width, lon_taps, row_scale, support, mix_weight):
     rows = field.shape[0]
     kinds = lon_taps.shape[1]
-    far_west, west, east, far_east = longitude_halo(field)
+    far_west, west, east, far_east, support = longitude_halo(field, support)
     short_taps = masked_taps(lon_taps, lon_width)
     entries = support.shape[0]
     lists = with_halo(support, (("lat", 0),), entries)

time: 91.3 us -> 92.6 us (1.014)
  waiting for transfers between devices: 19.3 us -> 20.8 us
  other arithmetic: 5.37 us -> 3.9 us
  starting transfers between devices: 42.5 us -> 43.9 us
    ppermute x2, starting transfers between devices: 19.6 us -> 16.1 us  [with_halo(): lax.ppermute(lax.slice_in_dim(block, block.shape[dim] - width, None, axis...]
    ppermute x4, starting transfers between devices: 18.9 us -> 22.3 us  [shifted(): lax.ppermute(value, axis, [(i, (i + by) % length) for i in range(length)])]
    ppermute x2, starting transfers between devices: 3.97 us -> 5.51 us  [with_halo(): lax.ppermute(lax.slice_in_dim(block, 0, width, axis=dim), axis, backward)]
    ppermute x4, waiting for transfers between devices: 7.56 us -> 9.03 us  [shifted(): lax.ppermute(value, axis, [(i, (i + by) % length) for i in range(length)])]
  transfers between devices with their start and end apart: 8 -> 8, of which waited for: 4 -> 6; matrix products, arithmetic and copies ran while one was open for 5% -> 4% of each run, Pallas kernels for 5% -> 5%
where the time goes in v5:
time: 92.6 us; the launch traced here: 92.1 us
  starting transfers between devices  43.9 us (47%)
  waiting for transfers between devices  20.8 us (22%)
  Pallas kernels  20.3 us (22%)
  other arithmetic  3.9 us (4%)
  local copies, waits for them, and re-layouts  2.7 us (3%)
    ppermute x4, starting transfers between devices, shifted(): lax.ppermute(value, axis, [(i, (i + by) % length) for i in range(length)])  22.3 us
    ppermute x2, starting transfers between devices, with_halo(): lax.ppermute(lax.slice_in_dim(block, block.shape[dim] - width, None, axis...  16.1 us
    pallas_call x1, Pallas kernels, block_partials(): pl.pallas_call(_block_kernel, grid=(kinds,), in_specs=[pl.BlockSpec(memor...  15.5 us
    ppermute x2, waiting for transfers between devices, with_halo(): lax.ppermute(lax.slice_in_dim(block, 0, width, axis=dim), axis, backward)  10.6 us
    ppermute x4, waiting for transfers between devices, shifted(): lax.ppermute(value, axis, [(i, (i + by) % length) for i in range(length)])  9.03 us
    ppermute x2, starting transfers between devices, with_halo(): lax.ppermute(lax.slice_in_dim(block, 0, width, axis=dim), axis, backward)  5.51 us
    pallas_call x1, Pallas kernels, band_matrix(): pl.pallas_call(_toeplitz_kernel, grid=(rows,), in_specs=[pl.BlockSpec((1,...  4.76 us
  transfers between devices with their start and end apart: 8, of which 6 were waited for; matrix products, arithmetic and copies ran while one was open for 4% of the time, Pallas kernels for 5%

profile of v5, /device:TPU:7, one launch (start us, length us, event | category | flops | bytes accessed | tf_op | source)
XLA Modules:
  0.0 92.1 jit_solution(3056987351525948278)
XLA Ops:
  0.0 3.2 %collective-permute-start = (bf16[4,128,512]{2,1,0:T(8,128)(2,1)}, bf16[4,128,512]{2,1,0:T(8,128)(2,1)S(1)}, u32[]{:S(2)}, u32[]{:S(2)}) collective-permute-start(bf16[4,128,512]{2,1,0:T(8,128)(2,1)} %local_ref.1), channel_id=1, source_target_pairs={{0,1},{1,2},{2,3},{3,4},{4,5},{5,6},{6,7},{7,8},{8,9},{9,10},{10,1... | collective-permute-start | bytes 1572872 | tf_op jit(solution)/shard_map/ppermute | solution.py:14
  3.2 9.2 %collective-permute-start.1 = (bf16[4,128,512]{2,1,0:T(8,128)(2,1)}, bf16[4,128,512]{2,1,0:T(8,128)(2,1)S(1)}, u32[]{:S(2)}, u32[]{:S(2)}) collective-permute-start(bf16[4,128,512]{2,1,0:T(8,128)(2,1)} %local_ref.1), channel_id=1, source_target_pairs={{0,31},{1,0},{2,1},{3,2},{4,3},{5,4},{6,5},{7,6},{8,7},{9,8},{10,9... | collective-permute-start | bytes 1572872 | tf_op jit(solution)/shard_map/ppermute | solution.py:14
  12.5 0.7 broadcast_compare_fusion
  13.2 0.9 fusion.4
  14.1 0.7 pad_convert_fusion.taps_ref
  14.8 0.0 copy-start.6
  14.8 4.8 %shard_map.64.band_ref = bf16[4,9,128,640]{3,2,1,0:T(8,128)(2,1)} custom-call(f32[4,9,640]{2,1,0:T(8,128)} %pad_convert_fusion.taps_ref), custom_call_target="tpu_custom_call" | custom-call | tf_op jit(solution)/shard_map/pallas_call | solution.py:74
  19.6 2.8 %collective-permute-done.west_ref = bf16[4,128,512]{2,1,0:T(8,128)(2,1)S(1)} collective-permute-done((bf16[4,128,512]{2,1,0:T(8,128)(2,1)}, bf16[4,128,512]{2,1,0:T(8,128)(2,1)S(1)}, u32[]{:S(2)}, u32[]{:S(2)}) %collective-permute-start) | collective-permute-done | bytes 524320 | tf_op jit(solution)/shard_map/ppermute | solution.py:14
  22.4 0.0 copy-start.2
  22.4 1.0 %collective-permute-done.1.east_ref = bf16[4,128,512]{2,1,0:T(8,128)(2,1)S(1)} collective-permute-done((bf16[4,128,512]{2,1,0:T(8,128)(2,1)}, bf16[4,128,512]{2,1,0:T(8,128)(2,1)S(1)}, u32[]{:S(2)}, u32[]{:S(2)}) %collective-permute-start.1) | collective-permute-done | bytes 524320 | tf_op jit(solution)/shard_map/ppermute | solution.py:14
  23.3 0.0 copy-done.6
  23.3 0.0 copy-start.3
  23.3 3.5 %collective-permute-start.3 = (s32[96,3]{0,1:T(4,128)S(1)}, s32[96,3]{0,1:T(4,128)S(1)}, u32[]{:S(2)}, u32[]{:S(2)}) collective-permute-start(s32[96,3]{0,1:T(4,128)S(1)} %copy-done.6), channel_id=1, source_target_pairs={{32,0},{64,32},{96,64},{128,96},{160,128},{192,160},{224,192},{256... | collective-permute-start | bytes 3464 | tf_op jit(solution)/shard_map/ppermute | solution.py:25
  26.8 8.1 %collective-permute-start.2 = (s32[96,3]{0,1:T(4,128)S(1)}, s32[96,3]{0,1:T(4,128)S(1)}, u32[]{:S(2)}, u32[]{:S(2)}) collective-permute-start(s32[96,3]{0,1:T(4,128)S(1)} %copy-done.6), channel_id=1, source_target_pairs={{0,32},{32,64},{64,96},{96,128},{128,160},{160,192},{192,224},{224... | collective-permute-start | bytes 3464 | tf_op jit(solution)/shard_map/ppermute | solution.py:22
  35.0 1.9 %collective-permute-start.4 = (bf16[4,128,512]{2,1,0:T(8,128)(2,1)S(1)}, bf16[4,128,512]{2,1,0:T(8,128)(2,1)S(1)}, u32[]{:S(2)}, u32[]{:S(2)}) collective-permute-start(bf16[4,128,512]{2,1,0:T(8,128)(2,1)S(1)} %collective-permute-done.west_ref), channel_id=1, source_target_pairs={{0,1},{1,2},{2,3},{3,4},{4,5},{5,6},{6,7},{7,8},{8,9},{9,10},{10,1... | collective-permute-start | bytes 1572872 | tf_op jit(solution)/shard_map/ppermute | solution.py:14
  36.9 7.9 %collective-permute-start.5 = (bf16[4,128,512]{2,1,0:T(8,128)(2,1)S(1)}, bf16[4,128,512]{2,1,0:T(8,128)(2,1)S(1)}, u32[]{:S(2)}, u32[]{:S(2)}) collective-permute-start(bf16[4,128,512]{2,1,0:T(8,128)(2,1)S(1)} %collective-permute-done.1.east_ref), channel_id=1, source_target_pairs={{0,31},{1,0},{2,1},{3,2},{4,3},{5,4},{6,5},{7,6},{8,7},{9,8},{10,9... | collective-permute-start | bytes 1572872 | tf_op jit(solution)/shard_map/ppermute | solution.py:14
  44.8 0.0 collective-permute-done.3
  44.8 0.0 collective-permute-done.2
  44.9 0.1 pad_add_fusion.1
  44.9 0.1 pad_add_fusion
  45.0 0.3 fusion.6
  45.3 0.7 reshape_reshape.3.counts_ref
  46.0 3.5 %collective-permute-done.4.far_west_ref = bf16[4,128,512]{2,1,0:T(8,128)(2,1)S(1)} collective-permute-done((bf16[4,128,512]{2,1,0:T(8,128)(2,1)S(1)}, bf16[4,128,512]{2,1,0:T(8,128)(2,1)S(1)}, u32[]{:S(2)}, u32[]{:S(2)}) %collective-permute-start.4) | collective-permute-done | bytes 524320 | tf_op jit(solution)/shard_map/ppermute | solution.py:14
  49.5 0.0 copy-start.4
  49.5 1.8 %collective-permute-done.5.far_east_ref = bf16[4,128,512]{2,1,0:T(8,128)(2,1)S(1)} collective-permute-done((bf16[4,128,512]{2,1,0:T(8,128)(2,1)S(1)}, bf16[4,128,512]{2,1,0:T(8,128)(2,1)S(1)}, u32[]{:S(2)}, u32[]{:S(2)}) %collective-permute-start.5) | collective-permute-done | bytes 524320 | tf_op jit(solution)/shard_map/ppermute | solution.py:14
  51.3 0.0 copy-done.2
  51.3 0.0 copy-done.3
  51.3 0.0 copy-done.4
  51.3 0.0 copy-start.5
  51.3 0.8 copy-done.5
  52.1 15.5 %shard_map.65 = (bf16[4,128,512]{2,1,0:T(8,128)(2,1)}, f32[4,128,512]{2,1,0:T(8,128)}) custom-call(f32[288]{0:T(512)} %reshape_reshape.3.counts_ref, bf16[4,9,128,640]{3,2,1,0:T(8,128)(2,1)} %shard_map.64.band_ref, bf16[4,128,512]{2,1,0:T(8,128)(2,1)} %copy-done.4, bf16[4,128,512]{2,1,0:T(8,128)(2,1)} %copy-done.2, bf16[4,128,512]{2,1,0:T(8,128)(2,1)} %local_ref.1, ...), custom_call_target="tpu_custom_call" | custom-call | tf_op jit(solution)/shard_map/pallas_call | solution.py:129
  67.7 0.0 copy-start
  67.7 1.1 %fusion.12 = (bf16[2,128,512]{2,1,0:T(8,128)(2,1)S(1)}, bf16[2,128,512]{2,1,0:T(8,128)(2,1)S(1)}) fusion(bf16[4,128,512]{2,1,0:T(8,128)(2,1)} %get-tuple-element.14), kind=kLoop, calls=%fused_computation.35 | loop fusion | bytes 1048576 | tf_op jit(solution)/shard_map/slice | solution.py:23
  68.8 8.0 %collective-permute-start.6 = (bf16[2,128,512]{2,1,0:T(8,128)(2,1)S(1)}, bf16[2,128,512]{2,1,0:T(8,128)(2,1)S(1)}, u32[]{:S(2)}, u32[]{:S(2)}) collective-permute-start(bf16[2,128,512]{2,1,0:T(8,128)(2,1)S(1)} %get-tuple-element.15), channel_id=1, source_target_pairs={{0,32},{32,64},{64,96},{96,128},{128,160},{160,192},{192,224},{224... | collective-permute-start | bytes 786440 | tf_op jit(solution)/shard_map/ppermute | solution.py:22
  76.8 0.0 copy-start.1
  76.8 0.0 copy-start.7
  76.8 0.0 copy-start.8
  76.8 2.1 %collective-permute-start.7 = (bf16[2,128,512]{2,1,0:T(8,128)(2,1)S(1)}, bf16[2,128,512]{2,1,0:T(8,128)(2,1)S(1)}, u32[]{:S(2)}, u32[]{:S(2)}) collective-permute-start(bf16[2,128,512]{2,1,0:T(8,128)(2,1)S(1)} %get-tuple-element.16), channel_id=1, source_target_pairs={{32,0},{64,32},{96,64},{128,96},{160,128},{192,160},{224,192},{256... | collective-permute-start | bytes 786440 | tf_op jit(solution)/shard_map/ppermute | solution.py:25
  78.9 1.2 %collective-permute-done.6 = bf16[2,128,512]{2,1,0:T(8,128)(2,1)S(1)} collective-permute-done((bf16[2,128,512]{2,1,0:T(8,128)(2,1)S(1)}, bf16[2,128,512]{2,1,0:T(8,128)(2,1)S(1)}, u32[]{:S(2)}, u32[]{:S(2)}) %collective-permute-start.6) | collective-permute-done | bytes 262176 | tf_op jit(solution)/shard_map/ppermute | solution.py:22
  80.1 10.6 %collective-permute-done.7 = bf16[2,128,512]{2,1,0:T(8,128)(2,1)S(1)} collective-permute-done((bf16[2,128,512]{2,1,0:T(8,128)(2,1)S(1)}, bf16[2,128,512]{2,1,0:T(8,128)(2,1)S(1)}, u32[]{:S(2)}, u32[]{:S(2)}) %collective-permute-start.7) | collective-permute-done | bytes 262176 | tf_op jit(solution)/shard_map/ppermute | solution.py:25
  90.7 0.0 copy-done
  90.7 0.2 maximum_convert_fusion
  90.9 0.0 copy-done.1
  90.9 0.0 copy-done.7
  90.9 0.0 copy-done.8
  90.9 1.2 %fusion.3 = bf16[4,128,512]{2,1,0:T(8,128)(2,1)} fusion(f32[4,128,512]{2,1,0:T(8,128)S(1)} %copy-done.1, f32[8,128,512]{2,1,0:T(8,128)S(1)} %maximum_convert_fusion, f32[2,128,512]{2,1,0:T(8,128)S(1)} %maximum_convert_fusion.1, f32[4]{0:T(128)S(1)} %copy-done.7, pred[4]{0:T(512)(128)(4,1)S(1)} %copy-done.8), kind=kLoop, calls=%fused_computation.4 | loop fusion | flops 1310720 | bytes 3145748 | tf_op jit(solution)/shard_map/convert_element_type | solution.py:177
  (8 shorter events, 0.1 us)
Async XLA Ops:
  0.0 22.4 %collective-permute-start = (bf16[4,128,512]{2,1,0:T(8,128)(2,1)}, bf16[4,128,512]{2,1,0:T(8,128)(2,1)S(1)}, u32[]{:S(2)}, u32[]{:S(2)}) collective-permute-start(bf16[4,128,512]{2,1,0:T(8,128)(2,1)} %local_ref.1), channel_id=1, source_target_pairs={{0,1},{1,2},{2,3},{3,4},{4,5},{5,6},{6,7},{7,8},{8,9},{9,10},{10,1... | collective-permute-start | bytes 1572872 | tf_op jit(solution)/shard_map/ppermute | solution.py:14
  3.2 20.1 %collective-permute-start.1 = (bf16[4,128,512]{2,1,0:T(8,128)(2,1)}, bf16[4,128,512]{2,1,0:T(8,128)(2,1)S(1)}, u32[]{:S(2)}, u32[]{:S(2)}) collective-permute-start(bf16[4,128,512]{2,1,0:T(8,128)(2,1)} %local_ref.1), channel_id=1, source_target_pairs={{0,31},{1,0},{2,1},{3,2},{4,3},{5,4},{6,5},{7,6},{8,7},{9,8},{10,9... | collective-permute-start | bytes 1572872 | tf_op jit(solution)/shard_map/ppermute | solution.py:14
  14.8 8.5 %copy-start.6 = (s32[96,3]{0,1:T(4,128)S(1)}, s32[96,3]{0,1:T(4,128)}, u32[]{:S(2)}) copy-start(s32[96,3]{0,1:T(4,128)} %param.10) | copy-start | bytes 3460
  22.4 28.9 %copy-start.2 = (bf16[4,128,512]{2,1,0:T(8,128)(2,1)}, bf16[4,128,512]{2,1,0:T(8,128)(2,1)S(1)}, u32[]{:S(2)}) copy-start(bf16[4,128,512]{2,1,0:T(8,128)(2,1)S(1)} %collective-permute-done.west_ref) | copy-start | bytes 1572868
  23.3 27.9 %copy-start.3 = (bf16[4,128,512]{2,1,0:T(8,128)(2,1)}, bf16[4,128,512]{2,1,0:T(8,128)(2,1)S(1)}, u32[]{:S(2)}) copy-start(bf16[4,128,512]{2,1,0:T(8,128)(2,1)S(1)} %collective-permute-done.1.east_ref) | copy-start | bytes 1572868
  23.3 21.5 %collective-permute-start.3 = (s32[96,3]{0,1:T(4,128)S(1)}, s32[96,3]{0,1:T(4,128)S(1)}, u32[]{:S(2)}, u32[]{:S(2)}) collective-permute-start(s32[96,3]{0,1:T(4,128)S(1)} %copy-done.6), channel_id=1, source_target_pairs={{32,0},{64,32},{96,64},{128,96},{160,128},{192,160},{224,192},{256... | collective-permute-start | bytes 3464 | tf_op jit(solution)/shard_map/ppermute | solution.py:25
  26.8 18.0 %collective-permute-start.2 = (s32[96,3]{0,1:T(4,128)S(1)}, s32[96,3]{0,1:T(4,128)S(1)}, u32[]{:S(2)}, u32[]{:S(2)}) collective-permute-start(s32[96,3]{0,1:T(4,128)S(1)} %copy-done.6), channel_id=1, source_target_pairs={{0,32},{32,64},{64,96},{96,128},{128,160},{160,192},{192,224},{224... | collective-permute-start | bytes 3464 | tf_op jit(solution)/shard_map/ppermute | solution.py:22
  35.0 14.6 %collective-permute-start.4 = (bf16[4,128,512]{2,1,0:T(8,128)(2,1)S(1)}, bf16[4,128,512]{2,1,0:T(8,128)(2,1)S(1)}, u32[]{:S(2)}, u32[]{:S(2)}) collective-permute-start(bf16[4,128,512]{2,1,0:T(8,128)(2,1)S(1)} %collective-permute-done.west_ref), channel_id=1, source_target_pairs={{0,1},{1,2},{2,3},{3,4},{4,5},{5,6},{6,7},{7,8},{8,9},{9,10},{10,1... | collective-permute-start | bytes 1572872 | tf_op jit(solution)/shard_map/ppermute | solution.py:14
  36.9 14.4 %collective-permute-start.5 = (bf16[4,128,512]{2,1,0:T(8,128)(2,1)S(1)}, bf16[4,128,512]{2,1,0:T(8,128)(2,1)S(1)}, u32[]{:S(2)}, u32[]{:S(2)}) collective-permute-start(bf16[4,128,512]{2,1,0:T(8,128)(2,1)S(1)} %collective-permute-done.1.east_ref), channel_id=1, source_target_pairs={{0,31},{1,0},{2,1},{3,2},{4,3},{5,4},{6,5},{7,6},{8,7},{9,8},{10,9... | collective-permute-start | bytes 1572872 | tf_op jit(solution)/shard_map/ppermute | solution.py:14
  49.5 1.8 %copy-start.4 = (bf16[4,128,512]{2,1,0:T(8,128)(2,1)}, bf16[4,128,512]{2,1,0:T(8,128)(2,1)S(1)}, u32[]{:S(2)}) copy-start(bf16[4,128,512]{2,1,0:T(8,128)(2,1)S(1)} %collective-permute-done.4.far_west_ref) | copy-start | bytes 1572868
  51.3 0.9 copy-start.5
  67.7 23.0 %copy-start = (bf16[4,128,512]{2,1,0:T(8,128)(2,1)S(1)}, bf16[4,128,512]{2,1,0:T(8,128)(2,1)}, u32[]{:S(2)}) copy-start(bf16[4,128,512]{2,1,0:T(8,128)(2,1)} %get-tuple-element.14) | copy-start | bytes 1572868
  68.8 11.3 %collective-permute-start.6 = (bf16[2,128,512]{2,1,0:T(8,128)(2,1)S(1)}, bf16[2,128,512]{2,1,0:T(8,128)(2,1)S(1)}, u32[]{:S(2)}, u32[]{:S(2)}) collective-permute-start(bf16[2,128,512]{2,1,0:T(8,128)(2,1)S(1)} %get-tuple-element.15), channel_id=1, source_target_pairs={{0,32},{32,64},{64,96},{96,128},{128,160},{160,192},{192,224},{224... | collective-permute-start | bytes 786440 | tf_op jit(solution)/shard_map/ppermute | solution.py:22
  76.8 14.1 %copy-start.1 = (f32[4,128,512]{2,1,0:T(8,128)S(1)}, f32[4,128,512]{2,1,0:T(8,128)}, u32[]{:S(2)}) copy-start(f32[4,128,512]{2,1,0:T(8,128)} %get-tuple-element.13) | copy-start | bytes 3145732
  76.8 14.1 %copy-start.7 = (f32[4]{0:T(128)S(1)}, f32[4]{0:T(128)}, u32[]{:S(2)}) copy-start(f32[4]{0:T(128)} %param.9) | copy-start | bytes 52
  76.8 14.1 %copy-start.8 = (pred[4]{0:T(512)(128)(4,1)S(1)}, pred[4]{0:T(512)(128)(4,1)}, u32[]{:S(2)}) copy-start(pred[4]{0:T(512)(128)(4,1)} %constant.24.clone.1) | copy-start | bytes 16
  76.8 13.8 %collective-permute-start.7 = (bf16[2,128,512]{2,1,0:T(8,128)(2,1)S(1)}, bf16[2,128,512]{2,1,0:T(8,128)(2,1)S(1)}, u32[]{:S(2)}, u32[]{:S(2)}) collective-permute-start(bf16[2,128,512]{2,1,0:T(8,128)(2,1)S(1)} %get-tuple-element.16), channel_id=1, source_target_pairs={{32,0},{64,32},{96,64},{128,96},{160,128},{192,160},{224,192},{256... | collective-permute-start | bytes 786440 | tf_op jit(solution)/shard_map/ppermute | solution.py:25

commit v6 on v5

--- a/solution.py
+++ b/solution.py
@@ -38,9 +38,9 @@
 def longitude_halo(source, support):
     west = shifted(source, "lon", 1)
     east = shifted(source, "lon", -1)
-    west, east, support = lax.optimization_barrier((west, east, support))
     far_west = shifted(west, "lon", 1)
     far_east = shifted(east, "lon", -1)
+    far_west, far_east, support = lax.optimization_barrier((far_west, far_east, support))
     return far_west, west, east, far_east, support
 
 

time: 92.6 us -> 98 us (1.058)
  waiting for transfers between devices: 20.8 us -> 25 us
  starting transfers between devices: 43.9 us -> 46 us
    ppermute x4, waiting for transfers between devices: 9.03 us -> 12.5 us  [shifted(): lax.ppermute(value, axis, [(i, (i + by) % length) for i in range(length)])]
    ppermute x2, starting transfers between devices: 16.1 us -> 18 us  [with_halo(): lax.ppermute(lax.slice_in_dim(block, block.shape[dim] - width, None, axis...]
  transfers between devices with their start and end apart: 8 -> 8, of which waited for: 6 -> 6; matrix products, arithmetic and copies ran while one was open for 4% -> 2% of each run, Pallas kernels for 5% -> 5%
where the time goes in v6:
time: 98 us; the launch traced here: 97.5 us
  starting transfers between devices  46 us (47%)
  waiting for transfers between devices  25 us (26%)
  Pallas kernels  20.3 us (21%)
  other arithmetic  3.9 us (4%)
  local copies, waits for them, and re-layouts  1.85 us (2%)
    ppermute x4, starting transfers between devices, shifted(): lax.ppermute(value, axis, [(i, (i + by) % length) for i in range(length)])  21.6 us
    ppermute x2, starting transfers between devices, with_halo(): lax.ppermute(lax.slice_in_dim(block, block.shape[dim] - width, None, axis...  18 us
    pallas_call x1, Pallas kernels, block_partials(): pl.pallas_call(_block_kernel, grid=(kinds,), in_specs=[pl.BlockSpec(memor...  15.5 us
    ppermute x4, waiting for transfers between devices, shifted(): lax.ppermute(value, axis, [(i, (i + by) % length) for i in range(length)])  12.5 us
    ppermute x2, waiting for transfers between devices, with_halo(): lax.ppermute(lax.slice_in_dim(block, 0, width, axis=dim), axis, backward)  10.6 us
    ppermute x2, starting transfers between devices, with_halo(): lax.ppermute(lax.slice_in_dim(block, 0, width, axis=dim), axis, backward)  6.39 us
    pallas_call x1, Pallas kernels, band_matrix(): pl.pallas_call(_toeplitz_kernel, grid=(rows,), in_specs=[pl.BlockSpec((1,...  4.76 us
  transfers between devices with their start and end apart: 8, of which 6 were waited for; matrix products, arithmetic and copies ran while one was open for 2% of the time, Pallas kernels for 5%

profile of v6, /device:TPU:7, one launch (start us, length us, event | category | flops | bytes accessed | tf_op | source)
XLA Modules:
  0.0 97.5 jit_solution(8494457973603927921)
XLA Ops:
  0.0 3.2 %collective-permute-start = (bf16[4,128,512]{2,1,0:T(8,128)(2,1)}, bf16[4,128,512]{2,1,0:T(8,128)(2,1)S(1)}, u32[]{:S(2)}, u32[]{:S(2)}) collective-permute-start(bf16[4,128,512]{2,1,0:T(8,128)(2,1)} %local_ref.1), channel_id=1, source_target_pairs={{0,1},{1,2},{2,3},{3,4},{4,5},{5,6},{6,7},{7,8},{8,9},{9,10},{10,1... | collective-permute-start | bytes 1572872 | tf_op jit(solution)/shard_map/ppermute | solution.py:14
  3.2 9.2 %collective-permute-start.2 = (bf16[4,128,512]{2,1,0:T(8,128)(2,1)}, bf16[4,128,512]{2,1,0:T(8,128)(2,1)S(1)}, u32[]{:S(2)}, u32[]{:S(2)}) collective-permute-start(bf16[4,128,512]{2,1,0:T(8,128)(2,1)} %local_ref.1), channel_id=1, source_target_pairs={{0,31},{1,0},{2,1},{3,2},{4,3},{5,4},{6,5},{7,6},{8,7},{9,8},{10,9... | collective-permute-start | bytes 1572872 | tf_op jit(solution)/shard_map/ppermute | solution.py:14
  12.5 9.9 %collective-permute-done.west_ref = bf16[4,128,512]{2,1,0:T(8,128)(2,1)S(1)} collective-permute-done((bf16[4,128,512]{2,1,0:T(8,128)(2,1)}, bf16[4,128,512]{2,1,0:T(8,128)(2,1)S(1)}, u32[]{:S(2)}, u32[]{:S(2)}) %collective-permute-start) | collective-permute-done | bytes 524320 | tf_op jit(solution)/shard_map/ppermute | solution.py:14
  22.4 0.0 copy-start.2
  22.4 1.9 %collective-permute-start.1 = (bf16[4,128,512]{2,1,0:T(8,128)(2,1)S(1)}, bf16[4,128,512]{2,1,0:T(8,128)(2,1)S(1)}, u32[]{:S(2)}, u32[]{:S(2)}) collective-permute-start(bf16[4,128,512]{2,1,0:T(8,128)(2,1)S(1)} %collective-permute-done.west_ref), channel_id=1, source_target_pairs={{0,1},{1,2},{2,3},{3,4},{4,5},{5,6},{6,7},{7,8},{8,9},{9,10},{10,1... | collective-permute-start | bytes 1572872 | tf_op jit(solution)/shard_map/ppermute | solution.py:14
  24.3 0.0 collective-permute-done.2.east_ref
  24.3 0.0 copy-start.3
  24.3 7.3 %collective-permute-start.3 = (bf16[4,128,512]{2,1,0:T(8,128)(2,1)S(1)}, bf16[4,128,512]{2,1,0:T(8,128)(2,1)S(1)}, u32[]{:S(2)}, u32[]{:S(2)}) collective-permute-start(bf16[4,128,512]{2,1,0:T(8,128)(2,1)S(1)} %collective-permute-done.2.east_ref), channel_id=1, source_target_pairs={{0,31},{1,0},{2,1},{3,2},{4,3},{5,4},{6,5},{7,6},{8,7},{9,8},{10,9... | collective-permute-start | bytes 1572872 | tf_op jit(solution)/shard_map/ppermute | solution.py:14
  31.6 0.7 broadcast_compare_fusion
  32.3 0.9 fusion.4
  33.2 0.7 pad_convert_fusion.taps_ref
  33.9 0.0 copy-start.6
  33.9 4.8 %shard_map.64.band_ref = bf16[4,9,128,640]{3,2,1,0:T(8,128)(2,1)} custom-call(f32[4,9,640]{2,1,0:T(8,128)} %pad_convert_fusion.taps_ref), custom_call_target="tpu_custom_call" | custom-call | tf_op jit(solution)/shard_map/pallas_call | solution.py:74
  38.7 0.0 copy-done.2
  38.7 0.0 copy-done.3
  38.7 1.7 %collective-permute-done.1.far_west_ref = bf16[4,128,512]{2,1,0:T(8,128)(2,1)S(1)} collective-permute-done((bf16[4,128,512]{2,1,0:T(8,128)(2,1)S(1)}, bf16[4,128,512]{2,1,0:T(8,128)(2,1)S(1)}, u32[]{:S(2)}, u32[]{:S(2)}) %collective-permute-start.1) | collective-permute-done | bytes 524320 | tf_op jit(solution)/shard_map/ppermute | solution.py:14
  40.3 0.0 copy-start.4
  40.3 0.9 collective-permute-done.3.far_east_ref
  41.3 0.0 copy-done.6
  41.3 0.0 copy-start.5
  41.3 4.3 %collective-permute-start.5 = (s32[96,3]{0,1:T(4,128)S(1)}, s32[96,3]{0,1:T(4,128)S(1)}, u32[]{:S(2)}, u32[]{:S(2)}) collective-permute-start(s32[96,3]{0,1:T(4,128)S(1)} %copy-done.6), channel_id=1, source_target_pairs={{32,0},{64,32},{96,64},{128,96},{160,128},{192,160},{224,192},{256... | collective-permute-start | bytes 3464 | tf_op jit(solution)/shard_map/ppermute | solution.py:25
  45.6 7.8 %collective-permute-start.4 = (s32[96,3]{0,1:T(4,128)S(1)}, s32[96,3]{0,1:T(4,128)S(1)}, u32[]{:S(2)}, u32[]{:S(2)}) collective-permute-start(s32[96,3]{0,1:T(4,128)S(1)} %copy-done.6), channel_id=1, source_target_pairs={{0,32},{32,64},{64,96},{96,128},{128,160},{160,192},{192,224},{224... | collective-permute-start | bytes 3464 | tf_op jit(solution)/shard_map/ppermute | solution.py:22
  53.4 0.0 collective-permute-done.5
  53.4 0.7 collective-permute-done.4
  54.1 0.1 pad_add_fusion.1
  54.2 0.1 pad_add_fusion
  54.3 0.3 fusion.6
  54.6 0.7 reshape_reshape.3.counts_ref
  55.3 0.0 copy-done.4
  55.3 0.0 copy-done.5
  55.3 15.5 %shard_map.65 = (bf16[4,128,512]{2,1,0:T(8,128)(2,1)}, f32[4,128,512]{2,1,0:T(8,128)}) custom-call(f32[288]{0:T(512)} %reshape_reshape.3.counts_ref, bf16[4,9,128,640]{3,2,1,0:T(8,128)(2,1)} %shard_map.64.band_ref, bf16[4,128,512]{2,1,0:T(8,128)(2,1)} %copy-done.4, bf16[4,128,512]{2,1,0:T(8,128)(2,1)} %copy-done.2, bf16[4,128,512]{2,1,0:T(8,128)(2,1)} %local_ref.1, ...), custom_call_target="tpu_custom_call" | custom-call | tf_op jit(solution)/shard_map/pallas_call | solution.py:129
  70.8 0.0 copy-start
  70.8 1.1 %fusion.12 = (bf16[2,128,512]{2,1,0:T(8,128)(2,1)S(1)}, bf16[2,128,512]{2,1,0:T(8,128)(2,1)S(1)}) fusion(bf16[4,128,512]{2,1,0:T(8,128)(2,1)} %get-tuple-element.14), kind=kLoop, calls=%fused_computation.35 | loop fusion | bytes 1048576 | tf_op jit(solution)/shard_map/slice | solution.py:23
  72.0 10.2 %collective-permute-start.6 = (bf16[2,128,512]{2,1,0:T(8,128)(2,1)S(1)}, bf16[2,128,512]{2,1,0:T(8,128)(2,1)S(1)}, u32[]{:S(2)}, u32[]{:S(2)}) collective-permute-start(bf16[2,128,512]{2,1,0:T(8,128)(2,1)S(1)} %get-tuple-element.15), channel_id=1, source_target_pairs={{0,32},{32,64},{64,96},{96,128},{128,160},{160,192},{192,224},{224... | collective-permute-start | bytes 786440 | tf_op jit(solution)/shard_map/ppermute | solution.py:22
  82.2 0.0 copy-start.1
  82.2 0.0 copy-start.7
  82.2 0.0 copy-start.8
  82.2 2.1 %collective-permute-start.7 = (bf16[2,128,512]{2,1,0:T(8,128)(2,1)S(1)}, bf16[2,128,512]{2,1,0:T(8,128)(2,1)S(1)}, u32[]{:S(2)}, u32[]{:S(2)}) collective-permute-start(bf16[2,128,512]{2,1,0:T(8,128)(2,1)S(1)} %get-tuple-element.16), channel_id=1, source_target_pairs={{32,0},{64,32},{96,64},{128,96},{160,128},{192,160},{224,192},{256... | collective-permute-start | bytes 786440 | tf_op jit(solution)/shard_map/ppermute | solution.py:25
  84.3 1.2 %collective-permute-done.6 = bf16[2,128,512]{2,1,0:T(8,128)(2,1)S(1)} collective-permute-done((bf16[2,128,512]{2,1,0:T(8,128)(2,1)S(1)}, bf16[2,128,512]{2,1,0:T(8,128)(2,1)S(1)}, u32[]{:S(2)}, u32[]{:S(2)}) %collective-permute-start.6) | collective-permute-done | bytes 262176 | tf_op jit(solution)/shard_map/ppermute | solution.py:22
  85.5 10.6 %collective-permute-done.7 = bf16[2,128,512]{2,1,0:T(8,128)(2,1)S(1)} collective-permute-done((bf16[2,128,512]{2,1,0:T(8,128)(2,1)S(1)}, bf16[2,128,512]{2,1,0:T(8,128)(2,1)S(1)}, u32[]{:S(2)}, u32[]{:S(2)}) %collective-permute-start.7) | collective-permute-done | bytes 262176 | tf_op jit(solution)/shard_map/ppermute | solution.py:25
  96.1 0.0 copy-done
  96.1 0.2 maximum_convert_fusion
  96.3 0.0 copy-done.1
  96.3 0.0 copy-done.7
  96.3 0.0 copy-done.8
  96.3 1.2 %fusion.3 = bf16[4,128,512]{2,1,0:T(8,128)(2,1)} fusion(f32[4,128,512]{2,1,0:T(8,128)S(1)} %copy-done.1, f32[8,128,512]{2,1,0:T(8,128)S(1)} %maximum_convert_fusion, f32[2,128,512]{2,1,0:T(8,128)S(1)} %maximum_convert_fusion.1, f32[4]{0:T(128)S(1)} %copy-done.7, pred[4]{0:T(512)(128)(4,1)S(1)} %copy-done.8), kind=kLoop, calls=%fused_computation.4 | loop fusion | flops 1310720 | bytes 3145748 | tf_op jit(solution)/shard_map/convert_element_type | solution.py:177
  (8 shorter events, 0.1 us)
Async XLA Ops:
  0.0 22.4 %collective-permute-start = (bf16[4,128,512]{2,1,0:T(8,128)(2,1)}, bf16[4,128,512]{2,1,0:T(8,128)(2,1)S(1)}, u32[]{:S(2)}, u32[]{:S(2)}) collective-permute-start(bf16[4,128,512]{2,1,0:T(8,128)(2,1)} %local_ref.1), channel_id=1, source_target_pairs={{0,1},{1,2},{2,3},{3,4},{4,5},{5,6},{6,7},{7,8},{8,9},{9,10},{10,1... | collective-permute-start | bytes 1572872 | tf_op jit(solution)/shard_map/ppermute | solution.py:14
  3.2 21.1 %collective-permute-start.2 = (bf16[4,128,512]{2,1,0:T(8,128)(2,1)}, bf16[4,128,512]{2,1,0:T(8,128)(2,1)S(1)}, u32[]{:S(2)}, u32[]{:S(2)}) collective-permute-start(bf16[4,128,512]{2,1,0:T(8,128)(2,1)} %local_ref.1), channel_id=1, source_target_pairs={{0,31},{1,0},{2,1},{3,2},{4,3},{5,4},{6,5},{7,6},{8,7},{9,8},{10,9... | collective-permute-start | bytes 1572872 | tf_op jit(solution)/shard_map/ppermute | solution.py:14
  22.4 16.3 %copy-start.2 = (bf16[4,128,512]{2,1,0:T(8,128)(2,1)}, bf16[4,128,512]{2,1,0:T(8,128)(2,1)S(1)}, u32[]{:S(2)}) copy-start(bf16[4,128,512]{2,1,0:T(8,128)(2,1)S(1)} %collective-permute-done.west_ref) | copy-start | bytes 1572868
  22.4 18.0 %collective-permute-start.1 = (bf16[4,128,512]{2,1,0:T(8,128)(2,1)S(1)}, bf16[4,128,512]{2,1,0:T(8,128)(2,1)S(1)}, u32[]{:S(2)}, u32[]{:S(2)}) collective-permute-start(bf16[4,128,512]{2,1,0:T(8,128)(2,1)S(1)} %collective-permute-done.west_ref), channel_id=1, source_target_pairs={{0,1},{1,2},{2,3},{3,4},{4,5},{5,6},{6,7},{7,8},{8,9},{9,10},{10,1... | collective-permute-start | bytes 1572872 | tf_op jit(solution)/shard_map/ppermute | solution.py:14
  24.3 14.4 %copy-start.3 = (bf16[4,128,512]{2,1,0:T(8,128)(2,1)}, bf16[4,128,512]{2,1,0:T(8,128)(2,1)S(1)}, u32[]{:S(2)}) copy-start(bf16[4,128,512]{2,1,0:T(8,128)(2,1)S(1)} %collective-permute-done.2.east_ref) | copy-start | bytes 1572868
  24.3 17.0 %collective-permute-start.3 = (bf16[4,128,512]{2,1,0:T(8,128)(2,1)S(1)}, bf16[4,128,512]{2,1,0:T(8,128)(2,1)S(1)}, u32[]{:S(2)}, u32[]{:S(2)}) collective-permute-start(bf16[4,128,512]{2,1,0:T(8,128)(2,1)S(1)} %collective-permute-done.2.east_ref), channel_id=1, source_target_pairs={{0,31},{1,0},{2,1},{3,2},{4,3},{5,4},{6,5},{7,6},{8,7},{9,8},{10,9... | collective-permute-start | bytes 1572872 | tf_op jit(solution)/shard_map/ppermute | solution.py:14
  33.9 7.4 %copy-start.6 = (s32[96,3]{0,1:T(4,128)S(1)}, s32[96,3]{0,1:T(4,128)}, u32[]{:S(2)}) copy-start(s32[96,3]{0,1:T(4,128)} %param.10) | copy-start | bytes 3460
  40.3 15.0 %copy-start.4 = (bf16[4,128,512]{2,1,0:T(8,128)(2,1)}, bf16[4,128,512]{2,1,0:T(8,128)(2,1)S(1)}, u32[]{:S(2)}) copy-start(bf16[4,128,512]{2,1,0:T(8,128)(2,1)S(1)} %collective-permute-done.1.far_west_ref) | copy-start | bytes 1572868
  41.3 14.0 %copy-start.5 = (bf16[4,128,512]{2,1,0:T(8,128)(2,1)}, bf16[4,128,512]{2,1,0:T(8,128)(2,1)S(1)}, u32[]{:S(2)}) copy-start(bf16[4,128,512]{2,1,0:T(8,128)(2,1)S(1)} %collective-permute-done.3.far_east_ref) | copy-start | bytes 1572868
  41.3 12.1 %collective-permute-start.5 = (s32[96,3]{0,1:T(4,128)S(1)}, s32[96,3]{0,1:T(4,128)S(1)}, u32[]{:S(2)}, u32[]{:S(2)}) collective-permute-start(s32[96,3]{0,1:T(4,128)S(1)} %copy-done.6), channel_id=1, source_target_pairs={{32,0},{64,32},{96,64},{128,96},{160,128},{192,160},{224,192},{256... | collective-permute-start | bytes 3464 | tf_op jit(solution)/shard_map/ppermute | solution.py:25
  45.6 8.5 %collective-permute-start.4 = (s32[96,3]{0,1:T(4,128)S(1)}, s32[96,3]{0,1:T(4,128)S(1)}, u32[]{:S(2)}, u32[]{:S(2)}) collective-permute-start(s32[96,3]{0,1:T(4,128)S(1)} %copy-done.6), channel_id=1, source_target_pairs={{0,32},{32,64},{64,96},{96,128},{128,160},{160,192},{192,224},{224... | collective-permute-start | bytes 3464 | tf_op jit(solution)/shard_map/ppermute | solution.py:22
  70.8 25.3 %copy-start = (bf16[4,128,512]{2,1,0:T(8,128)(2,1)S(1)}, bf16[4,128,512]{2,1,0:T(8,128)(2,1)}, u32[]{:S(2)}) copy-start(bf16[4,128,512]{2,1,0:T(8,128)(2,1)} %get-tuple-element.14) | copy-start | bytes 1572868
  72.0 13.5 %collective-permute-start.6 = (bf16[2,128,512]{2,1,0:T(8,128)(2,1)S(1)}, bf16[2,128,512]{2,1,0:T(8,128)(2,1)S(1)}, u32[]{:S(2)}, u32[]{:S(2)}) collective-permute-start(bf16[2,128,512]{2,1,0:T(8,128)(2,1)S(1)} %get-tuple-element.15), channel_id=1, source_target_pairs={{0,32},{32,64},{64,96},{96,128},{128,160},{160,192},{192,224},{224... | collective-permute-start | bytes 786440 | tf_op jit(solution)/shard_map/ppermute | solution.py:22
  82.2 14.1 %copy-start.1 = (f32[4,128,512]{2,1,0:T(8,128)S(1)}, f32[4,128,512]{2,1,0:T(8,128)}, u32[]{:S(2)}) copy-start(f32[4,128,512]{2,1,0:T(8,128)} %get-tuple-element.13) | copy-start | bytes 3145732
  82.2 14.1 %copy-start.7 = (f32[4]{0:T(128)S(1)}, f32[4]{0:T(128)}, u32[]{:S(2)}) copy-start(f32[4]{0:T(128)} %param.9) | copy-start | bytes 52
  82.2 14.1 %copy-start.8 = (pred[4]{0:T(512)(128)(4,1)S(1)}, pred[4]{0:T(512)(128)(4,1)}, u32[]{:S(2)}) copy-start(pred[4]{0:T(512)(128)(4,1)} %constant.24.clone.1) | copy-start | bytes 16
  82.2 13.8 %collective-permute-start.7 = (bf16[2,128,512]{2,1,0:T(8,128)(2,1)S(1)}, bf16[2,128,512]{2,1,0:T(8,128)(2,1)S(1)}, u32[]{:S(2)}, u32[]{:S(2)}) collective-permute-start(bf16[2,128,512]{2,1,0:T(8,128)(2,1)S(1)} %get-tuple-element.16), channel_id=1, source_target_pairs={{32,0},{64,32},{96,64},{128,96},{160,128},{192,160},{224,192},{256... | collective-permute-start | bytes 786440 | tf_op jit(solution)/shard_map/ppermute | solution.py:25

commit v7 on v2

--- a/solution.py
+++ b/solution.py
@@ -80,7 +80,7 @@
 
 
 def _block_kernel(counts_ref, band_ref, far_west_ref, west_ref, local_ref, east_ref, far_east_ref,
-                  weight_ref, edge_ref, inner_ref, window_ref, response_ref, mixed_ref, total_ref):
+                  weight_ref, upper_ref, lower_ref, inner_ref, window_ref, response_ref, mixed_ref, total_ref):
     kind = pl.program_id(0)
     kinds = pl.num_programs(0)
     input_rows, cols, _ = local_ref.shape
@@ -115,8 +115,8 @@
     @pl.when(kind == kinds - 1)
     def _():
         inner_ref[...] = total_ref[RIM : RIM + input_rows]
-        edge_ref[:RIM] = total_ref[:RIM].astype(edge_ref.dtype)
-        edge_ref[RIM:] = total_ref[RIM + input_rows :].astype(edge_ref.dtype)
+        upper_ref[...] = total_ref[:RIM].astype(upper_ref.dtype)
+        lower_ref[...] = total_ref[RIM + input_rows :].astype(lower_ref.dtype)
 
 
 def block_partials(counts, short_taps, parts, mix_weight):
@@ -134,9 +134,10 @@
         ]
         + [whole(parts[0].shape)] * len(parts)
         + [pl.BlockSpec((1,) + mix_weight.shape[1:], lambda k: (k, 0, 0))],
-        out_specs=[whole((2 * RIM, cols, channels)), whole((rows, cols, channels))],
+        out_specs=[whole((RIM, cols, channels))] * 2 + [whole((rows, cols, channels))],
         out_shape=[
-            jax.ShapeDtypeStruct((2 * RIM, cols, channels), jnp.bfloat16),
+            jax.ShapeDtypeStruct((RIM, cols, channels), jnp.bfloat16),
+            jax.ShapeDtypeStruct((RIM, cols, channels), jnp.bfloat16),
             jax.ShapeDtypeStruct((rows, cols, channels), jnp.float32),
         ],
         scratch_shapes=[
@@ -167,12 +168,16 @@
         [(support[:, 1] >= 0) & (support[:, 1] < rows), above[:, 1] >= rows, below[:, 1] < 0]
     )
     counts = coupling(out_rows, in_rows, basis, valid, rows + 2 * RIM, rows, kinds)
-    outgoing, inner = block_partials(
+    upper, lower, inner = block_partials(
         counts, short_taps, (far_west, west, field, east, far_east), mix_weight
     )
-    incoming = with_halo(outgoing, (("lat", 0),), RIM).astype(jnp.float32)
-    inner = inner + jnp.pad(incoming[:RIM], ((0, rows - RIM), (0, 0), (0, 0)))
-    inner = inner + jnp.pad(incoming[3 * RIM :], ((rows - RIM, 0), (0, 0), (0, 0)))
+    count = lax.axis_size("lat")
+    forward = [(i, i + 1) for i in range(count - 1)]
+    backward = [(target, source) for source, target in forward]
+    from_below = lax.ppermute(upper, "lat", backward).astype(jnp.float32)
+    from_above = lax.ppermute(lower, "lat", forward).astype(jnp.float32)
+    inner = inner + jnp.pad(from_above, ((0, rows - RIM), (0, 0), (0, 0)))
+    inner = inner + jnp.pad(from_below, ((rows - RIM, 0), (0, 0), (0, 0)))
     return (inner * row_scale[:, None, None]).astype(jnp.bfloat16)
 
 

time: 91.3 us -> 91 us (level)
  local copies, waits for them, and re-layouts: 2.69 us -> 1.55 us
    ppermute x0 -> x2, waiting for transfers between devices: none -> 12 us  [the longest x1 10.3 us: on_device(): from_below = lax.ppermute(upper, 'lat', backward).astype(jnp.float32)]
    ppermute x2 -> x1, waiting for transfers between devices: 10.6 us -> 0.01 us  [with_halo(): lax.ppermute(lax.slice_in_dim(block, 0, width, axis=dim), axis, backward)]
    ppermute x0 -> x2, starting transfers between devices: none -> 10.4 us  [the longest x1 8.52 us: on_device(): from_above = lax.ppermute(lower, 'lat', forward).astype(jnp.float32)]
    ppermute x2 -> x1, starting transfers between devices: 19.6 us -> 11.1 us  [with_halo(): lax.ppermute(lax.slice_in_dim(block, block.shape[dim] - width, None, axis...]
    ppermute x2 -> x1, starting transfers between devices: 3.97 us -> 1.92 us  [with_halo(): lax.ppermute(lax.slice_in_dim(block, 0, width, axis=dim), axis, backward)]
    ppermute x2 -> x1, waiting for transfers between devices: 1.2 us -> 0.01 us  [with_halo(): lax.ppermute(lax.slice_in_dim(block, block.shape[dim] - width, None, axis...]
    slice x1 -> x0, local copies, waits for them, and re-layouts: 1.12 us -> none  [with_halo(): lax.slice_in_dim(block, block.shape[dim] - width, None, axis=dim)]
    convert_element_type x1, other arithmetic: 1.18 us -> 2.25 us  [on_device(): return (inner * row_scale[:, None, None]).astype(jnp.bfloat16)]
  transfers between devices with their start and end apart: 8 -> 8, of which waited for: 4 -> 4; matrix products, arithmetic and copies ran while one was open for 5% -> 6% of each run, Pallas kernels for 5% -> 5%
where the time goes in v7:
time: 91 us; the launch traced here: 90.4 us
  starting transfers between devices  42.4 us (47%)
  Pallas kernels  20.2 us (22%)
  waiting for transfers between devices  19.5 us (21%)
  other arithmetic  6.24 us (7%)
  local copies, waits for them, and re-layouts  1.55 us (2%)
    ppermute x4, starting transfers between devices, shifted(): lax.ppermute(value, axis, [(i, (i + by) % length) for i in range(length)])  18.9 us
    pallas_call x1, Pallas kernels, block_partials(): pl.pallas_call(_block_kernel, grid=(kinds,), in_specs=[pl.BlockSpec(memor...  15.5 us
    ppermute x1, starting transfers between devices, with_halo(): lax.ppermute(lax.slice_in_dim(block, block.shape[dim] - width, None, axis...  11.1 us
    ppermute x1, waiting for transfers between devices, on_device(): from_below = lax.ppermute(upper, 'lat', backward).astype(jnp.float32)  10.3 us
    ppermute x1, starting transfers between devices, on_device(): from_above = lax.ppermute(lower, 'lat', forward).astype(jnp.float32)  8.52 us
    ppermute x4, waiting for transfers between devices, shifted(): lax.ppermute(value, axis, [(i, (i + by) % length) for i in range(length)])  7.55 us
    pallas_call x1, Pallas kernels, band_matrix(): pl.pallas_call(_toeplitz_kernel, grid=(rows,), in_specs=[pl.BlockSpec((1,...  4.74 us
    convert_element_type x1, other arithmetic, on_device(): return (inner * row_scale[:, None, None]).astype(jnp.bfloat16)  2.25 us
  transfers between devices with their start and end apart: 8, of which 4 were waited for; matrix products, arithmetic and copies ran while one was open for 6% of the time, Pallas kernels for 5%

profile of v7, /device:TPU:7, one launch (start us, length us, event | category | flops | bytes accessed | tf_op | source)
XLA Modules:
  0.0 90.4 jit_solution(14590381676485069063)
XLA Ops:
  0.0 11.1 %collective-permute-start = (s32[96,3]{0,1:T(4,128)}, s32[96,3]{0,1:T(4,128)S(1)}, u32[]{:S(2)}, u32[]{:S(2)}) collective-permute-start(s32[96,3]{0,1:T(4,128)} %param.10), channel_id=1, source_target_pairs={{0,32},{32,64},{64,96},{96,128},{128,160},{160,192},{192,224},{224... | collective-permute-start | bytes 3464 | tf_op jit(solution)/shard_map/ppermute | solution.py:22
  11.1 1.9 %collective-permute-start.1 = (s32[96,3]{0,1:T(4,128)}, s32[96,3]{0,1:T(4,128)S(1)}, u32[]{:S(2)}, u32[]{:S(2)}) collective-permute-start(s32[96,3]{0,1:T(4,128)} %param.10), channel_id=1, source_target_pairs={{32,0},{64,32},{96,64},{128,96},{160,128},{192,160},{224,192},{256... | collective-permute-start | bytes 3464 | tf_op jit(solution)/shard_map/ppermute | solution.py:25
  13.0 3.2 %collective-permute-start.2 = (bf16[4,128,512]{2,1,0:T(8,128)(2,1)}, bf16[4,128,512]{2,1,0:T(8,128)(2,1)S(1)}, u32[]{:S(2)}, u32[]{:S(2)}) collective-permute-start(bf16[4,128,512]{2,1,0:T(8,128)(2,1)} %local_ref.1), channel_id=1, source_target_pairs={{0,1},{1,2},{2,3},{3,4},{4,5},{5,6},{6,7},{7,8},{8,9},{9,10},{10,1... | collective-permute-start | bytes 1572872 | tf_op jit(solution)/shard_map/ppermute | solution.py:14
  16.3 6.5 %collective-permute-start.4 = (bf16[4,128,512]{2,1,0:T(8,128)(2,1)}, bf16[4,128,512]{2,1,0:T(8,128)(2,1)S(1)}, u32[]{:S(2)}, u32[]{:S(2)}) collective-permute-start(bf16[4,128,512]{2,1,0:T(8,128)(2,1)} %local_ref.1), channel_id=1, source_target_pairs={{0,31},{1,0},{2,1},{3,2},{4,3},{5,4},{6,5},{7,6},{8,7},{9,8},{10,9... | collective-permute-start | bytes 1572872 | tf_op jit(solution)/shard_map/ppermute | solution.py:14
  22.8 0.7 compare_and_fusion
  23.5 0.8 add_bitcast_fusion.4
  24.3 0.7 broadcast_compare_fusion
  25.0 0.9 %fusion = bf16[4,9,513]{2,1,0:T(8,128)(2,1)S(1)} fusion(f32[4,9,513]{2,0,1:T(4,128)} %param.8, pred[4,513]{1,0:T(4,128)(4,1)S(1)} %broadcast_compare_fusion), kind=kLoop, calls=%fused_computation.2 | loop fusion | flops 18468 | bytes 112860 | tf_op jit(solution)/shard_map/convert_element_type | solution.py:35
  25.9 0.7 pad_convert_fusion.taps_ref
  26.6 4.7 %shard_map.64.band_ref = bf16[4,9,128,640]{3,2,1,0:T(8,128)(2,1)} custom-call(f32[4,9,640]{2,1,0:T(8,128)} %pad_convert_fusion.taps_ref), custom_call_target="tpu_custom_call" | custom-call | tf_op jit(solution)/shard_map/pallas_call | solution.py:73
  31.4 0.0 collective-permute-done
  31.4 0.0 collective-permute-done.1
  31.4 0.1 pad_add_fusion.1
  31.5 0.0 collective-permute-done.2.west_ref
  31.5 0.0 copy-start
  31.5 1.9 %collective-permute-start.3 = (bf16[4,128,512]{2,1,0:T(8,128)(2,1)S(1)}, bf16[4,128,512]{2,1,0:T(8,128)(2,1)S(1)}, u32[]{:S(2)}, u32[]{:S(2)}) collective-permute-start(bf16[4,128,512]{2,1,0:T(8,128)(2,1)S(1)} %collective-permute-done.2.west_ref), channel_id=1, source_target_pairs={{0,1},{1,2},{2,3},{3,4},{4,5},{5,6},{6,7},{7,8},{8,9},{9,10},{10,1... | collective-permute-start | bytes 1572872 | tf_op jit(solution)/shard_map/ppermute | solution.py:14
  33.4 0.0 collective-permute-done.4.east_ref
  33.4 0.0 copy-start.1
  33.4 7.3 %collective-permute-start.5 = (bf16[4,128,512]{2,1,0:T(8,128)(2,1)S(1)}, bf16[4,128,512]{2,1,0:T(8,128)(2,1)S(1)}, u32[]{:S(2)}, u32[]{:S(2)}) collective-permute-start(bf16[4,128,512]{2,1,0:T(8,128)(2,1)S(1)} %collective-permute-done.4.east_ref), channel_id=1, source_target_pairs={{0,31},{1,0},{2,1},{3,2},{4,3},{5,4},{6,5},{7,6},{8,7},{9,8},{10,9... | collective-permute-start | bytes 1572872 | tf_op jit(solution)/shard_map/ppermute | solution.py:14
  40.7 0.1 pad_add_fusion
  40.8 0.3 fusion.2
  41.1 0.7 reshape_reshape.3.counts_ref
  41.8 0.0 copy-start.4
  41.8 5.8 %collective-permute-done.3.far_west_ref = bf16[4,128,512]{2,1,0:T(8,128)(2,1)S(1)} collective-permute-done((bf16[4,128,512]{2,1,0:T(8,128)(2,1)S(1)}, bf16[4,128,512]{2,1,0:T(8,128)(2,1)S(1)}, u32[]{:S(2)}, u32[]{:S(2)}) %collective-permute-start.3) | collective-permute-done | bytes 524320 | tf_op jit(solution)/shard_map/ppermute | solution.py:14
  47.6 0.0 copy-start.2
  47.6 1.8 %collective-permute-done.5.far_east_ref = bf16[4,128,512]{2,1,0:T(8,128)(2,1)S(1)} collective-permute-done((bf16[4,128,512]{2,1,0:T(8,128)(2,1)S(1)}, bf16[4,128,512]{2,1,0:T(8,128)(2,1)S(1)}, u32[]{:S(2)}, u32[]{:S(2)}) %collective-permute-start.5) | collective-permute-done | bytes 524320 | tf_op jit(solution)/shard_map/ppermute | solution.py:14
  49.4 0.0 copy-done
  49.4 0.0 copy-done.1
  49.4 0.0 copy-done.2
  49.4 0.0 copy-start.3
  49.4 0.8 copy-done.3
  50.2 15.5 %shard_map.65 = (bf16[2,128,512]{2,1,0:T(8,128)(2,1)}, bf16[2,128,512]{2,1,0:T(8,128)(2,1)}, f32[4,128,512]{2,1,0:T(8,128)}) custom-call(f32[288]{0:T(512)} %reshape_reshape.3.counts_ref, bf16[4,9,128,640]{3,2,1,0:T(8,128)(2,1)} %shard_map.64.band_ref, bf16[4,128,512]{2,1,0:T(8,128)(2,1)} %copy-done.2, bf16[4,128,512]{2,1,0:T(8,128)(2,1)} %copy-done, ...), custom_call_target="tpu_custom_call" | custom-call | tf_op jit(solution)/shard_map/pallas_call | solution.py:128
  65.7 8.5 %collective-permute-start.6 = (bf16[2,128,512]{2,1,0:T(8,128)(2,1)}, bf16[2,128,512]{2,1,0:T(8,128)(2,1)S(1)}, u32[]{:S(2)}, u32[]{:S(2)}) collective-permute-start(bf16[2,128,512]{2,1,0:T(8,128)(2,1)} %get-tuple-element.9), channel_id=1, source_target_pairs={{0,32},{32,64},{64,96},{96,128},{128,160},{160,192},{192,224},{224... | collective-permute-start | bytes 786440 | tf_op jit(solution)/shard_map/ppermute | solution.py:178
  74.2 1.9 %collective-permute-start.7 = (bf16[2,128,512]{2,1,0:T(8,128)(2,1)}, bf16[2,128,512]{2,1,0:T(8,128)(2,1)S(1)}, u32[]{:S(2)}, u32[]{:S(2)}) collective-permute-start(bf16[2,128,512]{2,1,0:T(8,128)(2,1)} %get-tuple-element.10), channel_id=1, source_target_pairs={{32,0},{64,32},{96,64},{128,96},{160,128},{192,160},{224,192},{256... | collective-permute-start | bytes 786440 | tf_op jit(solution)/shard_map/ppermute | solution.py:177
  76.2 1.7 %collective-permute-done.6 = bf16[2,128,512]{2,1,0:T(8,128)(2,1)S(1)} collective-permute-done((bf16[2,128,512]{2,1,0:T(8,128)(2,1)}, bf16[2,128,512]{2,1,0:T(8,128)(2,1)S(1)}, u32[]{:S(2)}, u32[]{:S(2)}) %collective-permute-start.6) | collective-permute-done | bytes 262176 | tf_op jit(solution)/shard_map/ppermute | solution.py:178
  77.8 10.3 %collective-permute-done.7 = bf16[2,128,512]{2,1,0:T(8,128)(2,1)S(1)} collective-permute-done((bf16[2,128,512]{2,1,0:T(8,128)(2,1)}, bf16[2,128,512]{2,1,0:T(8,128)(2,1)S(1)}, u32[]{:S(2)}, u32[]{:S(2)}) %collective-permute-start.7) | collective-permute-done | bytes 262176 | tf_op jit(solution)/shard_map/ppermute | solution.py:177
  88.2 0.0 copy-done.4
  88.2 2.2 %multiply_convert_fusion = bf16[4,128,512]{2,1,0:T(8,128)(2,1)} fusion(f32[4,128,512]{2,1,0:T(8,128)} %get-tuple-element.8, f32[4]{0:T(128)S(1)} %copy-done.4, bf16[2,128,512]{2,1,0:T(8,128)(2,1)S(1)} %collective-permute-done.7, bf16[2,128,512]{2,1,0:T(8,128)(2,1)S(1)} %collective-permute-done.6), kind=kLoop, calls=%fused_computation | loop fusion | flops 1572864 | bytes 2097168 | tf_op jit(solution)/shard_map/convert_element_type | solution.py:181
  (5 shorter events, 0.0 us)
Async XLA Ops:
  0.0 31.4 %collective-permute-start = (s32[96,3]{0,1:T(4,128)}, s32[96,3]{0,1:T(4,128)S(1)}, u32[]{:S(2)}, u32[]{:S(2)}) collective-permute-start(s32[96,3]{0,1:T(4,128)} %param.10), channel_id=1, source_target_pairs={{0,32},{32,64},{64,96},{96,128},{128,160},{160,192},{192,224},{224... | collective-permute-start | bytes 3464 | tf_op jit(solution)/shard_map/ppermute | solution.py:22
  11.1 20.3 %collective-permute-start.1 = (s32[96,3]{0,1:T(4,128)}, s32[96,3]{0,1:T(4,128)S(1)}, u32[]{:S(2)}, u32[]{:S(2)}) collective-permute-start(s32[96,3]{0,1:T(4,128)} %param.10), channel_id=1, source_target_pairs={{32,0},{64,32},{96,64},{128,96},{160,128},{192,160},{224,192},{256... | collective-permute-start | bytes 3464 | tf_op jit(solution)/shard_map/ppermute | solution.py:25
  13.0 18.4 %collective-permute-start.2 = (bf16[4,128,512]{2,1,0:T(8,128)(2,1)}, bf16[4,128,512]{2,1,0:T(8,128)(2,1)S(1)}, u32[]{:S(2)}, u32[]{:S(2)}) collective-permute-start(bf16[4,128,512]{2,1,0:T(8,128)(2,1)} %local_ref.1), channel_id=1, source_target_pairs={{0,1},{1,2},{2,3},{3,4},{4,5},{5,6},{6,7},{7,8},{8,9},{9,10},{10,1... | collective-permute-start | bytes 1572872 | tf_op jit(solution)/shard_map/ppermute | solution.py:14
  16.3 17.2 %collective-permute-start.4 = (bf16[4,128,512]{2,1,0:T(8,128)(2,1)}, bf16[4,128,512]{2,1,0:T(8,128)(2,1)S(1)}, u32[]{:S(2)}, u32[]{:S(2)}) collective-permute-start(bf16[4,128,512]{2,1,0:T(8,128)(2,1)} %local_ref.1), channel_id=1, source_target_pairs={{0,31},{1,0},{2,1},{3,2},{4,3},{5,4},{6,5},{7,6},{8,7},{9,8},{10,9... | collective-permute-start | bytes 1572872 | tf_op jit(solution)/shard_map/ppermute | solution.py:14
  31.5 17.9 %copy-start = (bf16[4,128,512]{2,1,0:T(8,128)(2,1)}, bf16[4,128,512]{2,1,0:T(8,128)(2,1)S(1)}, u32[]{:S(2)}) copy-start(bf16[4,128,512]{2,1,0:T(8,128)(2,1)S(1)} %collective-permute-done.2.west_ref) | copy-start | bytes 1572868
  31.5 16.1 %collective-permute-start.3 = (bf16[4,128,512]{2,1,0:T(8,128)(2,1)S(1)}, bf16[4,128,512]{2,1,0:T(8,128)(2,1)S(1)}, u32[]{:S(2)}, u32[]{:S(2)}) collective-permute-start(bf16[4,128,512]{2,1,0:T(8,128)(2,1)S(1)} %collective-permute-done.2.west_ref), channel_id=1, source_target_pairs={{0,1},{1,2},{2,3},{3,4},{4,5},{5,6},{6,7},{7,8},{8,9},{9,10},{10,1... | collective-permute-start | bytes 1572872 | tf_op jit(solution)/shard_map/ppermute | solution.py:14
  33.4 15.9 %copy-start.1 = (bf16[4,128,512]{2,1,0:T(8,128)(2,1)}, bf16[4,128,512]{2,1,0:T(8,128)(2,1)S(1)}, u32[]{:S(2)}) copy-start(bf16[4,128,512]{2,1,0:T(8,128)(2,1)S(1)} %collective-permute-done.4.east_ref) | copy-start | bytes 1572868
  33.4 15.9 %collective-permute-start.5 = (bf16[4,128,512]{2,1,0:T(8,128)(2,1)S(1)}, bf16[4,128,512]{2,1,0:T(8,128)(2,1)S(1)}, u32[]{:S(2)}, u32[]{:S(2)}) collective-permute-start(bf16[4,128,512]{2,1,0:T(8,128)(2,1)S(1)} %collective-permute-done.4.east_ref), channel_id=1, source_target_pairs={{0,31},{1,0},{2,1},{3,2},{4,3},{5,4},{6,5},{7,6},{8,7},{9,8},{10,9... | collective-permute-start | bytes 1572872 | tf_op jit(solution)/shard_map/ppermute | solution.py:14
  41.8 46.3 %copy-start.4 = (f32[4]{0:T(128)S(1)}, f32[4]{0:T(128)}, u32[]{:S(2)}) copy-start(f32[4]{0:T(128)} %param.9) | copy-start | bytes 52
  47.6 1.8 %copy-start.2 = (bf16[4,128,512]{2,1,0:T(8,128)(2,1)}, bf16[4,128,512]{2,1,0:T(8,128)(2,1)S(1)}, u32[]{:S(2)}) copy-start(bf16[4,128,512]{2,1,0:T(8,128)(2,1)S(1)} %collective-permute-done.3.far_west_ref) | copy-start | bytes 1572868
  49.4 0.9 copy-start.3
  65.7 12.1 %collective-permute-start.6 = (bf16[2,128,512]{2,1,0:T(8,128)(2,1)}, bf16[2,128,512]{2,1,0:T(8,128)(2,1)S(1)}, u32[]{:S(2)}, u32[]{:S(2)}) collective-permute-start(bf16[2,128,512]{2,1,0:T(8,128)(2,1)} %get-tuple-element.9), channel_id=1, source_target_pairs={{0,32},{32,64},{64,96},{96,128},{128,160},{160,192},{192,224},{224... | collective-permute-start | bytes 786440 | tf_op jit(solution)/shard_map/ppermute | solution.py:178
  74.2 13.9 %collective-permute-start.7 = (bf16[2,128,512]{2,1,0:T(8,128)(2,1)}, bf16[2,128,512]{2,1,0:T(8,128)(2,1)S(1)}, u32[]{:S(2)}, u32[]{:S(2)}) collective-permute-start(bf16[2,128,512]{2,1,0:T(8,128)(2,1)} %get-tuple-element.10), channel_id=1, source_target_pairs={{32,0},{64,32},{96,64},{128,96},{160,128},{192,160},{224,192},{256... | collective-permute-start | bytes 786440 | tf_op jit(solution)/shard_map/ppermute | solution.py:177

commit v8 on v7

--- a/solution.py
+++ b/solution.py
@@ -119,11 +119,10 @@
         lower_ref[...] = total_ref[RIM + input_rows :].astype(lower_ref.dtype)
 
 
-def block_partials(counts, short_taps, parts, mix_weight):
+def block_partials(counts, band, parts, mix_weight):
     rows, cols, channels = parts[0].shape
-    kinds = short_taps.shape[1]
+    kinds = band.shape[1]
     window = cols * len(parts)
-    band = band_matrix(short_taps, cols, window)
     whole = lambda shape: pl.BlockSpec(shape, lambda k: (0,) * len(shape))
     return pl.pallas_call(
         _block_kernel,
@@ -155,6 +154,9 @@
     kinds = lon_taps.shape[1]
     far_west, west, east, far_east = longitude_halo(field)
     short_taps = masked_taps(lon_taps, lon_width)
+    cols = field.shape[1]
+    band = band_matrix(short_taps, cols, cols * (2 * SPAN + 1))
+    band, support = lax.optimization_barrier((band, support))
     entries = support.shape[0]
     lists = with_halo(support, (("lat", 0),), entries)
     above = lists[:entries]
@@ -169,7 +171,7 @@
     )
     counts = coupling(out_rows, in_rows, basis, valid, rows + 2 * RIM, rows, kinds)
     upper, lower, inner = block_partials(
-        counts, short_taps, (far_west, west, field, east, far_east), mix_weight
+        counts, band, (far_west, west, field, east, far_east), mix_weight
     )
     count = lax.axis_size("lat")
     forward = [(i, i + 1) for i in range(count - 1)]

time: 91 us -> 92.1 us (1.012)
  starting transfers between devices: 42.4 us -> 45 us
  other arithmetic: 6.24 us -> 4.77 us
    ppermute x4, starting transfers between devices: 18.9 us -> 21.8 us  [shifted(): lax.ppermute(value, axis, [(i, (i + by) % length) for i in range(length)])]
    ppermute x1, starting transfers between devices: 11.1 us -> 8.72 us  [with_halo(): lax.ppermute(lax.slice_in_dim(block, block.shape[dim] - width, None, axis...]
    ppermute x1, starting transfers between devices: 8.52 us -> 9.72 us  [on_device(): from_above = lax.ppermute(lower, 'lat', forward).astype(jnp.float32)]
    ppermute x1, starting transfers between devices: 1.92 us -> 2.85 us  [with_halo(): lax.ppermute(lax.slice_in_dim(block, 0, width, axis=dim), axis, backward)]
  transfers between devices with their start and end apart: 8 -> 8, of which waited for: 4 -> 5; matrix products, arithmetic and copies ran while one was open for 6% -> 4% of each run, Pallas kernels for 5% -> 5%
where the time goes in v8:
time: 92.1 us; the launch traced here: 91.5 us
  starting transfers between devices  45 us (49%)
  Pallas kernels  20.2 us (22%)
  waiting for transfers between devices  19.5 us (21%)
  other arithmetic  4.77 us (5%)
  local copies, waits for them, and re-layouts  1.57 us (2%)
    ppermute x4, starting transfers between devices, shifted(): lax.ppermute(value, axis, [(i, (i + by) % length) for i in range(length)])  21.8 us
    pallas_call x1, Pallas kernels, block_partials(): pl.pallas_call(_block_kernel, grid=(kinds,), in_specs=[pl.BlockSpec(memor...  15.5 us
    ppermute x1, waiting for transfers between devices, on_device(): from_below = lax.ppermute(upper, 'lat', backward).astype(jnp.float32)  10.3 us
    ppermute x1, starting transfers between devices, on_device(): from_above = lax.ppermute(lower, 'lat', forward).astype(jnp.float32)  9.72 us
    ppermute x1, starting transfers between devices, with_halo(): lax.ppermute(lax.slice_in_dim(block, block.shape[dim] - width, None, axis...  8.72 us
    ppermute x4, waiting for transfers between devices, shifted(): lax.ppermute(value, axis, [(i, (i + by) % length) for i in range(length)])  6.85 us
    pallas_call x1, Pallas kernels, band_matrix(): pl.pallas_call(_toeplitz_kernel, grid=(rows,), in_specs=[pl.BlockSpec((1,...  4.77 us
    ppermute x1, starting transfers between devices, with_halo(): lax.ppermute(lax.slice_in_dim(block, 0, width, axis=dim), axis, backward)  2.85 us
  transfers between devices with their start and end apart: 8, of which 5 were waited for; matrix products, arithmetic and copies ran while one was open for 4% of the time, Pallas kernels for 5%

profile of v8, /device:TPU:7, one launch (start us, length us, event | category | flops | bytes accessed | tf_op | source)
XLA Modules:
  0.0 91.5 jit_solution(5436914457183691978)
XLA Ops:
  0.0 0.0 copy-start.4
  0.0 3.3 %collective-permute-start.2 = (bf16[4,128,512]{2,1,0:T(8,128)(2,1)}, bf16[4,128,512]{2,1,0:T(8,128)(2,1)S(1)}, u32[]{:S(2)}, u32[]{:S(2)}) collective-permute-start(bf16[4,128,512]{2,1,0:T(8,128)(2,1)} %local_ref.1), channel_id=1, source_target_pairs={{0,1},{1,2},{2,3},{3,4},{4,5},{5,6},{6,7},{7,8},{8,9},{9,10},{10,1... | collective-permute-start | bytes 1572872 | tf_op jit(solution)/shard_map/ppermute | solution.py:14
  3.3 9.2 %collective-permute-start.4 = (bf16[4,128,512]{2,1,0:T(8,128)(2,1)}, bf16[4,128,512]{2,1,0:T(8,128)(2,1)S(1)}, u32[]{:S(2)}, u32[]{:S(2)}) collective-permute-start(bf16[4,128,512]{2,1,0:T(8,128)(2,1)} %local_ref.1), channel_id=1, source_target_pairs={{0,31},{1,0},{2,1},{3,2},{4,3},{5,4},{6,5},{7,6},{8,7},{9,8},{10,9... | collective-permute-start | bytes 1572872 | tf_op jit(solution)/shard_map/ppermute | solution.py:14
  12.6 0.7 broadcast_compare_fusion
  13.3 0.9 fusion
  14.2 0.7 pad_convert_fusion.taps_ref
  14.9 4.8 %shard_map.64.band_ref = bf16[4,9,128,640]{3,2,1,0:T(8,128)(2,1)} custom-call(f32[4,9,640]{2,1,0:T(8,128)} %pad_convert_fusion.taps_ref), custom_call_target="tpu_custom_call" | custom-call | tf_op jit(solution)/shard_map/pallas_call | solution.py:73
  19.7 0.0 copy-done.4
  19.7 2.9 %collective-permute-start.1 = (s32[96,3]{0,1:T(4,128)S(1)}, s32[96,3]{0,1:T(4,128)S(1)}, u32[]{:S(2)}, u32[]{:S(2)}) collective-permute-start(s32[96,3]{0,1:T(4,128)S(1)} %copy-done.4), channel_id=1, source_target_pairs={{32,0},{64,32},{96,64},{128,96},{160,128},{192,160},{224,192},{256... | collective-permute-start | bytes 3464 | tf_op jit(solution)/shard_map/ppermute | solution.py:25
  22.6 8.7 %collective-permute-start = (s32[96,3]{0,1:T(4,128)S(1)}, s32[96,3]{0,1:T(4,128)S(1)}, u32[]{:S(2)}, u32[]{:S(2)}) collective-permute-start(s32[96,3]{0,1:T(4,128)S(1)} %copy-done.4), channel_id=1, source_target_pairs={{0,32},{32,64},{64,96},{96,128},{128,160},{160,192},{192,224},{224... | collective-permute-start | bytes 3464 | tf_op jit(solution)/shard_map/ppermute | solution.py:22
  31.3 0.0 collective-permute-done.1
  31.3 0.7 collective-permute-done
  32.0 0.1 pad_add_fusion.1
  32.1 0.0 collective-permute-done.2.west_ref
  32.1 0.0 copy-start
  32.1 1.9 %collective-permute-start.3 = (bf16[4,128,512]{2,1,0:T(8,128)(2,1)S(1)}, bf16[4,128,512]{2,1,0:T(8,128)(2,1)S(1)}, u32[]{:S(2)}, u32[]{:S(2)}) collective-permute-start(bf16[4,128,512]{2,1,0:T(8,128)(2,1)S(1)} %collective-permute-done.2.west_ref), channel_id=1, source_target_pairs={{0,1},{1,2},{2,3},{3,4},{4,5},{5,6},{6,7},{7,8},{8,9},{9,10},{10,1... | collective-permute-start | bytes 1572872 | tf_op jit(solution)/shard_map/ppermute | solution.py:14
  34.0 0.0 collective-permute-done.4.east_ref
  34.0 0.0 copy-start.1
  34.0 7.3 %collective-permute-start.5 = (bf16[4,128,512]{2,1,0:T(8,128)(2,1)S(1)}, bf16[4,128,512]{2,1,0:T(8,128)(2,1)S(1)}, u32[]{:S(2)}, u32[]{:S(2)}) collective-permute-start(bf16[4,128,512]{2,1,0:T(8,128)(2,1)S(1)} %collective-permute-done.4.east_ref), channel_id=1, source_target_pairs={{0,31},{1,0},{2,1},{3,2},{4,3},{5,4},{6,5},{7,6},{8,7},{9,8},{10,9... | collective-permute-start | bytes 1572872 | tf_op jit(solution)/shard_map/ppermute | solution.py:14
  41.3 0.1 pad_add_fusion
  41.4 0.3 fusion.2
  41.7 0.7 reshape_reshape.3.counts_ref
  42.4 0.0 copy-start.5
  42.4 5.1 %collective-permute-done.3.far_west_ref = bf16[4,128,512]{2,1,0:T(8,128)(2,1)S(1)} collective-permute-done((bf16[4,128,512]{2,1,0:T(8,128)(2,1)S(1)}, bf16[4,128,512]{2,1,0:T(8,128)(2,1)S(1)}, u32[]{:S(2)}, u32[]{:S(2)}) %collective-permute-start.3) | collective-permute-done | bytes 524320 | tf_op jit(solution)/shard_map/ppermute | solution.py:14
  47.5 0.0 copy-start.2
  47.5 1.8 %collective-permute-done.5.far_east_ref = bf16[4,128,512]{2,1,0:T(8,128)(2,1)S(1)} collective-permute-done((bf16[4,128,512]{2,1,0:T(8,128)(2,1)S(1)}, bf16[4,128,512]{2,1,0:T(8,128)(2,1)S(1)}, u32[]{:S(2)}, u32[]{:S(2)}) %collective-permute-start.5) | collective-permute-done | bytes 524320 | tf_op jit(solution)/shard_map/ppermute | solution.py:14
  49.3 0.0 copy-done
  49.3 0.0 copy-done.1
  49.3 0.0 copy-done.2
  49.3 0.0 copy-start.3
  49.3 0.9 copy-done.3
  50.1 15.5 %shard_map.65 = (bf16[2,128,512]{2,1,0:T(8,128)(2,1)}, bf16[2,128,512]{2,1,0:T(8,128)(2,1)}, f32[4,128,512]{2,1,0:T(8,128)}) custom-call(f32[288]{0:T(512)} %reshape_reshape.3.counts_ref, bf16[4,9,128,640]{3,2,1,0:T(8,128)(2,1)} %shard_map.64.band_ref, bf16[4,128,512]{2,1,0:T(8,128)(2,1)} %copy-done.2, bf16[4,128,512]{2,1,0:T(8,128)(2,1)} %copy-done, ...), custom_call_target="tpu_custom_call" | custom-call | tf_op jit(solution)/shard_map/pallas_call | solution.py:127
  65.6 9.7 %collective-permute-start.6 = (bf16[2,128,512]{2,1,0:T(8,128)(2,1)}, bf16[2,128,512]{2,1,0:T(8,128)(2,1)S(1)}, u32[]{:S(2)}, u32[]{:S(2)}) collective-permute-start(bf16[2,128,512]{2,1,0:T(8,128)(2,1)} %get-tuple-element.13), channel_id=1, source_target_pairs={{0,32},{32,64},{64,96},{96,128},{128,160},{160,192},{192,224},{224... | collective-permute-start | bytes 786440 | tf_op jit(solution)/shard_map/ppermute | solution.py:180
  75.4 1.9 %collective-permute-start.7 = (bf16[2,128,512]{2,1,0:T(8,128)(2,1)}, bf16[2,128,512]{2,1,0:T(8,128)(2,1)S(1)}, u32[]{:S(2)}, u32[]{:S(2)}) collective-permute-start(bf16[2,128,512]{2,1,0:T(8,128)(2,1)} %get-tuple-element.14), channel_id=1, source_target_pairs={{32,0},{64,32},{96,64},{128,96},{160,128},{192,160},{224,192},{256... | collective-permute-start | bytes 786440 | tf_op jit(solution)/shard_map/ppermute | solution.py:179
  77.3 1.7 %collective-permute-done.6 = bf16[2,128,512]{2,1,0:T(8,128)(2,1)S(1)} collective-permute-done((bf16[2,128,512]{2,1,0:T(8,128)(2,1)}, bf16[2,128,512]{2,1,0:T(8,128)(2,1)S(1)}, u32[]{:S(2)}, u32[]{:S(2)}) %collective-permute-start.6) | collective-permute-done | bytes 262176 | tf_op jit(solution)/shard_map/ppermute | solution.py:180
  79.0 10.3 %collective-permute-done.7 = bf16[2,128,512]{2,1,0:T(8,128)(2,1)S(1)} collective-permute-done((bf16[2,128,512]{2,1,0:T(8,128)(2,1)}, bf16[2,128,512]{2,1,0:T(8,128)(2,1)S(1)}, u32[]{:S(2)}, u32[]{:S(2)}) %collective-permute-start.7) | collective-permute-done | bytes 262176 | tf_op jit(solution)/shard_map/ppermute | solution.py:179
  89.3 0.0 copy-done.5
  89.3 2.2 %multiply_convert_fusion = bf16[4,128,512]{2,1,0:T(8,128)(2,1)} fusion(f32[4,128,512]{2,1,0:T(8,128)} %get-tuple-element.12, f32[4]{0:T(128)S(1)} %copy-done.5, bf16[2,128,512]{2,1,0:T(8,128)(2,1)S(1)} %collective-permute-done.7, bf16[2,128,512]{2,1,0:T(8,128)(2,1)S(1)} %collective-permute-done.6), kind=kLoop, calls=%fused_computation | loop fusion | flops 1572864 | bytes 2097168 | tf_op jit(solution)/shard_map/convert_element_type | solution.py:183
  (7 shorter events, 0.0 us)
Async XLA Ops:
  0.0 19.7 %copy-start.4 = (s32[96,3]{0,1:T(4,128)S(1)}, s32[96,3]{0,1:T(4,128)}, u32[]{:S(2)}) copy-start(s32[96,3]{0,1:T(4,128)} %param.10) | copy-start | bytes 3460
  0.0 32.1 %collective-permute-start.2 = (bf16[4,128,512]{2,1,0:T(8,128)(2,1)}, bf16[4,128,512]{2,1,0:T(8,128)(2,1)S(1)}, u32[]{:S(2)}, u32[]{:S(2)}) collective-permute-start(bf16[4,128,512]{2,1,0:T(8,128)(2,1)} %local_ref.1), channel_id=1, source_target_pairs={{0,1},{1,2},{2,3},{3,4},{4,5},{5,6},{6,7},{7,8},{8,9},{9,10},{10,1... | collective-permute-start | bytes 1572872 | tf_op jit(solution)/shard_map/ppermute | solution.py:14
  3.3 30.7 %collective-permute-start.4 = (bf16[4,128,512]{2,1,0:T(8,128)(2,1)}, bf16[4,128,512]{2,1,0:T(8,128)(2,1)S(1)}, u32[]{:S(2)}, u32[]{:S(2)}) collective-permute-start(bf16[4,128,512]{2,1,0:T(8,128)(2,1)} %local_ref.1), channel_id=1, source_target_pairs={{0,31},{1,0},{2,1},{3,2},{4,3},{5,4},{6,5},{7,6},{8,7},{9,8},{10,9... | collective-permute-start | bytes 1572872 | tf_op jit(solution)/shard_map/ppermute | solution.py:14
  19.7 11.6 %collective-permute-start.1 = (s32[96,3]{0,1:T(4,128)S(1)}, s32[96,3]{0,1:T(4,128)S(1)}, u32[]{:S(2)}, u32[]{:S(2)}) collective-permute-start(s32[96,3]{0,1:T(4,128)S(1)} %copy-done.4), channel_id=1, source_target_pairs={{32,0},{64,32},{96,64},{128,96},{160,128},{192,160},{224,192},{256... | collective-permute-start | bytes 3464 | tf_op jit(solution)/shard_map/ppermute | solution.py:25
  22.6 9.4 %collective-permute-start = (s32[96,3]{0,1:T(4,128)S(1)}, s32[96,3]{0,1:T(4,128)S(1)}, u32[]{:S(2)}, u32[]{:S(2)}) collective-permute-start(s32[96,3]{0,1:T(4,128)S(1)} %copy-done.4), channel_id=1, source_target_pairs={{0,32},{32,64},{64,96},{96,128},{128,160},{160,192},{192,224},{224... | collective-permute-start | bytes 3464 | tf_op jit(solution)/shard_map/ppermute | solution.py:22
  32.1 17.2 %copy-start = (bf16[4,128,512]{2,1,0:T(8,128)(2,1)}, bf16[4,128,512]{2,1,0:T(8,128)(2,1)S(1)}, u32[]{:S(2)}) copy-start(bf16[4,128,512]{2,1,0:T(8,128)(2,1)S(1)} %collective-permute-done.2.west_ref) | copy-start | bytes 1572868
  32.1 15.4 %collective-permute-start.3 = (bf16[4,128,512]{2,1,0:T(8,128)(2,1)S(1)}, bf16[4,128,512]{2,1,0:T(8,128)(2,1)S(1)}, u32[]{:S(2)}, u32[]{:S(2)}) collective-permute-start(bf16[4,128,512]{2,1,0:T(8,128)(2,1)S(1)} %collective-permute-done.2.west_ref), channel_id=1, source_target_pairs={{0,1},{1,2},{2,3},{3,4},{4,5},{5,6},{6,7},{7,8},{8,9},{9,10},{10,1... | collective-permute-start | bytes 1572872 | tf_op jit(solution)/shard_map/ppermute | solution.py:14
  34.0 15.2 %copy-start.1 = (bf16[4,128,512]{2,1,0:T(8,128)(2,1)}, bf16[4,128,512]{2,1,0:T(8,128)(2,1)S(1)}, u32[]{:S(2)}) copy-start(bf16[4,128,512]{2,1,0:T(8,128)(2,1)S(1)} %collective-permute-done.4.east_ref) | copy-start | bytes 1572868
  34.0 15.2 %collective-permute-start.5 = (bf16[4,128,512]{2,1,0:T(8,128)(2,1)S(1)}, bf16[4,128,512]{2,1,0:T(8,128)(2,1)S(1)}, u32[]{:S(2)}, u32[]{:S(2)}) collective-permute-start(bf16[4,128,512]{2,1,0:T(8,128)(2,1)S(1)} %collective-permute-done.4.east_ref), channel_id=1, source_target_pairs={{0,31},{1,0},{2,1},{3,2},{4,3},{5,4},{6,5},{7,6},{8,7},{9,8},{10,9... | collective-permute-start | bytes 1572872 | tf_op jit(solution)/shard_map/ppermute | solution.py:14
  42.4 46.9 %copy-start.5 = (f32[4]{0:T(128)S(1)}, f32[4]{0:T(128)}, u32[]{:S(2)}) copy-start(f32[4]{0:T(128)} %param.9) | copy-start | bytes 52
  47.5 1.8 %copy-start.2 = (bf16[4,128,512]{2,1,0:T(8,128)(2,1)}, bf16[4,128,512]{2,1,0:T(8,128)(2,1)S(1)}, u32[]{:S(2)}) copy-start(bf16[4,128,512]{2,1,0:T(8,128)(2,1)S(1)} %collective-permute-done.3.far_west_ref) | copy-start | bytes 1572868
  49.3 0.9 copy-start.3
  65.6 13.3 %collective-permute-start.6 = (bf16[2,128,512]{2,1,0:T(8,128)(2,1)}, bf16[2,128,512]{2,1,0:T(8,128)(2,1)S(1)}, u32[]{:S(2)}, u32[]{:S(2)}) collective-permute-start(bf16[2,128,512]{2,1,0:T(8,128)(2,1)} %get-tuple-element.13), channel_id=1, source_target_pairs={{0,32},{32,64},{64,96},{96,128},{128,160},{160,192},{192,224},{224... | collective-permute-start | bytes 786440 | tf_op jit(solution)/shard_map/ppermute | solution.py:180
  75.4 13.9 %collective-permute-start.7 = (bf16[2,128,512]{2,1,0:T(8,128)(2,1)}, bf16[2,128,512]{2,1,0:T(8,128)(2,1)S(1)}, u32[]{:S(2)}, u32[]{:S(2)}) collective-permute-start(bf16[2,128,512]{2,1,0:T(8,128)(2,1)} %get-tuple-element.14), channel_id=1, source_target_pairs={{32,0},{64,32},{96,64},{128,96},{160,128},{192,160},{224,192},{256... | collective-permute-start | bytes 786440 | tf_op jit(solution)/shard_map/ppermute | solution.py:179

commit v9 on v7

--- a/solution.py
+++ b/solution.py
@@ -91,7 +91,6 @@
     def _():
         for index, part in enumerate(parts):
             window_ref[:, index * cols : (index + 1) * cols, :] = part[...]
-        total_ref[...] = jnp.zeros_like(total_ref)
 
     for in_row in range(input_rows):
         response = jnp.dot(band_ref[in_row, 0], window_ref[in_row], preferred_element_type=jnp.float32)
@@ -99,18 +98,23 @@
     mixed_ref[...] = jnp.dot(response_ref[...], weight_ref[0], preferred_element_type=jnp.float32)
     chunk = 16
 
-    def body(step, carry):
-        start = pl.multiple_of(step * chunk, chunk)
-        pieces = [mixed_ref[pl.ds(in_row * cols + start, chunk), :] for in_row in range(input_rows)]
-        for out_row in range(output_rows):
-            total = total_ref[out_row, pl.ds(start, chunk), :]
-            for in_row in range(max(0, out_row - 2 * RIM), min(input_rows, out_row + 1)):
-                scale = counts_ref[(out_row * kinds + kind) * input_rows + in_row]
-                total = total + scale * pieces[in_row]
-            total_ref[out_row, pl.ds(start, chunk), :] = total
-        return carry
-
-    lax.fori_loop(0, cols // chunk, body, 0)
+    def accumulate(first):
+        def body(step, carry):
+            start = pl.multiple_of(step * chunk, chunk)
+            pieces = [mixed_ref[pl.ds(in_row * cols + start, chunk), :] for in_row in range(input_rows)]
+            for out_row in range(output_rows):
+                total = None if first else total_ref[out_row, pl.ds(start, chunk), :]
+                for in_row in range(max(0, out_row - 2 * RIM), min(input_rows, out_row + 1)):
+                    scale = counts_ref[(out_row * kinds + kind) * input_rows + in_row]
+                    term = scale * pieces[in_row]
+                    total = term if total is None else total + term
+                total_ref[out_row, pl.ds(start, chunk), :] = total
+            return carry
+
+        lax.fori_loop(0, cols // chunk, body, 0)
+
+    pl.when(kind == 0)(lambda: accumulate(True))
+    pl.when(kind > 0)(lambda: accumulate(False))
 
     @pl.when(kind == kinds - 1)
     def _():

time: 91 us -> 90.8 us (level)
  no operation moved by 1% of the time
where the time goes in v9:
time: 90.8 us; the launch traced here: 90.2 us
  starting transfers between devices  42.4 us (47%)
  Pallas kernels  20 us (22%)
  waiting for transfers between devices  19.5 us (21%)
  other arithmetic  6.24 us (7%)
  local copies, waits for them, and re-layouts  1.55 us (2%)
    ppermute x4, starting transfers between devices, shifted(): lax.ppermute(value, axis, [(i, (i + by) % length) for i in range(length)])  18.9 us
    pallas_call x1, Pallas kernels, block_partials(): pl.pallas_call(_block_kernel, grid=(kinds,), in_specs=[pl.BlockSpec(memor...  15.3 us
    ppermute x1, starting transfers between devices, with_halo(): lax.ppermute(lax.slice_in_dim(block, block.shape[dim] - width, None, axis...  11.1 us
    ppermute x1, waiting for transfers between devices, on_device(): from_below = lax.ppermute(upper, 'lat', backward).astype(jnp.float32)  10.3 us
    ppermute x1, starting transfers between devices, on_device(): from_above = lax.ppermute(lower, 'lat', forward).astype(jnp.float32)  8.52 us
    ppermute x4, waiting for transfers between devices, shifted(): lax.ppermute(value, axis, [(i, (i + by) % length) for i in range(length)])  7.55 us
    pallas_call x1, Pallas kernels, band_matrix(): pl.pallas_call(_toeplitz_kernel, grid=(rows,), in_specs=[pl.BlockSpec((1,...  4.74 us
    convert_element_type x1, other arithmetic, on_device(): return (inner * row_scale[:, None, None]).astype(jnp.bfloat16)  2.25 us
  transfers between devices with their start and end apart: 8, of which 4 were waited for; matrix products, arithmetic and copies ran while one was open for 6% of the time, Pallas kernels for 5%

profile of v9, /device:TPU:7, one launch (start us, length us, event | category | flops | bytes accessed | tf_op | source)
XLA Modules:
  0.0 90.2 jit_solution(16449343232219857772)
XLA Ops:
  0.0 11.1 %collective-permute-start = (s32[96,3]{0,1:T(4,128)}, s32[96,3]{0,1:T(4,128)S(1)}, u32[]{:S(2)}, u32[]{:S(2)}) collective-permute-start(s32[96,3]{0,1:T(4,128)} %param.10), channel_id=1, source_target_pairs={{0,32},{32,64},{64,96},{96,128},{128,160},{160,192},{192,224},{224... | collective-permute-start | bytes 3464 | tf_op jit(solution)/shard_map/ppermute | solution.py:22
  11.1 1.9 %collective-permute-start.1 = (s32[96,3]{0,1:T(4,128)}, s32[96,3]{0,1:T(4,128)S(1)}, u32[]{:S(2)}, u32[]{:S(2)}) collective-permute-start(s32[96,3]{0,1:T(4,128)} %param.10), channel_id=1, source_target_pairs={{32,0},{64,32},{96,64},{128,96},{160,128},{192,160},{224,192},{256... | collective-permute-start | bytes 3464 | tf_op jit(solution)/shard_map/ppermute | solution.py:25
  13.0 3.2 %collective-permute-start.2 = (bf16[4,128,512]{2,1,0:T(8,128)(2,1)}, bf16[4,128,512]{2,1,0:T(8,128)(2,1)S(1)}, u32[]{:S(2)}, u32[]{:S(2)}) collective-permute-start(bf16[4,128,512]{2,1,0:T(8,128)(2,1)} %local_ref.1), channel_id=1, source_target_pairs={{0,1},{1,2},{2,3},{3,4},{4,5},{5,6},{6,7},{7,8},{8,9},{9,10},{10,1... | collective-permute-start | bytes 1572872 | tf_op jit(solution)/shard_map/ppermute | solution.py:14
  16.3 6.5 %collective-permute-start.4 = (bf16[4,128,512]{2,1,0:T(8,128)(2,1)}, bf16[4,128,512]{2,1,0:T(8,128)(2,1)S(1)}, u32[]{:S(2)}, u32[]{:S(2)}) collective-permute-start(bf16[4,128,512]{2,1,0:T(8,128)(2,1)} %local_ref.1), channel_id=1, source_target_pairs={{0,31},{1,0},{2,1},{3,2},{4,3},{5,4},{6,5},{7,6},{8,7},{9,8},{10,9... | collective-permute-start | bytes 1572872 | tf_op jit(solution)/shard_map/ppermute | solution.py:14
  22.8 0.7 compare_and_fusion
  23.5 0.8 add_bitcast_fusion.4
  24.3 0.7 broadcast_compare_fusion
  25.0 0.9 %fusion = bf16[4,9,513]{2,1,0:T(8,128)(2,1)S(1)} fusion(f32[4,9,513]{2,0,1:T(4,128)} %param.8, pred[4,513]{1,0:T(4,128)(4,1)S(1)} %broadcast_compare_fusion), kind=kLoop, calls=%fused_computation.2 | loop fusion | flops 18468 | bytes 112860 | tf_op jit(solution)/shard_map/convert_element_type | solution.py:35
  25.9 0.7 pad_convert_fusion.taps_ref
  26.6 4.7 %shard_map.64.band_ref = bf16[4,9,128,640]{3,2,1,0:T(8,128)(2,1)} custom-call(f32[4,9,640]{2,1,0:T(8,128)} %pad_convert_fusion.taps_ref), custom_call_target="tpu_custom_call" | custom-call | tf_op jit(solution)/shard_map/pallas_call | solution.py:73
  31.4 0.0 collective-permute-done
  31.4 0.0 collective-permute-done.1
  31.4 0.1 pad_add_fusion.1
  31.5 0.0 collective-permute-done.2.west_ref
  31.5 0.0 copy-start
  31.5 1.9 %collective-permute-start.3 = (bf16[4,128,512]{2,1,0:T(8,128)(2,1)S(1)}, bf16[4,128,512]{2,1,0:T(8,128)(2,1)S(1)}, u32[]{:S(2)}, u32[]{:S(2)}) collective-permute-start(bf16[4,128,512]{2,1,0:T(8,128)(2,1)S(1)} %collective-permute-done.2.west_ref), channel_id=1, source_target_pairs={{0,1},{1,2},{2,3},{3,4},{4,5},{5,6},{6,7},{7,8},{8,9},{9,10},{10,1... | collective-permute-start | bytes 1572872 | tf_op jit(solution)/shard_map/ppermute | solution.py:14
  33.4 0.0 collective-permute-done.4.east_ref
  33.4 0.0 copy-start.1
  33.4 7.3 %collective-permute-start.5 = (bf16[4,128,512]{2,1,0:T(8,128)(2,1)S(1)}, bf16[4,128,512]{2,1,0:T(8,128)(2,1)S(1)}, u32[]{:S(2)}, u32[]{:S(2)}) collective-permute-start(bf16[4,128,512]{2,1,0:T(8,128)(2,1)S(1)} %collective-permute-done.4.east_ref), channel_id=1, source_target_pairs={{0,31},{1,0},{2,1},{3,2},{4,3},{5,4},{6,5},{7,6},{8,7},{9,8},{10,9... | collective-permute-start | bytes 1572872 | tf_op jit(solution)/shard_map/ppermute | solution.py:14
  40.7 0.1 pad_add_fusion
  40.8 0.3 fusion.2
  41.1 0.7 reshape_reshape.3.counts_ref
  41.8 0.0 copy-start.4
  41.8 5.8 %collective-permute-done.3.far_west_ref = bf16[4,128,512]{2,1,0:T(8,128)(2,1)S(1)} collective-permute-done((bf16[4,128,512]{2,1,0:T(8,128)(2,1)S(1)}, bf16[4,128,512]{2,1,0:T(8,128)(2,1)S(1)}, u32[]{:S(2)}, u32[]{:S(2)}) %collective-permute-start.3) | collective-permute-done | bytes 524320 | tf_op jit(solution)/shard_map/ppermute | solution.py:14
  47.6 0.0 copy-start.2
  47.6 1.8 %collective-permute-done.5.far_east_ref = bf16[4,128,512]{2,1,0:T(8,128)(2,1)S(1)} collective-permute-done((bf16[4,128,512]{2,1,0:T(8,128)(2,1)S(1)}, bf16[4,128,512]{2,1,0:T(8,128)(2,1)S(1)}, u32[]{:S(2)}, u32[]{:S(2)}) %collective-permute-start.5) | collective-permute-done | bytes 524320 | tf_op jit(solution)/shard_map/ppermute | solution.py:14
  49.4 0.0 copy-done
  49.4 0.0 copy-done.1
  49.4 0.0 copy-done.2
  49.4 0.0 copy-start.3
  49.4 0.8 copy-done.3
  50.2 15.3 %shard_map.65 = (bf16[2,128,512]{2,1,0:T(8,128)(2,1)}, bf16[2,128,512]{2,1,0:T(8,128)(2,1)}, f32[4,128,512]{2,1,0:T(8,128)}) custom-call(f32[288]{0:T(512)} %reshape_reshape.3.counts_ref, bf16[4,9,128,640]{3,2,1,0:T(8,128)(2,1)} %shard_map.64.band_ref, bf16[4,128,512]{2,1,0:T(8,128)(2,1)} %copy-done.2, bf16[4,128,512]{2,1,0:T(8,128)(2,1)} %copy-done, ...), custom_call_target="tpu_custom_call" | custom-call | tf_op jit(solution)/shard_map/pallas_call | solution.py:132
  65.5 8.5 %collective-permute-start.6 = (bf16[2,128,512]{2,1,0:T(8,128)(2,1)}, bf16[2,128,512]{2,1,0:T(8,128)(2,1)S(1)}, u32[]{:S(2)}, u32[]{:S(2)}) collective-permute-start(bf16[2,128,512]{2,1,0:T(8,128)(2,1)} %get-tuple-element.9), channel_id=1, source_target_pairs={{0,32},{32,64},{64,96},{96,128},{128,160},{160,192},{192,224},{224... | collective-permute-start | bytes 786440 | tf_op jit(solution)/shard_map/ppermute | solution.py:182
  74.0 1.9 %collective-permute-start.7 = (bf16[2,128,512]{2,1,0:T(8,128)(2,1)}, bf16[2,128,512]{2,1,0:T(8,128)(2,1)S(1)}, u32[]{:S(2)}, u32[]{:S(2)}) collective-permute-start(bf16[2,128,512]{2,1,0:T(8,128)(2,1)} %get-tuple-element.10), channel_id=1, source_target_pairs={{32,0},{64,32},{96,64},{128,96},{160,128},{192,160},{224,192},{256... | collective-permute-start | bytes 786440 | tf_op jit(solution)/shard_map/ppermute | solution.py:181
  76.0 1.7 %collective-permute-done.6 = bf16[2,128,512]{2,1,0:T(8,128)(2,1)S(1)} collective-permute-done((bf16[2,128,512]{2,1,0:T(8,128)(2,1)}, bf16[2,128,512]{2,1,0:T(8,128)(2,1)S(1)}, u32[]{:S(2)}, u32[]{:S(2)}) %collective-permute-start.6) | collective-permute-done | bytes 262176 | tf_op jit(solution)/shard_map/ppermute | solution.py:182
  77.6 10.3 %collective-permute-done.7 = bf16[2,128,512]{2,1,0:T(8,128)(2,1)S(1)} collective-permute-done((bf16[2,128,512]{2,1,0:T(8,128)(2,1)}, bf16[2,128,512]{2,1,0:T(8,128)(2,1)S(1)}, u32[]{:S(2)}, u32[]{:S(2)}) %collective-permute-start.7) | collective-permute-done | bytes 262176 | tf_op jit(solution)/shard_map/ppermute | solution.py:181
  88.0 0.0 copy-done.4
  88.0 2.2 %multiply_convert_fusion = bf16[4,128,512]{2,1,0:T(8,128)(2,1)} fusion(f32[4,128,512]{2,1,0:T(8,128)} %get-tuple-element.8, f32[4]{0:T(128)S(1)} %copy-done.4, bf16[2,128,512]{2,1,0:T(8,128)(2,1)S(1)} %collective-permute-done.7, bf16[2,128,512]{2,1,0:T(8,128)(2,1)S(1)} %collective-permute-done.6), kind=kLoop, calls=%fused_computation | loop fusion | flops 1572864 | bytes 2097168 | tf_op jit(solution)/shard_map/convert_element_type | solution.py:185
  (5 shorter events, 0.0 us)
Async XLA Ops:
  0.0 31.4 %collective-permute-start = (s32[96,3]{0,1:T(4,128)}, s32[96,3]{0,1:T(4,128)S(1)}, u32[]{:S(2)}, u32[]{:S(2)}) collective-permute-start(s32[96,3]{0,1:T(4,128)} %param.10), channel_id=1, source_target_pairs={{0,32},{32,64},{64,96},{96,128},{128,160},{160,192},{192,224},{224... | collective-permute-start | bytes 3464 | tf_op jit(solution)/shard_map/ppermute | solution.py:22
  11.1 20.3 %collective-permute-start.1 = (s32[96,3]{0,1:T(4,128)}, s32[96,3]{0,1:T(4,128)S(1)}, u32[]{:S(2)}, u32[]{:S(2)}) collective-permute-start(s32[96,3]{0,1:T(4,128)} %param.10), channel_id=1, source_target_pairs={{32,0},{64,32},{96,64},{128,96},{160,128},{192,160},{224,192},{256... | collective-permute-start | bytes 3464 | tf_op jit(solution)/shard_map/ppermute | solution.py:25
  13.0 18.4 %collective-permute-start.2 = (bf16[4,128,512]{2,1,0:T(8,128)(2,1)}, bf16[4,128,512]{2,1,0:T(8,128)(2,1)S(1)}, u32[]{:S(2)}, u32[]{:S(2)}) collective-permute-start(bf16[4,128,512]{2,1,0:T(8,128)(2,1)} %local_ref.1), channel_id=1, source_target_pairs={{0,1},{1,2},{2,3},{3,4},{4,5},{5,6},{6,7},{7,8},{8,9},{9,10},{10,1... | collective-permute-start | bytes 1572872 | tf_op jit(solution)/shard_map/ppermute | solution.py:14
  16.3 17.2 %collective-permute-start.4 = (bf16[4,128,512]{2,1,0:T(8,128)(2,1)}, bf16[4,128,512]{2,1,0:T(8,128)(2,1)S(1)}, u32[]{:S(2)}, u32[]{:S(2)}) collective-permute-start(bf16[4,128,512]{2,1,0:T(8,128)(2,1)} %local_ref.1), channel_id=1, source_target_pairs={{0,31},{1,0},{2,1},{3,2},{4,3},{5,4},{6,5},{7,6},{8,7},{9,8},{10,9... | collective-permute-start | bytes 1572872 | tf_op jit(solution)/shard_map/ppermute | solution.py:14
  31.5 17.9 %copy-start = (bf16[4,128,512]{2,1,0:T(8,128)(2,1)}, bf16[4,128,512]{2,1,0:T(8,128)(2,1)S(1)}, u32[]{:S(2)}) copy-start(bf16[4,128,512]{2,1,0:T(8,128)(2,1)S(1)} %collective-permute-done.2.west_ref) | copy-start | bytes 1572868
  31.5 16.1 %collective-permute-start.3 = (bf16[4,128,512]{2,1,0:T(8,128)(2,1)S(1)}, bf16[4,128,512]{2,1,0:T(8,128)(2,1)S(1)}, u32[]{:S(2)}, u32[]{:S(2)}) collective-permute-start(bf16[4,128,512]{2,1,0:T(8,128)(2,1)S(1)} %collective-permute-done.2.west_ref), channel_id=1, source_target_pairs={{0,1},{1,2},{2,3},{3,4},{4,5},{5,6},{6,7},{7,8},{8,9},{9,10},{10,1... | collective-permute-start | bytes 1572872 | tf_op jit(solution)/shard_map/ppermute | solution.py:14
  33.4 15.9 %copy-start.1 = (bf16[4,128,512]{2,1,0:T(8,128)(2,1)}, bf16[4,128,512]{2,1,0:T(8,128)(2,1)S(1)}, u32[]{:S(2)}) copy-start(bf16[4,128,512]{2,1,0:T(8,128)(2,1)S(1)} %collective-permute-done.4.east_ref) | copy-start | bytes 1572868
  33.4 15.9 %collective-permute-start.5 = (bf16[4,128,512]{2,1,0:T(8,128)(2,1)S(1)}, bf16[4,128,512]{2,1,0:T(8,128)(2,1)S(1)}, u32[]{:S(2)}, u32[]{:S(2)}) collective-permute-start(bf16[4,128,512]{2,1,0:T(8,128)(2,1)S(1)} %collective-permute-done.4.east_ref), channel_id=1, source_target_pairs={{0,31},{1,0},{2,1},{3,2},{4,3},{5,4},{6,5},{7,6},{8,7},{9,8},{10,9... | collective-permute-start | bytes 1572872 | tf_op jit(solution)/shard_map/ppermute | solution.py:14
  41.8 46.1 %copy-start.4 = (f32[4]{0:T(128)S(1)}, f32[4]{0:T(128)}, u32[]{:S(2)}) copy-start(f32[4]{0:T(128)} %param.9) | copy-start | bytes 52
  47.6 1.8 %copy-start.2 = (bf16[4,128,512]{2,1,0:T(8,128)(2,1)}, bf16[4,128,512]{2,1,0:T(8,128)(2,1)S(1)}, u32[]{:S(2)}) copy-start(bf16[4,128,512]{2,1,0:T(8,128)(2,1)S(1)} %collective-permute-done.3.far_west_ref) | copy-start | bytes 1572868
  49.4 0.9 copy-start.3
  65.5 12.1 %collective-permute-start.6 = (bf16[2,128,512]{2,1,0:T(8,128)(2,1)}, bf16[2,128,512]{2,1,0:T(8,128)(2,1)S(1)}, u32[]{:S(2)}, u32[]{:S(2)}) collective-permute-start(bf16[2,128,512]{2,1,0:T(8,128)(2,1)} %get-tuple-element.9), channel_id=1, source_target_pairs={{0,32},{32,64},{64,96},{96,128},{128,160},{160,192},{192,224},{224... | collective-permute-start | bytes 786440 | tf_op jit(solution)/shard_map/ppermute | solution.py:182
  74.0 13.9 %collective-permute-start.7 = (bf16[2,128,512]{2,1,0:T(8,128)(2,1)}, bf16[2,128,512]{2,1,0:T(8,128)(2,1)S(1)}, u32[]{:S(2)}, u32[]{:S(2)}) collective-permute-start(bf16[2,128,512]{2,1,0:T(8,128)(2,1)} %get-tuple-element.10), channel_id=1, source_target_pairs={{32,0},{64,32},{96,64},{128,96},{160,128},{192,160},{224,192},{256... | collective-permute-start | bytes 786440 | tf_op jit(solution)/shard_map/ppermute | solution.py:181

commit v10 on v9

--- a/solution.py
+++ b/solution.py
@@ -98,7 +98,7 @@
     mixed_ref[...] = jnp.dot(response_ref[...], weight_ref[0], preferred_element_type=jnp.float32)
     chunk = 16
 
-    def accumulate(first):
+    def accumulate(first, last):
         def body(step, carry):
             start = pl.multiple_of(step * chunk, chunk)
             pieces = [mixed_ref[pl.ds(in_row * cols + start, chunk), :] for in_row in range(input_rows)]
@@ -108,19 +108,21 @@
                     scale = counts_ref[(out_row * kinds + kind) * input_rows + in_row]
                     term = scale * pieces[in_row]
                     total = term if total is None else total + term
-                total_ref[out_row, pl.ds(start, chunk), :] = total
+                if not last:
+                    total_ref[out_row, pl.ds(start, chunk), :] = total
+                elif out_row < RIM:
+                    upper_ref[out_row, pl.ds(start, chunk), :] = total.astype(upper_ref.dtype)
+                elif out_row < RIM + input_rows:
+                    inner_ref[out_row - RIM, pl.ds(start, chunk), :] = total
+                else:
+                    lower_ref[out_row - RIM - input_rows, pl.ds(start, chunk), :] = total.astype(lower_ref.dtype)
             return carry
 
         lax.fori_loop(0, cols // chunk, body, 0)
 
-    pl.when(kind == 0)(lambda: accumulate(True))
-    pl.when(kind > 0)(lambda: accumulate(False))
-
-    @pl.when(kind == kinds - 1)
-    def _():
-        inner_ref[...] = total_ref[RIM : RIM + input_rows]
-        upper_ref[...] = total_ref[:RIM].astype(upper_ref.dtype)
-        lower_ref[...] = total_ref[RIM + input_rows :].astype(lower_ref.dtype)
+    pl.when(kind == 0)(lambda: accumulate(True, False))
+    pl.when((kind > 0) & (kind < kinds - 1))(lambda: accumulate(False, False))
+    pl.when(kind == kinds - 1)(lambda: accumulate(False, True))
 
 
 def block_partials(counts, short_taps, parts, mix_weight):

time: 90.8 us -> 90.7 us (level)
  no operation moved by 1% of the time
where the time goes in v10:
time: 90.7 us; the launch traced here: 90.1 us
  starting transfers between devices  42.4 us (47%)
  Pallas kernels  19.9 us (22%)
  waiting for transfers between devices  19.5 us (21%)
  other arithmetic  6.24 us (7%)
  local copies, waits for them, and re-layouts  1.55 us (2%)
    ppermute x4, starting transfers between devices, shifted(): lax.ppermute(value, axis, [(i, (i + by) % length) for i in range(length)])  18.9 us
    pallas_call x1, Pallas kernels, block_partials(): pl.pallas_call(_block_kernel, grid=(kinds,), in_specs=[pl.BlockSpec(memor...  15.2 us
    ppermute x1, starting transfers between devices, with_halo(): lax.ppermute(lax.slice_in_dim(block, block.shape[dim] - width, None, axis...  11.1 us
    ppermute x1, waiting for transfers between devices, on_device(): from_below = lax.ppermute(upper, 'lat', backward).astype(jnp.float32)  10.3 us
    ppermute x1, starting transfers between devices, on_device(): from_above = lax.ppermute(lower, 'lat', forward).astype(jnp.float32)  8.52 us
    ppermute x4, waiting for transfers between devices, shifted(): lax.ppermute(value, axis, [(i, (i + by) % length) for i in range(length)])  7.55 us
    pallas_call x1, Pallas kernels, band_matrix(): pl.pallas_call(_toeplitz_kernel, grid=(rows,), in_specs=[pl.BlockSpec((1,...  4.74 us
    convert_element_type x1, other arithmetic, on_device(): return (inner * row_scale[:, None, None]).astype(jnp.bfloat16)  2.25 us
  transfers between devices with their start and end apart: 8, of which 4 were waited for; matrix products, arithmetic and copies ran while one was open for 6% of the time, Pallas kernels for 5%

profile of v10, /device:TPU:7, one launch (start us, length us, event | category | flops | bytes accessed | tf_op | source)
XLA Modules:
  0.0 90.1 jit_solution(4897593653407222470)
XLA Ops:
  0.0 11.1 %collective-permute-start = (s32[96,3]{0,1:T(4,128)}, s32[96,3]{0,1:T(4,128)S(1)}, u32[]{:S(2)}, u32[]{:S(2)}) collective-permute-start(s32[96,3]{0,1:T(4,128)} %param.10), channel_id=1, source_target_pairs={{0,32},{32,64},{64,96},{96,128},{128,160},{160,192},{192,224},{224... | collective-permute-start | bytes 3464 | tf_op jit(solution)/shard_map/ppermute | solution.py:22
  11.1 1.9 %collective-permute-start.1 = (s32[96,3]{0,1:T(4,128)}, s32[96,3]{0,1:T(4,128)S(1)}, u32[]{:S(2)}, u32[]{:S(2)}) collective-permute-start(s32[96,3]{0,1:T(4,128)} %param.10), channel_id=1, source_target_pairs={{32,0},{64,32},{96,64},{128,96},{160,128},{192,160},{224,192},{256... | collective-permute-start | bytes 3464 | tf_op jit(solution)/shard_map/ppermute | solution.py:25
  13.0 3.2 %collective-permute-start.2 = (bf16[4,128,512]{2,1,0:T(8,128)(2,1)}, bf16[4,128,512]{2,1,0:T(8,128)(2,1)S(1)}, u32[]{:S(2)}, u32[]{:S(2)}) collective-permute-start(bf16[4,128,512]{2,1,0:T(8,128)(2,1)} %local_ref.1), channel_id=1, source_target_pairs={{0,1},{1,2},{2,3},{3,4},{4,5},{5,6},{6,7},{7,8},{8,9},{9,10},{10,1... | collective-permute-start | bytes 1572872 | tf_op jit(solution)/shard_map/ppermute | solution.py:14
  16.3 6.5 %collective-permute-start.4 = (bf16[4,128,512]{2,1,0:T(8,128)(2,1)}, bf16[4,128,512]{2,1,0:T(8,128)(2,1)S(1)}, u32[]{:S(2)}, u32[]{:S(2)}) collective-permute-start(bf16[4,128,512]{2,1,0:T(8,128)(2,1)} %local_ref.1), channel_id=1, source_target_pairs={{0,31},{1,0},{2,1},{3,2},{4,3},{5,4},{6,5},{7,6},{8,7},{9,8},{10,9... | collective-permute-start | bytes 1572872 | tf_op jit(solution)/shard_map/ppermute | solution.py:14
  22.8 0.7 compare_and_fusion
  23.5 0.8 add_bitcast_fusion.4
  24.3 0.7 broadcast_compare_fusion
  25.0 0.9 %fusion = bf16[4,9,513]{2,1,0:T(8,128)(2,1)S(1)} fusion(f32[4,9,513]{2,0,1:T(4,128)} %param.8, pred[4,513]{1,0:T(4,128)(4,1)S(1)} %broadcast_compare_fusion), kind=kLoop, calls=%fused_computation.2 | loop fusion | flops 18468 | bytes 112860 | tf_op jit(solution)/shard_map/convert_element_type | solution.py:35
  25.9 0.7 pad_convert_fusion.taps_ref
  26.6 4.7 %shard_map.64.band_ref = bf16[4,9,128,640]{3,2,1,0:T(8,128)(2,1)} custom-call(f32[4,9,640]{2,1,0:T(8,128)} %pad_convert_fusion.taps_ref), custom_call_target="tpu_custom_call" | custom-call | tf_op jit(solution)/shard_map/pallas_call | solution.py:73
  31.4 0.0 collective-permute-done
  31.4 0.0 collective-permute-done.1
  31.4 0.1 pad_add_fusion.1
  31.5 0.0 collective-permute-done.2.west_ref
  31.5 0.0 copy-start
  31.5 1.9 %collective-permute-start.3 = (bf16[4,128,512]{2,1,0:T(8,128)(2,1)S(1)}, bf16[4,128,512]{2,1,0:T(8,128)(2,1)S(1)}, u32[]{:S(2)}, u32[]{:S(2)}) collective-permute-start(bf16[4,128,512]{2,1,0:T(8,128)(2,1)S(1)} %collective-permute-done.2.west_ref), channel_id=1, source_target_pairs={{0,1},{1,2},{2,3},{3,4},{4,5},{5,6},{6,7},{7,8},{8,9},{9,10},{10,1... | collective-permute-start | bytes 1572872 | tf_op jit(solution)/shard_map/ppermute | solution.py:14
  33.4 0.0 collective-permute-done.4.east_ref
  33.4 0.0 copy-start.1
  33.4 7.3 %collective-permute-start.5 = (bf16[4,128,512]{2,1,0:T(8,128)(2,1)S(1)}, bf16[4,128,512]{2,1,0:T(8,128)(2,1)S(1)}, u32[]{:S(2)}, u32[]{:S(2)}) collective-permute-start(bf16[4,128,512]{2,1,0:T(8,128)(2,1)S(1)} %collective-permute-done.4.east_ref), channel_id=1, source_target_pairs={{0,31},{1,0},{2,1},{3,2},{4,3},{5,4},{6,5},{7,6},{8,7},{9,8},{10,9... | collective-permute-start | bytes 1572872 | tf_op jit(solution)/shard_map/ppermute | solution.py:14
  40.7 0.1 pad_add_fusion
  40.8 0.3 fusion.2
  41.1 0.7 reshape_reshape.3.counts_ref
  41.8 0.0 copy-start.4
  41.8 5.8 %collective-permute-done.3.far_west_ref = bf16[4,128,512]{2,1,0:T(8,128)(2,1)S(1)} collective-permute-done((bf16[4,128,512]{2,1,0:T(8,128)(2,1)S(1)}, bf16[4,128,512]{2,1,0:T(8,128)(2,1)S(1)}, u32[]{:S(2)}, u32[]{:S(2)}) %collective-permute-start.3) | collective-permute-done | bytes 524320 | tf_op jit(solution)/shard_map/ppermute | solution.py:14
  47.6 0.0 copy-start.2
  47.6 1.8 %collective-permute-done.5.far_east_ref = bf16[4,128,512]{2,1,0:T(8,128)(2,1)S(1)} collective-permute-done((bf16[4,128,512]{2,1,0:T(8,128)(2,1)S(1)}, bf16[4,128,512]{2,1,0:T(8,128)(2,1)S(1)}, u32[]{:S(2)}, u32[]{:S(2)}) %collective-permute-start.5) | collective-permute-done | bytes 524320 | tf_op jit(solution)/shard_map/ppermute | solution.py:14
  49.4 0.0 copy-done
  49.4 0.0 copy-done.1
  49.4 0.0 copy-done.2
  49.4 0.0 copy-start.3
  49.4 0.8 copy-done.3
  50.2 15.2 %shard_map.65 = (bf16[2,128,512]{2,1,0:T(8,128)(2,1)}, bf16[2,128,512]{2,1,0:T(8,128)(2,1)}, f32[4,128,512]{2,1,0:T(8,128)}) custom-call(f32[288]{0:T(512)} %reshape_reshape.3.counts_ref, bf16[4,9,128,640]{3,2,1,0:T(8,128)(2,1)} %shard_map.64.band_ref, bf16[4,128,512]{2,1,0:T(8,128)(2,1)} %copy-done.2, bf16[4,128,512]{2,1,0:T(8,128)(2,1)} %copy-done, ...), custom_call_target="tpu_custom_call" | custom-call | tf_op jit(solution)/shard_map/pallas_call | solution.py:134
  65.4 8.5 %collective-permute-start.6 = (bf16[2,128,512]{2,1,0:T(8,128)(2,1)}, bf16[2,128,512]{2,1,0:T(8,128)(2,1)S(1)}, u32[]{:S(2)}, u32[]{:S(2)}) collective-permute-start(bf16[2,128,512]{2,1,0:T(8,128)(2,1)} %get-tuple-element.9), channel_id=1, source_target_pairs={{0,32},{32,64},{64,96},{96,128},{128,160},{160,192},{192,224},{224... | collective-permute-start | bytes 786440 | tf_op jit(solution)/shard_map/ppermute | solution.py:184
  73.9 1.9 %collective-permute-start.7 = (bf16[2,128,512]{2,1,0:T(8,128)(2,1)}, bf16[2,128,512]{2,1,0:T(8,128)(2,1)S(1)}, u32[]{:S(2)}, u32[]{:S(2)}) collective-permute-start(bf16[2,128,512]{2,1,0:T(8,128)(2,1)} %get-tuple-element.10), channel_id=1, source_target_pairs={{32,0},{64,32},{96,64},{128,96},{160,128},{192,160},{224,192},{256... | collective-permute-start | bytes 786440 | tf_op jit(solution)/shard_map/ppermute | solution.py:183
  75.9 1.7 %collective-permute-done.6 = bf16[2,128,512]{2,1,0:T(8,128)(2,1)S(1)} collective-permute-done((bf16[2,128,512]{2,1,0:T(8,128)(2,1)}, bf16[2,128,512]{2,1,0:T(8,128)(2,1)S(1)}, u32[]{:S(2)}, u32[]{:S(2)}) %collective-permute-start.6) | collective-permute-done | bytes 262176 | tf_op jit(solution)/shard_map/ppermute | solution.py:184
  77.6 10.3 %collective-permute-done.7 = bf16[2,128,512]{2,1,0:T(8,128)(2,1)S(1)} collective-permute-done((bf16[2,128,512]{2,1,0:T(8,128)(2,1)}, bf16[2,128,512]{2,1,0:T(8,128)(2,1)S(1)}, u32[]{:S(2)}, u32[]{:S(2)}) %collective-permute-start.7) | collective-permute-done | bytes 262176 | tf_op jit(solution)/shard_map/ppermute | solution.py:183
  87.9 0.0 copy-done.4
  87.9 2.2 %multiply_convert_fusion = bf16[4,128,512]{2,1,0:T(8,128)(2,1)} fusion(f32[4,128,512]{2,1,0:T(8,128)} %get-tuple-element.8, f32[4]{0:T(128)S(1)} %copy-done.4, bf16[2,128,512]{2,1,0:T(8,128)(2,1)S(1)} %collective-permute-done.7, bf16[2,128,512]{2,1,0:T(8,128)(2,1)S(1)} %collective-permute-done.6), kind=kLoop, calls=%fused_computation | loop fusion | flops 1572864 | bytes 2097168 | tf_op jit(solution)/shard_map/convert_element_type | solution.py:187
  (5 shorter events, 0.0 us)
Async XLA Ops:
  0.0 31.4 %collective-permute-start = (s32[96,3]{0,1:T(4,128)}, s32[96,3]{0,1:T(4,128)S(1)}, u32[]{:S(2)}, u32[]{:S(2)}) collective-permute-start(s32[96,3]{0,1:T(4,128)} %param.10), channel_id=1, source_target_pairs={{0,32},{32,64},{64,96},{96,128},{128,160},{160,192},{192,224},{224... | collective-permute-start | bytes 3464 | tf_op jit(solution)/shard_map/ppermute | solution.py:22
  11.1 20.3 %collective-permute-start.1 = (s32[96,3]{0,1:T(4,128)}, s32[96,3]{0,1:T(4,128)S(1)}, u32[]{:S(2)}, u32[]{:S(2)}) collective-permute-start(s32[96,3]{0,1:T(4,128)} %param.10), channel_id=1, source_target_pairs={{32,0},{64,32},{96,64},{128,96},{160,128},{192,160},{224,192},{256... | collective-permute-start | bytes 3464 | tf_op jit(solution)/shard_map/ppermute | solution.py:25
  13.0 18.4 %collective-permute-start.2 = (bf16[4,128,512]{2,1,0:T(8,128)(2,1)}, bf16[4,128,512]{2,1,0:T(8,128)(2,1)S(1)}, u32[]{:S(2)}, u32[]{:S(2)}) collective-permute-start(bf16[4,128,512]{2,1,0:T(8,128)(2,1)} %local_ref.1), channel_id=1, source_target_pairs={{0,1},{1,2},{2,3},{3,4},{4,5},{5,6},{6,7},{7,8},{8,9},{9,10},{10,1... | collective-permute-start | bytes 1572872 | tf_op jit(solution)/shard_map/ppermute | solution.py:14
  16.3 17.2 %collective-permute-start.4 = (bf16[4,128,512]{2,1,0:T(8,128)(2,1)}, bf16[4,128,512]{2,1,0:T(8,128)(2,1)S(1)}, u32[]{:S(2)}, u32[]{:S(2)}) collective-permute-start(bf16[4,128,512]{2,1,0:T(8,128)(2,1)} %local_ref.1), channel_id=1, source_target_pairs={{0,31},{1,0},{2,1},{3,2},{4,3},{5,4},{6,5},{7,6},{8,7},{9,8},{10,9... | collective-permute-start | bytes 1572872 | tf_op jit(solution)/shard_map/ppermute | solution.py:14
  31.5 17.9 %copy-start = (bf16[4,128,512]{2,1,0:T(8,128)(2,1)}, bf16[4,128,512]{2,1,0:T(8,128)(2,1)S(1)}, u32[]{:S(2)}) copy-start(bf16[4,128,512]{2,1,0:T(8,128)(2,1)S(1)} %collective-permute-done.2.west_ref) | copy-start | bytes 1572868
  31.5 16.1 %collective-permute-start.3 = (bf16[4,128,512]{2,1,0:T(8,128)(2,1)S(1)}, bf16[4,128,512]{2,1,0:T(8,128)(2,1)S(1)}, u32[]{:S(2)}, u32[]{:S(2)}) collective-permute-start(bf16[4,128,512]{2,1,0:T(8,128)(2,1)S(1)} %collective-permute-done.2.west_ref), channel_id=1, source_target_pairs={{0,1},{1,2},{2,3},{3,4},{4,5},{5,6},{6,7},{7,8},{8,9},{9,10},{10,1... | collective-permute-start | bytes 1572872 | tf_op jit(solution)/shard_map/ppermute | solution.py:14
  33.4 15.9 %copy-start.1 = (bf16[4,128,512]{2,1,0:T(8,128)(2,1)}, bf16[4,128,512]{2,1,0:T(8,128)(2,1)S(1)}, u32[]{:S(2)}) copy-start(bf16[4,128,512]{2,1,0:T(8,128)(2,1)S(1)} %collective-permute-done.4.east_ref) | copy-start | bytes 1572868
  33.4 15.9 %collective-permute-start.5 = (bf16[4,128,512]{2,1,0:T(8,128)(2,1)S(1)}, bf16[4,128,512]{2,1,0:T(8,128)(2,1)S(1)}, u32[]{:S(2)}, u32[]{:S(2)}) collective-permute-start(bf16[4,128,512]{2,1,0:T(8,128)(2,1)S(1)} %collective-permute-done.4.east_ref), channel_id=1, source_target_pairs={{0,31},{1,0},{2,1},{3,2},{4,3},{5,4},{6,5},{7,6},{8,7},{9,8},{10,9... | collective-permute-start | bytes 1572872 | tf_op jit(solution)/shard_map/ppermute | solution.py:14
  41.8 46.0 %copy-start.4 = (f32[4]{0:T(128)S(1)}, f32[4]{0:T(128)}, u32[]{:S(2)}) copy-start(f32[4]{0:T(128)} %param.9) | copy-start | bytes 52
  47.6 1.8 %copy-start.2 = (bf16[4,128,512]{2,1,0:T(8,128)(2,1)}, bf16[4,128,512]{2,1,0:T(8,128)(2,1)S(1)}, u32[]{:S(2)}) copy-start(bf16[4,128,512]{2,1,0:T(8,128)(2,1)S(1)} %collective-permute-done.3.far_west_ref) | copy-start | bytes 1572868
  49.4 0.9 copy-start.3
  65.4 12.1 %collective-permute-start.6 = (bf16[2,128,512]{2,1,0:T(8,128)(2,1)}, bf16[2,128,512]{2,1,0:T(8,128)(2,1)S(1)}, u32[]{:S(2)}, u32[]{:S(2)}) collective-permute-start(bf16[2,128,512]{2,1,0:T(8,128)(2,1)} %get-tuple-element.9), channel_id=1, source_target_pairs={{0,32},{32,64},{64,96},{96,128},{128,160},{160,192},{192,224},{224... | collective-permute-start | bytes 786440 | tf_op jit(solution)/shard_map/ppermute | solution.py:184
  73.9 13.9 %collective-permute-start.7 = (bf16[2,128,512]{2,1,0:T(8,128)(2,1)}, bf16[2,128,512]{2,1,0:T(8,128)(2,1)S(1)}, u32[]{:S(2)}, u32[]{:S(2)}) collective-permute-start(bf16[2,128,512]{2,1,0:T(8,128)(2,1)} %get-tuple-element.10), channel_id=1, source_target_pairs={{32,0},{64,32},{96,64},{128,96},{160,128},{192,160},{224,192},{256... | collective-permute-start | bytes 786440 | tf_op jit(solution)/shard_map/ppermute | solution.py:183

commit v11 on v9

--- a/solution.py
+++ b/solution.py
@@ -80,20 +80,22 @@
 
 
 def _block_kernel(counts_ref, band_ref, far_west_ref, west_ref, local_ref, east_ref, far_east_ref,
-                  weight_ref, upper_ref, lower_ref, inner_ref, window_ref, response_ref, mixed_ref, total_ref):
+                  weight_ref, upper_ref, lower_ref, inner_ref, response_ref, mixed_ref, total_ref):
     kind = pl.program_id(0)
     kinds = pl.num_programs(0)
     input_rows, cols, _ = local_ref.shape
     output_rows = input_rows + 2 * RIM
     parts = (far_west_ref, west_ref, local_ref, east_ref, far_east_ref)
 
-    @pl.when(kind == 0)
-    def _():
+    for in_row in range(input_rows):
+        response = None
         for index, part in enumerate(parts):
-            window_ref[:, index * cols : (index + 1) * cols, :] = part[...]
-
-    for in_row in range(input_rows):
-        response = jnp.dot(band_ref[in_row, 0], window_ref[in_row], preferred_element_type=jnp.float32)
+            term = jnp.dot(
+                band_ref[in_row, 0, :, index * cols : (index + 1) * cols],
+                part[in_row],
+                preferred_element_type=jnp.float32,
+            )
+            response = term if response is None else response + term
         response_ref[in_row * cols : (in_row + 1) * cols, :] = response.astype(jnp.bfloat16)
     mixed_ref[...] = jnp.dot(response_ref[...], weight_ref[0], preferred_element_type=jnp.float32)
     chunk = 16
@@ -145,7 +147,6 @@
             jax.ShapeDtypeStruct((rows, cols, channels), jnp.float32),
         ],
         scratch_shapes=[
-            pltpu.VMEM((rows, window, channels), jnp.bfloat16),
             pltpu.VMEM((rows * cols, channels), jnp.bfloat16),
             pltpu.VMEM((rows * cols, mix_weight.shape[2]), jnp.float32),
             pltpu.VMEM((rows + 2 * RIM, cols, mix_weight.shape[2]), jnp.float32),

time: 90.8 us -> 92.8 us (1.022)
  Pallas kernels: 20 us -> 22.1 us
    pallas_call x1, Pallas kernels: 15.3 us -> 17.3 us  [block_partials(): pl.pallas_call(_block_kernel, grid=(kinds,), in_specs=[pl.BlockSpec(memor...]
  transfers between devices with their start and end apart: 8 -> 8, of which waited for: 4 -> 4; matrix products, arithmetic and copies ran while one was open for 6% -> 5% of each run, Pallas kernels for 5% -> 5%
where the time goes in v11:
time: 92.8 us; the launch traced here: 92.3 us
  starting transfers between devices  42.4 us (46%)
  Pallas kernels  22.1 us (24%)
  waiting for transfers between devices  19.5 us (21%)
  other arithmetic  6.24 us (7%)
  local copies, waits for them, and re-layouts  1.55 us (2%)
    ppermute x4, starting transfers between devices, shifted(): lax.ppermute(value, axis, [(i, (i + by) % length) for i in range(length)])  18.9 us
    pallas_call x1, Pallas kernels, block_partials(): pl.pallas_call(_block_kernel, grid=(kinds,), in_specs=[pl.BlockSpec(memor...  17.3 us
    ppermute x1, starting transfers between devices, with_halo(): lax.ppermute(lax.slice_in_dim(block, block.shape[dim] - width, None, axis...  11.1 us
    ppermute x1, waiting for transfers between devices, on_device(): from_below = lax.ppermute(upper, 'lat', backward).astype(jnp.float32)  10.3 us
    ppermute x1, starting transfers between devices, on_device(): from_above = lax.ppermute(lower, 'lat', forward).astype(jnp.float32)  8.53 us
    ppermute x4, waiting for transfers between devices, shifted(): lax.ppermute(value, axis, [(i, (i + by) % length) for i in range(length)])  7.55 us
    pallas_call x1, Pallas kernels, band_matrix(): pl.pallas_call(_toeplitz_kernel, grid=(rows,), in_specs=[pl.BlockSpec((1,...  4.74 us
    convert_element_type x1, other arithmetic, on_device(): return (inner * row_scale[:, None, None]).astype(jnp.bfloat16)  2.25 us
  transfers between devices with their start and end apart: 8, of which 4 were waited for; matrix products, arithmetic and copies ran while one was open for 5% of the time, Pallas kernels for 5%

profile of v11, /device:TPU:7, one launch (start us, length us, event | category | flops | bytes accessed | tf_op | source)
XLA Modules:
  0.0 92.3 jit_solution(13874899896732616549)
XLA Ops:
  0.0 11.1 %collective-permute-start = (s32[96,3]{0,1:T(4,128)}, s32[96,3]{0,1:T(4,128)S(1)}, u32[]{:S(2)}, u32[]{:S(2)}) collective-permute-start(s32[96,3]{0,1:T(4,128)} %param.10), channel_id=1, source_target_pairs={{0,32},{32,64},{64,96},{96,128},{128,160},{160,192},{192,224},{224... | collective-permute-start | bytes 3464 | tf_op jit(solution)/shard_map/ppermute | solution.py:22
  11.1 1.9 %collective-permute-start.1 = (s32[96,3]{0,1:T(4,128)}, s32[96,3]{0,1:T(4,128)S(1)}, u32[]{:S(2)}, u32[]{:S(2)}) collective-permute-start(s32[96,3]{0,1:T(4,128)} %param.10), channel_id=1, source_target_pairs={{32,0},{64,32},{96,64},{128,96},{160,128},{192,160},{224,192},{256... | collective-permute-start | bytes 3464 | tf_op jit(solution)/shard_map/ppermute | solution.py:25
  13.0 3.2 %collective-permute-start.2 = (bf16[4,128,512]{2,1,0:T(8,128)(2,1)}, bf16[4,128,512]{2,1,0:T(8,128)(2,1)S(1)}, u32[]{:S(2)}, u32[]{:S(2)}) collective-permute-start(bf16[4,128,512]{2,1,0:T(8,128)(2,1)} %local_ref.1), channel_id=1, source_target_pairs={{0,1},{1,2},{2,3},{3,4},{4,5},{5,6},{6,7},{7,8},{8,9},{9,10},{10,1... | collective-permute-start | bytes 1572872 | tf_op jit(solution)/shard_map/ppermute | solution.py:14
  16.3 6.5 %collective-permute-start.4 = (bf16[4,128,512]{2,1,0:T(8,128)(2,1)}, bf16[4,128,512]{2,1,0:T(8,128)(2,1)S(1)}, u32[]{:S(2)}, u32[]{:S(2)}) collective-permute-start(bf16[4,128,512]{2,1,0:T(8,128)(2,1)} %local_ref.1), channel_id=1, source_target_pairs={{0,31},{1,0},{2,1},{3,2},{4,3},{5,4},{6,5},{7,6},{8,7},{9,8},{10,9... | collective-permute-start | bytes 1572872 | tf_op jit(solution)/shard_map/ppermute | solution.py:14
  22.8 0.7 compare_and_fusion
  23.5 0.8 add_bitcast_fusion.4
  24.3 0.7 broadcast_compare_fusion
  25.0 0.9 fusion
  25.9 0.7 pad_convert_fusion.taps_ref
  26.6 4.7 %shard_map.64.band_ref = bf16[4,9,128,640]{3,2,1,0:T(8,128)(2,1)} custom-call(f32[4,9,640]{2,1,0:T(8,128)} %pad_convert_fusion.taps_ref), custom_call_target="tpu_custom_call" | custom-call | tf_op jit(solution)/shard_map/pallas_call | solution.py:73
  31.4 0.0 collective-permute-done
  31.4 0.0 collective-permute-done.1
  31.4 0.1 pad_add_fusion.1
  31.5 0.0 collective-permute-done.2.west_ref
  31.5 0.0 copy-start
  31.5 1.9 %collective-permute-start.3 = (bf16[4,128,512]{2,1,0:T(8,128)(2,1)S(1)}, bf16[4,128,512]{2,1,0:T(8,128)(2,1)S(1)}, u32[]{:S(2)}, u32[]{:S(2)}) collective-permute-start(bf16[4,128,512]{2,1,0:T(8,128)(2,1)S(1)} %collective-permute-done.2.west_ref), channel_id=1, source_target_pairs={{0,1},{1,2},{2,3},{3,4},{4,5},{5,6},{6,7},{7,8},{8,9},{9,10},{10,1... | collective-permute-start | bytes 1572872 | tf_op jit(solution)/shard_map/ppermute | solution.py:14
  33.4 0.0 collective-permute-done.4.east_ref
  33.4 0.0 copy-start.1
  33.4 7.3 %collective-permute-start.5 = (bf16[4,128,512]{2,1,0:T(8,128)(2,1)S(1)}, bf16[4,128,512]{2,1,0:T(8,128)(2,1)S(1)}, u32[]{:S(2)}, u32[]{:S(2)}) collective-permute-start(bf16[4,128,512]{2,1,0:T(8,128)(2,1)S(1)} %collective-permute-done.4.east_ref), channel_id=1, source_target_pairs={{0,31},{1,0},{2,1},{3,2},{4,3},{5,4},{6,5},{7,6},{8,7},{9,8},{10,9... | collective-permute-start | bytes 1572872 | tf_op jit(solution)/shard_map/ppermute | solution.py:14
  40.7 0.1 pad_add_fusion
  40.8 0.3 fusion.2
  41.1 0.7 reshape_reshape.3.counts_ref
  41.8 0.0 copy-start.4
  41.8 5.8 %collective-permute-done.3.far_west_ref = bf16[4,128,512]{2,1,0:T(8,128)(2,1)S(1)} collective-permute-done((bf16[4,128,512]{2,1,0:T(8,128)(2,1)S(1)}, bf16[4,128,512]{2,1,0:T(8,128)(2,1)S(1)}, u32[]{:S(2)}, u32[]{:S(2)}) %collective-permute-start.3) | collective-permute-done | bytes 524320 | tf_op jit(solution)/shard_map/ppermute | solution.py:14
  47.6 0.0 copy-start.2
  47.6 1.8 %collective-permute-done.5.far_east_ref = bf16[4,128,512]{2,1,0:T(8,128)(2,1)S(1)} collective-permute-done((bf16[4,128,512]{2,1,0:T(8,128)(2,1)S(1)}, bf16[4,128,512]{2,1,0:T(8,128)(2,1)S(1)}, u32[]{:S(2)}, u32[]{:S(2)}) %collective-permute-start.5) | collective-permute-done | bytes 524320 | tf_op jit(solution)/shard_map/ppermute | solution.py:14
  49.4 0.0 copy-done
  49.4 0.0 copy-done.1
  49.4 0.0 copy-done.2
  49.4 0.0 copy-start.3
  49.4 0.8 copy-done.3
  50.2 17.3 %shard_map.65 = (bf16[2,128,512]{2,1,0:T(8,128)(2,1)}, bf16[2,128,512]{2,1,0:T(8,128)(2,1)}, f32[4,128,512]{2,1,0:T(8,128)}) custom-call(f32[288]{0:T(512)} %reshape_reshape.3.counts_ref, bf16[4,9,128,640]{3,2,1,0:T(8,128)(2,1)} %shard_map.64.band_ref, bf16[4,128,512]{2,1,0:T(8,128)(2,1)} %copy-done.2, bf16[4,128,512]{2,1,0:T(8,128)(2,1)} %copy-done, ...), custom_call_target="tpu_custom_call" | custom-call | tf_op jit(solution)/shard_map/pallas_call | solution.py:134
  67.6 8.5 %collective-permute-start.6 = (bf16[2,128,512]{2,1,0:T(8,128)(2,1)}, bf16[2,128,512]{2,1,0:T(8,128)(2,1)S(1)}, u32[]{:S(2)}, u32[]{:S(2)}) collective-permute-start(bf16[2,128,512]{2,1,0:T(8,128)(2,1)} %get-tuple-element.9), channel_id=1, source_target_pairs={{0,32},{32,64},{64,96},{96,128},{128,160},{160,192},{192,224},{224... | collective-permute-start | bytes 786440 | tf_op jit(solution)/shard_map/ppermute | solution.py:183
  76.1 1.9 %collective-permute-start.7 = (bf16[2,128,512]{2,1,0:T(8,128)(2,1)}, bf16[2,128,512]{2,1,0:T(8,128)(2,1)S(1)}, u32[]{:S(2)}, u32[]{:S(2)}) collective-permute-start(bf16[2,128,512]{2,1,0:T(8,128)(2,1)} %get-tuple-element.10), channel_id=1, source_target_pairs={{32,0},{64,32},{96,64},{128,96},{160,128},{192,160},{224,192},{256... | collective-permute-start | bytes 786440 | tf_op jit(solution)/shard_map/ppermute | solution.py:182
  78.0 1.7 %collective-permute-done.6 = bf16[2,128,512]{2,1,0:T(8,128)(2,1)S(1)} collective-permute-done((bf16[2,128,512]{2,1,0:T(8,128)(2,1)}, bf16[2,128,512]{2,1,0:T(8,128)(2,1)S(1)}, u32[]{:S(2)}, u32[]{:S(2)}) %collective-permute-start.6) | collective-permute-done | bytes 262176 | tf_op jit(solution)/shard_map/ppermute | solution.py:183
  79.7 10.3 %collective-permute-done.7 = bf16[2,128,512]{2,1,0:T(8,128)(2,1)S(1)} collective-permute-done((bf16[2,128,512]{2,1,0:T(8,128)(2,1)}, bf16[2,128,512]{2,1,0:T(8,128)(2,1)S(1)}, u32[]{:S(2)}, u32[]{:S(2)}) %collective-permute-start.7) | collective-permute-done | bytes 262176 | tf_op jit(solution)/shard_map/ppermute | solution.py:182
  90.0 0.0 copy-done.4
  90.0 2.2 %multiply_convert_fusion = bf16[4,128,512]{2,1,0:T(8,128)(2,1)} fusion(f32[4,128,512]{2,1,0:T(8,128)} %get-tuple-element.8, f32[4]{0:T(128)S(1)} %copy-done.4, bf16[2,128,512]{2,1,0:T(8,128)(2,1)S(1)} %collective-permute-done.7, bf16[2,128,512]{2,1,0:T(8,128)(2,1)S(1)} %collective-permute-done.6), kind=kLoop, calls=%fused_computation | loop fusion | flops 1572864 | bytes 2097168 | tf_op jit(solution)/shard_map/convert_element_type | solution.py:186
  (5 shorter events, 0.0 us)
Async XLA Ops:
  0.0 31.4 %collective-permute-start = (s32[96,3]{0,1:T(4,128)}, s32[96,3]{0,1:T(4,128)S(1)}, u32[]{:S(2)}, u32[]{:S(2)}) collective-permute-start(s32[96,3]{0,1:T(4,128)} %param.10), channel_id=1, source_target_pairs={{0,32},{32,64},{64,96},{96,128},{128,160},{160,192},{192,224},{224... | collective-permute-start | bytes 3464 | tf_op jit(solution)/shard_map/ppermute | solution.py:22
  11.1 20.3 %collective-permute-start.1 = (s32[96,3]{0,1:T(4,128)}, s32[96,3]{0,1:T(4,128)S(1)}, u32[]{:S(2)}, u32[]{:S(2)}) collective-permute-start(s32[96,3]{0,1:T(4,128)} %param.10), channel_id=1, source_target_pairs={{32,0},{64,32},{96,64},{128,96},{160,128},{192,160},{224,192},{256... | collective-permute-start | bytes 3464 | tf_op jit(solution)/shard_map/ppermute | solution.py:25
  13.0 18.4 %collective-permute-start.2 = (bf16[4,128,512]{2,1,0:T(8,128)(2,1)}, bf16[4,128,512]{2,1,0:T(8,128)(2,1)S(1)}, u32[]{:S(2)}, u32[]{:S(2)}) collective-permute-start(bf16[4,128,512]{2,1,0:T(8,128)(2,1)} %local_ref.1), channel_id=1, source_target_pairs={{0,1},{1,2},{2,3},{3,4},{4,5},{5,6},{6,7},{7,8},{8,9},{9,10},{10,1... | collective-permute-start | bytes 1572872 | tf_op jit(solution)/shard_map/ppermute | solution.py:14
  16.3 17.2 %collective-permute-start.4 = (bf16[4,128,512]{2,1,0:T(8,128)(2,1)}, bf16[4,128,512]{2,1,0:T(8,128)(2,1)S(1)}, u32[]{:S(2)}, u32[]{:S(2)}) collective-permute-start(bf16[4,128,512]{2,1,0:T(8,128)(2,1)} %local_ref.1), channel_id=1, source_target_pairs={{0,31},{1,0},{2,1},{3,2},{4,3},{5,4},{6,5},{7,6},{8,7},{9,8},{10,9... | collective-permute-start | bytes 1572872 | tf_op jit(solution)/shard_map/ppermute | solution.py:14
  31.5 17.9 %copy-start = (bf16[4,128,512]{2,1,0:T(8,128)(2,1)}, bf16[4,128,512]{2,1,0:T(8,128)(2,1)S(1)}, u32[]{:S(2)}) copy-start(bf16[4,128,512]{2,1,0:T(8,128)(2,1)S(1)} %collective-permute-done.2.west_ref) | copy-start | bytes 1572868
  31.5 16.1 %collective-permute-start.3 = (bf16[4,128,512]{2,1,0:T(8,128)(2,1)S(1)}, bf16[4,128,512]{2,1,0:T(8,128)(2,1)S(1)}, u32[]{:S(2)}, u32[]{:S(2)}) collective-permute-start(bf16[4,128,512]{2,1,0:T(8,128)(2,1)S(1)} %collective-permute-done.2.west_ref), channel_id=1, source_target_pairs={{0,1},{1,2},{2,3},{3,4},{4,5},{5,6},{6,7},{7,8},{8,9},{9,10},{10,1... | collective-permute-start | bytes 1572872 | tf_op jit(solution)/shard_map/ppermute | solution.py:14
  33.4 15.9 %copy-start.1 = (bf16[4,128,512]{2,1,0:T(8,128)(2,1)}, bf16[4,128,512]{2,1,0:T(8,128)(2,1)S(1)}, u32[]{:S(2)}) copy-start(bf16[4,128,512]{2,1,0:T(8,128)(2,1)S(1)} %collective-permute-done.4.east_ref) | copy-start | bytes 1572868
  33.4 15.9 %collective-permute-start.5 = (bf16[4,128,512]{2,1,0:T(8,128)(2,1)S(1)}, bf16[4,128,512]{2,1,0:T(8,128)(2,1)S(1)}, u32[]{:S(2)}, u32[]{:S(2)}) collective-permute-start(bf16[4,128,512]{2,1,0:T(8,128)(2,1)S(1)} %collective-permute-done.4.east_ref), channel_id=1, source_target_pairs={{0,31},{1,0},{2,1},{3,2},{4,3},{5,4},{6,5},{7,6},{8,7},{9,8},{10,9... | collective-permute-start | bytes 1572872 | tf_op jit(solution)/shard_map/ppermute | solution.py:14
  41.8 48.2 %copy-start.4 = (f32[4]{0:T(128)S(1)}, f32[4]{0:T(128)}, u32[]{:S(2)}) copy-start(f32[4]{0:T(128)} %param.9) | copy-start | bytes 52
  47.6 1.8 %copy-start.2 = (bf16[4,128,512]{2,1,0:T(8,128)(2,1)}, bf16[4,128,512]{2,1,0:T(8,128)(2,1)S(1)}, u32[]{:S(2)}) copy-start(bf16[4,128,512]{2,1,0:T(8,128)(2,1)S(1)} %collective-permute-done.3.far_west_ref) | copy-start | bytes 1572868
  49.4 0.9 copy-start.3
  67.6 12.1 %collective-permute-start.6 = (bf16[2,128,512]{2,1,0:T(8,128)(2,1)}, bf16[2,128,512]{2,1,0:T(8,128)(2,1)S(1)}, u32[]{:S(2)}, u32[]{:S(2)}) collective-permute-start(bf16[2,128,512]{2,1,0:T(8,128)(2,1)} %get-tuple-element.9), channel_id=1, source_target_pairs={{0,32},{32,64},{64,96},{96,128},{128,160},{160,192},{192,224},{224... | collective-permute-start | bytes 786440 | tf_op jit(solution)/shard_map/ppermute | solution.py:183
  76.1 13.9 %collective-permute-start.7 = (bf16[2,128,512]{2,1,0:T(8,128)(2,1)}, bf16[2,128,512]{2,1,0:T(8,128)(2,1)S(1)}, u32[]{:S(2)}, u32[]{:S(2)}) collective-permute-start(bf16[2,128,512]{2,1,0:T(8,128)(2,1)} %get-tuple-element.10), channel_id=1, source_target_pairs={{32,0},{64,32},{96,64},{128,96},{160,128},{192,160},{224,192},{256... | collective-permute-start | bytes 786440 | tf_op jit(solution)/shard_map/ppermute | solution.py:182

commit v12 on v9

--- a/solution.py
+++ b/solution.py
@@ -96,7 +96,7 @@
         response = jnp.dot(band_ref[in_row, 0], window_ref[in_row], preferred_element_type=jnp.float32)
         response_ref[in_row * cols : (in_row + 1) * cols, :] = response.astype(jnp.bfloat16)
     mixed_ref[...] = jnp.dot(response_ref[...], weight_ref[0], preferred_element_type=jnp.float32)
-    chunk = 16
+    chunk = 32
 
     def accumulate(first):
         def body(step, carry):

time: 90.8 us -> 90.6 us (level)
  no operation moved by 1% of the time
where the time goes in v12:
time: 90.6 us; the launch traced here: 89.9 us
  starting transfers between devices  42.4 us (47%)
  Pallas kernels  19.8 us (22%)
  waiting for transfers between devices  19.5 us (22%)
  other arithmetic  6.24 us (7%)
  local copies, waits for them, and re-layouts  1.55 us (2%)
    ppermute x4, starting transfers between devices, shifted(): lax.ppermute(value, axis, [(i, (i + by) % length) for i in range(length)])  18.9 us
    pallas_call x1, Pallas kernels, block_partials(): pl.pallas_call(_block_kernel, grid=(kinds,), in_specs=[pl.BlockSpec(memor...  15 us
    ppermute x1, starting transfers between devices, with_halo(): lax.ppermute(lax.slice_in_dim(block, block.shape[dim] - width, None, axis...  11.1 us
    ppermute x1, waiting for transfers between devices, on_device(): from_below = lax.ppermute(upper, 'lat', backward).astype(jnp.float32)  10.3 us
    ppermute x1, starting transfers between devices, on_device(): from_above = lax.ppermute(lower, 'lat', forward).astype(jnp.float32)  8.52 us
    ppermute x4, waiting for transfers between devices, shifted(): lax.ppermute(value, axis, [(i, (i + by) % length) for i in range(length)])  7.55 us
    pallas_call x1, Pallas kernels, band_matrix(): pl.pallas_call(_toeplitz_kernel, grid=(rows,), in_specs=[pl.BlockSpec((1,...  4.74 us
    convert_element_type x1, other arithmetic, on_device(): return (inner * row_scale[:, None, None]).astype(jnp.bfloat16)  2.25 us
  transfers between devices with their start and end apart: 8, of which 4 were waited for; matrix products, arithmetic and copies ran while one was open for 6% of the time, Pallas kernels for 5%

profile of v12, /device:TPU:7, one launch (start us, length us, event | category | flops | bytes accessed | tf_op | source)
XLA Modules:
  0.0 89.9 jit_solution(16320589691280698012)
XLA Ops:
  0.0 11.1 %collective-permute-start = (s32[96,3]{0,1:T(4,128)}, s32[96,3]{0,1:T(4,128)S(1)}, u32[]{:S(2)}, u32[]{:S(2)}) collective-permute-start(s32[96,3]{0,1:T(4,128)} %param.10), channel_id=1, source_target_pairs={{0,32},{32,64},{64,96},{96,128},{128,160},{160,192},{192,224},{224... | collective-permute-start | bytes 3464 | tf_op jit(solution)/shard_map/ppermute | solution.py:22
  11.1 1.9 %collective-permute-start.1 = (s32[96,3]{0,1:T(4,128)}, s32[96,3]{0,1:T(4,128)S(1)}, u32[]{:S(2)}, u32[]{:S(2)}) collective-permute-start(s32[96,3]{0,1:T(4,128)} %param.10), channel_id=1, source_target_pairs={{32,0},{64,32},{96,64},{128,96},{160,128},{192,160},{224,192},{256... | collective-permute-start | bytes 3464 | tf_op jit(solution)/shard_map/ppermute | solution.py:25
  13.0 3.2 %collective-permute-start.2 = (bf16[4,128,512]{2,1,0:T(8,128)(2,1)}, bf16[4,128,512]{2,1,0:T(8,128)(2,1)S(1)}, u32[]{:S(2)}, u32[]{:S(2)}) collective-permute-start(bf16[4,128,512]{2,1,0:T(8,128)(2,1)} %local_ref.1), channel_id=1, source_target_pairs={{0,1},{1,2},{2,3},{3,4},{4,5},{5,6},{6,7},{7,8},{8,9},{9,10},{10,1... | collective-permute-start | bytes 1572872 | tf_op jit(solution)/shard_map/ppermute | solution.py:14
  16.3 6.5 %collective-permute-start.4 = (bf16[4,128,512]{2,1,0:T(8,128)(2,1)}, bf16[4,128,512]{2,1,0:T(8,128)(2,1)S(1)}, u32[]{:S(2)}, u32[]{:S(2)}) collective-permute-start(bf16[4,128,512]{2,1,0:T(8,128)(2,1)} %local_ref.1), channel_id=1, source_target_pairs={{0,31},{1,0},{2,1},{3,2},{4,3},{5,4},{6,5},{7,6},{8,7},{9,8},{10,9... | collective-permute-start | bytes 1572872 | tf_op jit(solution)/shard_map/ppermute | solution.py:14
  22.8 0.7 compare_and_fusion
  23.5 0.8 add_bitcast_fusion.4
  24.3 0.7 broadcast_compare_fusion
  25.0 0.9 %fusion = bf16[4,9,513]{2,1,0:T(8,128)(2,1)S(1)} fusion(f32[4,9,513]{2,0,1:T(4,128)} %param.8, pred[4,513]{1,0:T(4,128)(4,1)S(1)} %broadcast_compare_fusion), kind=kLoop, calls=%fused_computation.2 | loop fusion | flops 18468 | bytes 112860 | tf_op jit(solution)/shard_map/convert_element_type | solution.py:35
  25.9 0.7 pad_convert_fusion.taps_ref
  26.6 4.7 %shard_map.64.band_ref = bf16[4,9,128,640]{3,2,1,0:T(8,128)(2,1)} custom-call(f32[4,9,640]{2,1,0:T(8,128)} %pad_convert_fusion.taps_ref), custom_call_target="tpu_custom_call" | custom-call | tf_op jit(solution)/shard_map/pallas_call | solution.py:73
  31.4 0.0 collective-permute-done
  31.4 0.0 collective-permute-done.1
  31.4 0.1 pad_add_fusion.1
  31.5 0.0 collective-permute-done.2.west_ref
  31.5 0.0 copy-start
  31.5 1.9 %collective-permute-start.3 = (bf16[4,128,512]{2,1,0:T(8,128)(2,1)S(1)}, bf16[4,128,512]{2,1,0:T(8,128)(2,1)S(1)}, u32[]{:S(2)}, u32[]{:S(2)}) collective-permute-start(bf16[4,128,512]{2,1,0:T(8,128)(2,1)S(1)} %collective-permute-done.2.west_ref), channel_id=1, source_target_pairs={{0,1},{1,2},{2,3},{3,4},{4,5},{5,6},{6,7},{7,8},{8,9},{9,10},{10,1... | collective-permute-start | bytes 1572872 | tf_op jit(solution)/shard_map/ppermute | solution.py:14
  33.4 0.0 collective-permute-done.4.east_ref
  33.4 0.0 copy-start.1
  33.4 7.3 %collective-permute-start.5 = (bf16[4,128,512]{2,1,0:T(8,128)(2,1)S(1)}, bf16[4,128,512]{2,1,0:T(8,128)(2,1)S(1)}, u32[]{:S(2)}, u32[]{:S(2)}) collective-permute-start(bf16[4,128,512]{2,1,0:T(8,128)(2,1)S(1)} %collective-permute-done.4.east_ref), channel_id=1, source_target_pairs={{0,31},{1,0},{2,1},{3,2},{4,3},{5,4},{6,5},{7,6},{8,7},{9,8},{10,9... | collective-permute-start | bytes 1572872 | tf_op jit(solution)/shard_map/ppermute | solution.py:14
  40.7 0.1 pad_add_fusion
  40.8 0.3 fusion.2
  41.1 0.7 reshape_reshape.3.counts_ref
  41.8 0.0 copy-start.4
  41.8 5.8 %collective-permute-done.3.far_west_ref = bf16[4,128,512]{2,1,0:T(8,128)(2,1)S(1)} collective-permute-done((bf16[4,128,512]{2,1,0:T(8,128)(2,1)S(1)}, bf16[4,128,512]{2,1,0:T(8,128)(2,1)S(1)}, u32[]{:S(2)}, u32[]{:S(2)}) %collective-permute-start.3) | collective-permute-done | bytes 524320 | tf_op jit(solution)/shard_map/ppermute | solution.py:14
  47.6 0.0 copy-start.2
  47.6 1.8 %collective-permute-done.5.far_east_ref = bf16[4,128,512]{2,1,0:T(8,128)(2,1)S(1)} collective-permute-done((bf16[4,128,512]{2,1,0:T(8,128)(2,1)S(1)}, bf16[4,128,512]{2,1,0:T(8,128)(2,1)S(1)}, u32[]{:S(2)}, u32[]{:S(2)}) %collective-permute-start.5) | collective-permute-done | bytes 524320 | tf_op jit(solution)/shard_map/ppermute | solution.py:14
  49.4 0.0 copy-done
  49.4 0.0 copy-done.1
  49.4 0.0 copy-done.2
  49.4 0.0 copy-start.3
  49.4 0.8 copy-done.3
  50.2 15.0 %shard_map.65 = (bf16[2,128,512]{2,1,0:T(8,128)(2,1)}, bf16[2,128,512]{2,1,0:T(8,128)(2,1)}, f32[4,128,512]{2,1,0:T(8,128)}) custom-call(f32[288]{0:T(512)} %reshape_reshape.3.counts_ref, bf16[4,9,128,640]{3,2,1,0:T(8,128)(2,1)} %shard_map.64.band_ref, bf16[4,128,512]{2,1,0:T(8,128)(2,1)} %copy-done.2, bf16[4,128,512]{2,1,0:T(8,128)(2,1)} %copy-done, ...), custom_call_target="tpu_custom_call" | custom-call | tf_op jit(solution)/shard_map/pallas_call | solution.py:132
  65.2 8.5 %collective-permute-start.6 = (bf16[2,128,512]{2,1,0:T(8,128)(2,1)}, bf16[2,128,512]{2,1,0:T(8,128)(2,1)S(1)}, u32[]{:S(2)}, u32[]{:S(2)}) collective-permute-start(bf16[2,128,512]{2,1,0:T(8,128)(2,1)} %get-tuple-element.9), channel_id=1, source_target_pairs={{0,32},{32,64},{64,96},{96,128},{128,160},{160,192},{192,224},{224... | collective-permute-start | bytes 786440 | tf_op jit(solution)/shard_map/ppermute | solution.py:182
  73.8 1.9 %collective-permute-start.7 = (bf16[2,128,512]{2,1,0:T(8,128)(2,1)}, bf16[2,128,512]{2,1,0:T(8,128)(2,1)S(1)}, u32[]{:S(2)}, u32[]{:S(2)}) collective-permute-start(bf16[2,128,512]{2,1,0:T(8,128)(2,1)} %get-tuple-element.10), channel_id=1, source_target_pairs={{32,0},{64,32},{96,64},{128,96},{160,128},{192,160},{224,192},{256... | collective-permute-start | bytes 786440 | tf_op jit(solution)/shard_map/ppermute | solution.py:181
  75.7 1.7 %collective-permute-done.6 = bf16[2,128,512]{2,1,0:T(8,128)(2,1)S(1)} collective-permute-done((bf16[2,128,512]{2,1,0:T(8,128)(2,1)}, bf16[2,128,512]{2,1,0:T(8,128)(2,1)S(1)}, u32[]{:S(2)}, u32[]{:S(2)}) %collective-permute-start.6) | collective-permute-done | bytes 262176 | tf_op jit(solution)/shard_map/ppermute | solution.py:182
  77.4 10.3 %collective-permute-done.7 = bf16[2,128,512]{2,1,0:T(8,128)(2,1)S(1)} collective-permute-done((bf16[2,128,512]{2,1,0:T(8,128)(2,1)}, bf16[2,128,512]{2,1,0:T(8,128)(2,1)S(1)}, u32[]{:S(2)}, u32[]{:S(2)}) %collective-permute-start.7) | collective-permute-done | bytes 262176 | tf_op jit(solution)/shard_map/ppermute | solution.py:181
  87.7 0.0 copy-done.4
  87.7 2.2 %multiply_convert_fusion = bf16[4,128,512]{2,1,0:T(8,128)(2,1)} fusion(f32[4,128,512]{2,1,0:T(8,128)} %get-tuple-element.8, f32[4]{0:T(128)S(1)} %copy-done.4, bf16[2,128,512]{2,1,0:T(8,128)(2,1)S(1)} %collective-permute-done.7, bf16[2,128,512]{2,1,0:T(8,128)(2,1)S(1)} %collective-permute-done.6), kind=kLoop, calls=%fused_computation | loop fusion | flops 1572864 | bytes 2097168 | tf_op jit(solution)/shard_map/convert_element_type | solution.py:185
  (5 shorter events, 0.0 us)
Async XLA Ops:
  0.0 31.4 %collective-permute-start = (s32[96,3]{0,1:T(4,128)}, s32[96,3]{0,1:T(4,128)S(1)}, u32[]{:S(2)}, u32[]{:S(2)}) collective-permute-start(s32[96,3]{0,1:T(4,128)} %param.10), channel_id=1, source_target_pairs={{0,32},{32,64},{64,96},{96,128},{128,160},{160,192},{192,224},{224... | collective-permute-start | bytes 3464 | tf_op jit(solution)/shard_map/ppermute | solution.py:22
  11.1 20.3 %collective-permute-start.1 = (s32[96,3]{0,1:T(4,128)}, s32[96,3]{0,1:T(4,128)S(1)}, u32[]{:S(2)}, u32[]{:S(2)}) collective-permute-start(s32[96,3]{0,1:T(4,128)} %param.10), channel_id=1, source_target_pairs={{32,0},{64,32},{96,64},{128,96},{160,128},{192,160},{224,192},{256... | collective-permute-start | bytes 3464 | tf_op jit(solution)/shard_map/ppermute | solution.py:25
  13.0 18.4 %collective-permute-start.2 = (bf16[4,128,512]{2,1,0:T(8,128)(2,1)}, bf16[4,128,512]{2,1,0:T(8,128)(2,1)S(1)}, u32[]{:S(2)}, u32[]{:S(2)}) collective-permute-start(bf16[4,128,512]{2,1,0:T(8,128)(2,1)} %local_ref.1), channel_id=1, source_target_pairs={{0,1},{1,2},{2,3},{3,4},{4,5},{5,6},{6,7},{7,8},{8,9},{9,10},{10,1... | collective-permute-start | bytes 1572872 | tf_op jit(solution)/shard_map/ppermute | solution.py:14
  16.3 17.2 %collective-permute-start.4 = (bf16[4,128,512]{2,1,0:T(8,128)(2,1)}, bf16[4,128,512]{2,1,0:T(8,128)(2,1)S(1)}, u32[]{:S(2)}, u32[]{:S(2)}) collective-permute-start(bf16[4,128,512]{2,1,0:T(8,128)(2,1)} %local_ref.1), channel_id=1, source_target_pairs={{0,31},{1,0},{2,1},{3,2},{4,3},{5,4},{6,5},{7,6},{8,7},{9,8},{10,9... | collective-permute-start | bytes 1572872 | tf_op jit(solution)/shard_map/ppermute | solution.py:14
  31.5 17.9 %copy-start = (bf16[4,128,512]{2,1,0:T(8,128)(2,1)}, bf16[4,128,512]{2,1,0:T(8,128)(2,1)S(1)}, u32[]{:S(2)}) copy-start(bf16[4,128,512]{2,1,0:T(8,128)(2,1)S(1)} %collective-permute-done.2.west_ref) | copy-start | bytes 1572868
  31.5 16.1 %collective-permute-start.3 = (bf16[4,128,512]{2,1,0:T(8,128)(2,1)S(1)}, bf16[4,128,512]{2,1,0:T(8,128)(2,1)S(1)}, u32[]{:S(2)}, u32[]{:S(2)}) collective-permute-start(bf16[4,128,512]{2,1,0:T(8,128)(2,1)S(1)} %collective-permute-done.2.west_ref), channel_id=1, source_target_pairs={{0,1},{1,2},{2,3},{3,4},{4,5},{5,6},{6,7},{7,8},{8,9},{9,10},{10,1... | collective-permute-start | bytes 1572872 | tf_op jit(solution)/shard_map/ppermute | solution.py:14
  33.4 15.9 %copy-start.1 = (bf16[4,128,512]{2,1,0:T(8,128)(2,1)}, bf16[4,128,512]{2,1,0:T(8,128)(2,1)S(1)}, u32[]{:S(2)}) copy-start(bf16[4,128,512]{2,1,0:T(8,128)(2,1)S(1)} %collective-permute-done.4.east_ref) | copy-start | bytes 1572868
  33.4 15.9 %collective-permute-start.5 = (bf16[4,128,512]{2,1,0:T(8,128)(2,1)S(1)}, bf16[4,128,512]{2,1,0:T(8,128)(2,1)S(1)}, u32[]{:S(2)}, u32[]{:S(2)}) collective-permute-start(bf16[4,128,512]{2,1,0:T(8,128)(2,1)S(1)} %collective-permute-done.4.east_ref), channel_id=1, source_target_pairs={{0,31},{1,0},{2,1},{3,2},{4,3},{5,4},{6,5},{7,6},{8,7},{9,8},{10,9... | collective-permute-start | bytes 1572872 | tf_op jit(solution)/shard_map/ppermute | solution.py:14
  41.8 45.9 %copy-start.4 = (f32[4]{0:T(128)S(1)}, f32[4]{0:T(128)}, u32[]{:S(2)}) copy-start(f32[4]{0:T(128)} %param.9) | copy-start | bytes 52
  47.6 1.8 %copy-start.2 = (bf16[4,128,512]{2,1,0:T(8,128)(2,1)}, bf16[4,128,512]{2,1,0:T(8,128)(2,1)S(1)}, u32[]{:S(2)}) copy-start(bf16[4,128,512]{2,1,0:T(8,128)(2,1)S(1)} %collective-permute-done.3.far_west_ref) | copy-start | bytes 1572868
  49.4 0.9 copy-start.3
  65.2 12.1 %collective-permute-start.6 = (bf16[2,128,512]{2,1,0:T(8,128)(2,1)}, bf16[2,128,512]{2,1,0:T(8,128)(2,1)S(1)}, u32[]{:S(2)}, u32[]{:S(2)}) collective-permute-start(bf16[2,128,512]{2,1,0:T(8,128)(2,1)} %get-tuple-element.9), channel_id=1, source_target_pairs={{0,32},{32,64},{64,96},{96,128},{128,160},{160,192},{192,224},{224... | collective-permute-start | bytes 786440 | tf_op jit(solution)/shard_map/ppermute | solution.py:182
  73.8 13.9 %collective-permute-start.7 = (bf16[2,128,512]{2,1,0:T(8,128)(2,1)}, bf16[2,128,512]{2,1,0:T(8,128)(2,1)S(1)}, u32[]{:S(2)}, u32[]{:S(2)}) collective-permute-start(bf16[2,128,512]{2,1,0:T(8,128)(2,1)} %get-tuple-element.10), channel_id=1, source_target_pairs={{32,0},{64,32},{96,64},{128,96},{160,128},{192,160},{224,192},{256... | collective-permute-start | bytes 786440 | tf_op jit(solution)/shard_map/ppermute | solution.py:181

commit v13 on v9

--- a/solution.py
+++ b/solution.py
@@ -80,7 +80,7 @@
 
 
 def _block_kernel(counts_ref, band_ref, far_west_ref, west_ref, local_ref, east_ref, far_east_ref,
-                  weight_ref, upper_ref, lower_ref, inner_ref, window_ref, response_ref, mixed_ref, total_ref):
+                  weight_ref, upper_ref, lower_ref, inner_ref, window_ref, response_ref, mixed_ref, total_ref, copy_sems):
     kind = pl.program_id(0)
     kinds = pl.num_programs(0)
     input_rows, cols, _ = local_ref.shape
@@ -89,8 +89,14 @@
 
     @pl.when(kind == 0)
     def _():
-        for index, part in enumerate(parts):
-            window_ref[:, index * cols : (index + 1) * cols, :] = part[...]
+        copies = [
+            pltpu.make_async_copy(part, window_ref.at[:, index * cols : (index + 1) * cols, :], copy_sems.at[index])
+            for index, part in enumerate(parts)
+        ]
+        for copy in copies:
+            copy.start()
+        for copy in copies:
+            copy.wait()
 
     for in_row in range(input_rows):
         response = jnp.dot(band_ref[in_row, 0], window_ref[in_row], preferred_element_type=jnp.float32)
@@ -136,7 +142,7 @@
             pl.BlockSpec(memory_space=pltpu.SMEM),
             pl.BlockSpec((rows, 1, cols, window), lambda k: (0, k, 0, 0)),
         ]
-        + [whole(parts[0].shape)] * len(parts)
+        + [pl.BlockSpec(memory_space=pl.ANY)] * len(parts)
         + [pl.BlockSpec((1,) + mix_weight.shape[1:], lambda k: (k, 0, 0))],
         out_specs=[whole((RIM, cols, channels))] * 2 + [whole((rows, cols, channels))],
         out_shape=[
@@ -149,6 +155,7 @@
             pltpu.VMEM((rows * cols, channels), jnp.bfloat16),
             pltpu.VMEM((rows * cols, mix_weight.shape[2]), jnp.float32),
             pltpu.VMEM((rows + 2 * RIM, cols, mix_weight.shape[2]), jnp.float32),
+            pltpu.SemaphoreType.DMA((len(parts),)),
         ],
         compiler_params=pltpu.CompilerParams(dimension_semantics=("arbitrary",)),
     )(counts.reshape(-1), band, *parts, mix_weight)

time: 90.8 us -> 91.7 us (level)
  transfers between devices with their start and end apart: 8 -> 8, of which waited for: 4 -> 4; matrix products, arithmetic and copies ran while one was open for 6% -> 5% of each run, Pallas kernels for 5% -> 5%
where the time goes in v13:
time: 91.7 us; the launch traced here: 91 us
  starting transfers between devices  42.4 us (46%)
  Pallas kernels  20.8 us (23%)
  waiting for transfers between devices  19.5 us (21%)
  other arithmetic  6.24 us (7%)
  local copies, waits for them, and re-layouts  1.55 us (2%)
    ppermute x4, starting transfers between devices, shifted(): lax.ppermute(value, axis, [(i, (i + by) % length) for i in range(length)])  18.9 us
    pallas_call x1, Pallas kernels, block_partials(): pl.pallas_call(_block_kernel, grid=(kinds,), in_specs=[pl.BlockSpec(memor...  16.1 us
    ppermute x1, starting transfers between devices, with_halo(): lax.ppermute(lax.slice_in_dim(block, block.shape[dim] - width, None, axis...  11.1 us
    ppermute x1, waiting for transfers between devices, on_device(): from_below = lax.ppermute(upper, 'lat', backward).astype(jnp.float32)  10.3 us
    ppermute x1, starting transfers between devices, on_device(): from_above = lax.ppermute(lower, 'lat', forward).astype(jnp.float32)  8.53 us
    ppermute x4, waiting for transfers between devices, shifted(): lax.ppermute(value, axis, [(i, (i + by) % length) for i in range(length)])  7.55 us
    pallas_call x1, Pallas kernels, band_matrix(): pl.pallas_call(_toeplitz_kernel, grid=(rows,), in_specs=[pl.BlockSpec((1,...  4.74 us
    convert_element_type x1, other arithmetic, on_device(): return (inner * row_scale[:, None, None]).astype(jnp.bfloat16)  2.25 us
  transfers between devices with their start and end apart: 8, of which 4 were waited for; matrix products, arithmetic and copies ran while one was open for 5% of the time, Pallas kernels for 5%

profile of v13, /device:TPU:7, one launch (start us, length us, event | category | flops | bytes accessed | tf_op | source)
XLA Modules:
  0.0 91.0 jit_solution(15132223881100391063)
XLA Ops:
  0.0 11.1 %collective-permute-start = (s32[96,3]{0,1:T(4,128)}, s32[96,3]{0,1:T(4,128)S(1)}, u32[]{:S(2)}, u32[]{:S(2)}) collective-permute-start(s32[96,3]{0,1:T(4,128)} %param.10), channel_id=1, source_target_pairs={{0,32},{32,64},{64,96},{96,128},{128,160},{160,192},{192,224},{224... | collective-permute-start | bytes 3464 | tf_op jit(solution)/shard_map/ppermute | solution.py:22
  11.1 1.9 %collective-permute-start.1 = (s32[96,3]{0,1:T(4,128)}, s32[96,3]{0,1:T(4,128)S(1)}, u32[]{:S(2)}, u32[]{:S(2)}) collective-permute-start(s32[96,3]{0,1:T(4,128)} %param.10), channel_id=1, source_target_pairs={{32,0},{64,32},{96,64},{128,96},{160,128},{192,160},{224,192},{256... | collective-permute-start | bytes 3464 | tf_op jit(solution)/shard_map/ppermute | solution.py:25
  13.0 3.2 %collective-permute-start.2 = (bf16[4,128,512]{2,1,0:T(8,128)(2,1)}, bf16[4,128,512]{2,1,0:T(8,128)(2,1)S(1)}, u32[]{:S(2)}, u32[]{:S(2)}) collective-permute-start(bf16[4,128,512]{2,1,0:T(8,128)(2,1)} %local_ref.1), channel_id=1, source_target_pairs={{0,1},{1,2},{2,3},{3,4},{4,5},{5,6},{6,7},{7,8},{8,9},{9,10},{10,1... | collective-permute-start | bytes 1572872 | tf_op jit(solution)/shard_map/ppermute | solution.py:14
  16.3 6.5 %collective-permute-start.4 = (bf16[4,128,512]{2,1,0:T(8,128)(2,1)}, bf16[4,128,512]{2,1,0:T(8,128)(2,1)S(1)}, u32[]{:S(2)}, u32[]{:S(2)}) collective-permute-start(bf16[4,128,512]{2,1,0:T(8,128)(2,1)} %local_ref.1), channel_id=1, source_target_pairs={{0,31},{1,0},{2,1},{3,2},{4,3},{5,4},{6,5},{7,6},{8,7},{9,8},{10,9... | collective-permute-start | bytes 1572872 | tf_op jit(solution)/shard_map/ppermute | solution.py:14
  22.8 0.7 compare_and_fusion
  23.5 0.8 add_bitcast_fusion.4
  24.3 0.7 broadcast_compare_fusion
  25.0 0.9 %fusion = bf16[4,9,513]{2,1,0:T(8,128)(2,1)S(1)} fusion(f32[4,9,513]{2,0,1:T(4,128)} %param.8, pred[4,513]{1,0:T(4,128)(4,1)S(1)} %broadcast_compare_fusion), kind=kLoop, calls=%fused_computation.2 | loop fusion | flops 18468 | bytes 112860 | tf_op jit(solution)/shard_map/convert_element_type | solution.py:35
  25.9 0.7 pad_convert_fusion.taps_ref
  26.6 4.7 %shard_map.64.band_ref = bf16[4,9,128,640]{3,2,1,0:T(8,128)(2,1)} custom-call(f32[4,9,640]{2,1,0:T(8,128)} %pad_convert_fusion.taps_ref), custom_call_target="tpu_custom_call" | custom-call | tf_op jit(solution)/shard_map/pallas_call | solution.py:73
  31.4 0.0 collective-permute-done
  31.4 0.0 collective-permute-done.1
  31.4 0.1 pad_add_fusion.1
  31.5 0.0 collective-permute-done.2.west_ref
  31.5 0.0 copy-start
  31.5 1.9 %collective-permute-start.3 = (bf16[4,128,512]{2,1,0:T(8,128)(2,1)S(1)}, bf16[4,128,512]{2,1,0:T(8,128)(2,1)S(1)}, u32[]{:S(2)}, u32[]{:S(2)}) collective-permute-start(bf16[4,128,512]{2,1,0:T(8,128)(2,1)S(1)} %collective-permute-done.2.west_ref), channel_id=1, source_target_pairs={{0,1},{1,2},{2,3},{3,4},{4,5},{5,6},{6,7},{7,8},{8,9},{9,10},{10,1... | collective-permute-start | bytes 1572872 | tf_op jit(solution)/shard_map/ppermute | solution.py:14
  33.4 0.0 collective-permute-done.4.east_ref
  33.4 0.0 copy-start.1
  33.4 7.3 %collective-permute-start.5 = (bf16[4,128,512]{2,1,0:T(8,128)(2,1)S(1)}, bf16[4,128,512]{2,1,0:T(8,128)(2,1)S(1)}, u32[]{:S(2)}, u32[]{:S(2)}) collective-permute-start(bf16[4,128,512]{2,1,0:T(8,128)(2,1)S(1)} %collective-permute-done.4.east_ref), channel_id=1, source_target_pairs={{0,31},{1,0},{2,1},{3,2},{4,3},{5,4},{6,5},{7,6},{8,7},{9,8},{10,9... | collective-permute-start | bytes 1572872 | tf_op jit(solution)/shard_map/ppermute | solution.py:14
  40.7 0.1 pad_add_fusion
  40.8 0.3 fusion.2
  41.1 0.7 reshape_reshape.3.counts_ref
  41.8 0.0 copy-start.4
  41.8 5.8 %collective-permute-done.3.far_west_ref = bf16[4,128,512]{2,1,0:T(8,128)(2,1)S(1)} collective-permute-done((bf16[4,128,512]{2,1,0:T(8,128)(2,1)S(1)}, bf16[4,128,512]{2,1,0:T(8,128)(2,1)S(1)}, u32[]{:S(2)}, u32[]{:S(2)}) %collective-permute-start.3) | collective-permute-done | bytes 524320 | tf_op jit(solution)/shard_map/ppermute | solution.py:14
  47.6 0.0 copy-start.2
  47.6 1.8 %collective-permute-done.5.far_east_ref = bf16[4,128,512]{2,1,0:T(8,128)(2,1)S(1)} collective-permute-done((bf16[4,128,512]{2,1,0:T(8,128)(2,1)S(1)}, bf16[4,128,512]{2,1,0:T(8,128)(2,1)S(1)}, u32[]{:S(2)}, u32[]{:S(2)}) %collective-permute-start.5) | collective-permute-done | bytes 524320 | tf_op jit(solution)/shard_map/ppermute | solution.py:14
  49.4 0.0 copy-done
  49.4 0.0 copy-done.1
  49.4 0.0 copy-done.2
  49.4 0.0 copy-start.3
  49.4 0.8 copy-done.3
  50.2 16.1 %shard_map.65 = (bf16[2,128,512]{2,1,0:T(8,128)(2,1)}, bf16[2,128,512]{2,1,0:T(8,128)(2,1)}, f32[4,128,512]{2,1,0:T(8,128)}) custom-call(f32[288]{0:T(512)} %reshape_reshape.3.counts_ref, bf16[4,9,128,640]{3,2,1,0:T(8,128)(2,1)} %shard_map.64.band_ref, bf16[4,128,512]{2,1,0:T(8,128)(2,1)} %copy-done.2, bf16[4,128,512]{2,1,0:T(8,128)(2,1)} %copy-done, ...), custom_call_target="tpu_custom_call" | custom-call | tf_op jit(solution)/shard_map/pallas_call | solution.py:138
  66.3 8.5 %collective-permute-start.6 = (bf16[2,128,512]{2,1,0:T(8,128)(2,1)}, bf16[2,128,512]{2,1,0:T(8,128)(2,1)S(1)}, u32[]{:S(2)}, u32[]{:S(2)}) collective-permute-start(bf16[2,128,512]{2,1,0:T(8,128)(2,1)} %get-tuple-element.9), channel_id=1, source_target_pairs={{0,32},{32,64},{64,96},{96,128},{128,160},{160,192},{192,224},{224... | collective-permute-start | bytes 786440 | tf_op jit(solution)/shard_map/ppermute | solution.py:189
  74.9 1.9 %collective-permute-start.7 = (bf16[2,128,512]{2,1,0:T(8,128)(2,1)}, bf16[2,128,512]{2,1,0:T(8,128)(2,1)S(1)}, u32[]{:S(2)}, u32[]{:S(2)}) collective-permute-start(bf16[2,128,512]{2,1,0:T(8,128)(2,1)} %get-tuple-element.10), channel_id=1, source_target_pairs={{32,0},{64,32},{96,64},{128,96},{160,128},{192,160},{224,192},{256... | collective-permute-start | bytes 786440 | tf_op jit(solution)/shard_map/ppermute | solution.py:188
  76.8 1.7 %collective-permute-done.6 = bf16[2,128,512]{2,1,0:T(8,128)(2,1)S(1)} collective-permute-done((bf16[2,128,512]{2,1,0:T(8,128)(2,1)}, bf16[2,128,512]{2,1,0:T(8,128)(2,1)S(1)}, u32[]{:S(2)}, u32[]{:S(2)}) %collective-permute-start.6) | collective-permute-done | bytes 262176 | tf_op jit(solution)/shard_map/ppermute | solution.py:189
  78.5 10.3 %collective-permute-done.7 = bf16[2,128,512]{2,1,0:T(8,128)(2,1)S(1)} collective-permute-done((bf16[2,128,512]{2,1,0:T(8,128)(2,1)}, bf16[2,128,512]{2,1,0:T(8,128)(2,1)S(1)}, u32[]{:S(2)}, u32[]{:S(2)}) %collective-permute-start.7) | collective-permute-done | bytes 262176 | tf_op jit(solution)/shard_map/ppermute | solution.py:188
  88.8 0.0 copy-done.4
  88.8 2.2 %multiply_convert_fusion = bf16[4,128,512]{2,1,0:T(8,128)(2,1)} fusion(f32[4,128,512]{2,1,0:T(8,128)} %get-tuple-element.8, f32[4]{0:T(128)S(1)} %copy-done.4, bf16[2,128,512]{2,1,0:T(8,128)(2,1)S(1)} %collective-permute-done.7, bf16[2,128,512]{2,1,0:T(8,128)(2,1)S(1)} %collective-permute-done.6), kind=kLoop, calls=%fused_computation | loop fusion | flops 1572864 | bytes 2097168 | tf_op jit(solution)/shard_map/convert_element_type | solution.py:192
  (5 shorter events, 0.0 us)
Async XLA Ops:
  0.0 31.4 %collective-permute-start = (s32[96,3]{0,1:T(4,128)}, s32[96,3]{0,1:T(4,128)S(1)}, u32[]{:S(2)}, u32[]{:S(2)}) collective-permute-start(s32[96,3]{0,1:T(4,128)} %param.10), channel_id=1, source_target_pairs={{0,32},{32,64},{64,96},{96,128},{128,160},{160,192},{192,224},{224... | collective-permute-start | bytes 3464 | tf_op jit(solution)/shard_map/ppermute | solution.py:22
  11.1 20.3 %collective-permute-start.1 = (s32[96,3]{0,1:T(4,128)}, s32[96,3]{0,1:T(4,128)S(1)}, u32[]{:S(2)}, u32[]{:S(2)}) collective-permute-start(s32[96,3]{0,1:T(4,128)} %param.10), channel_id=1, source_target_pairs={{32,0},{64,32},{96,64},{128,96},{160,128},{192,160},{224,192},{256... | collective-permute-start | bytes 3464 | tf_op jit(solution)/shard_map/ppermute | solution.py:25
  13.0 18.4 %collective-permute-start.2 = (bf16[4,128,512]{2,1,0:T(8,128)(2,1)}, bf16[4,128,512]{2,1,0:T(8,128)(2,1)S(1)}, u32[]{:S(2)}, u32[]{:S(2)}) collective-permute-start(bf16[4,128,512]{2,1,0:T(8,128)(2,1)} %local_ref.1), channel_id=1, source_target_pairs={{0,1},{1,2},{2,3},{3,4},{4,5},{5,6},{6,7},{7,8},{8,9},{9,10},{10,1... | collective-permute-start | bytes 1572872 | tf_op jit(solution)/shard_map/ppermute | solution.py:14
  16.3 17.2 %collective-permute-start.4 = (bf16[4,128,512]{2,1,0:T(8,128)(2,1)}, bf16[4,128,512]{2,1,0:T(8,128)(2,1)S(1)}, u32[]{:S(2)}, u32[]{:S(2)}) collective-permute-start(bf16[4,128,512]{2,1,0:T(8,128)(2,1)} %local_ref.1), channel_id=1, source_target_pairs={{0,31},{1,0},{2,1},{3,2},{4,3},{5,4},{6,5},{7,6},{8,7},{9,8},{10,9... | collective-permute-start | bytes 1572872 | tf_op jit(solution)/shard_map/ppermute | solution.py:14
  31.5 17.9 %copy-start = (bf16[4,128,512]{2,1,0:T(8,128)(2,1)}, bf16[4,128,512]{2,1,0:T(8,128)(2,1)S(1)}, u32[]{:S(2)}) copy-start(bf16[4,128,512]{2,1,0:T(8,128)(2,1)S(1)} %collective-permute-done.2.west_ref) | copy-start | bytes 1572868
  31.5 16.1 %collective-permute-start.3 = (bf16[4,128,512]{2,1,0:T(8,128)(2,1)S(1)}, bf16[4,128,512]{2,1,0:T(8,128)(2,1)S(1)}, u32[]{:S(2)}, u32[]{:S(2)}) collective-permute-start(bf16[4,128,512]{2,1,0:T(8,128)(2,1)S(1)} %collective-permute-done.2.west_ref), channel_id=1, source_target_pairs={{0,1},{1,2},{2,3},{3,4},{4,5},{5,6},{6,7},{7,8},{8,9},{9,10},{10,1... | collective-permute-start | bytes 1572872 | tf_op jit(solution)/shard_map/ppermute | solution.py:14
  33.4 15.9 %copy-start.1 = (bf16[4,128,512]{2,1,0:T(8,128)(2,1)}, bf16[4,128,512]{2,1,0:T(8,128)(2,1)S(1)}, u32[]{:S(2)}) copy-start(bf16[4,128,512]{2,1,0:T(8,128)(2,1)S(1)} %collective-permute-done.4.east_ref) | copy-start | bytes 1572868
  33.4 15.9 %collective-permute-start.5 = (bf16[4,128,512]{2,1,0:T(8,128)(2,1)S(1)}, bf16[4,128,512]{2,1,0:T(8,128)(2,1)S(1)}, u32[]{:S(2)}, u32[]{:S(2)}) collective-permute-start(bf16[4,128,512]{2,1,0:T(8,128)(2,1)S(1)} %collective-permute-done.4.east_ref), channel_id=1, source_target_pairs={{0,31},{1,0},{2,1},{3,2},{4,3},{5,4},{6,5},{7,6},{8,7},{9,8},{10,9... | collective-permute-start | bytes 1572872 | tf_op jit(solution)/shard_map/ppermute | solution.py:14
  41.8 47.0 %copy-start.4 = (f32[4]{0:T(128)S(1)}, f32[4]{0:T(128)}, u32[]{:S(2)}) copy-start(f32[4]{0:T(128)} %param.9) | copy-start | bytes 52
  47.6 1.8 %copy-start.2 = (bf16[4,128,512]{2,1,0:T(8,128)(2,1)}, bf16[4,128,512]{2,1,0:T(8,128)(2,1)S(1)}, u32[]{:S(2)}) copy-start(bf16[4,128,512]{2,1,0:T(8,128)(2,1)S(1)} %collective-permute-done.3.far_west_ref) | copy-start | bytes 1572868
  49.4 0.9 copy-start.3
  66.3 12.1 %collective-permute-start.6 = (bf16[2,128,512]{2,1,0:T(8,128)(2,1)}, bf16[2,128,512]{2,1,0:T(8,128)(2,1)S(1)}, u32[]{:S(2)}, u32[]{:S(2)}) collective-permute-start(bf16[2,128,512]{2,1,0:T(8,128)(2,1)} %get-tuple-element.9), channel_id=1, source_target_pairs={{0,32},{32,64},{64,96},{96,128},{128,160},{160,192},{192,224},{224... | collective-permute-start | bytes 786440 | tf_op jit(solution)/shard_map/ppermute | solution.py:189
  74.9 13.9 %collective-permute-start.7 = (bf16[2,128,512]{2,1,0:T(8,128)(2,1)}, bf16[2,128,512]{2,1,0:T(8,128)(2,1)S(1)}, u32[]{:S(2)}, u32[]{:S(2)}) collective-permute-start(bf16[2,128,512]{2,1,0:T(8,128)(2,1)} %get-tuple-element.10), channel_id=1, source_target_pairs={{32,0},{64,32},{96,64},{128,96},{160,128},{192,160},{224,192},{256... | collective-permute-start | bytes 786440 | tf_op jit(solution)/shard_map/ppermute | solution.py:188
